TPU v7x, 1024 devices: a whole 4x4x32 slice. The times are simulated.
1024 devices in a mesh: mapx: 16 (over z_lo, core), mapy: 16 (over z_hi, x), layer: 4 (over y).
Axes of the slice: x: 4, y: 4, z: 32 (z_hi: 4, z_lo: 8; z = z_hi * 8 + z_lo), core: 2. Of those that a mesh axis runs over, the one named last changes fastest.
Arguments:
- velocity: float32 [16, 2, 8, 128, 2048], P(None, None, 'layer', 'mapx', 'mapy'), may hold values from -6 to 6
- viscosity: float32 [8, 128, 2048], P('layer', 'mapx', 'mapy'), may hold values from 0.5 to 5
- friction: float32 [128, 2048], P('mapx', 'mapy'), may hold values from 0.05 to 0.5
- owner: int32 [16, 16, 1024, 1], P('mapx', 'mapy'), may hold values from 0 to 63; in each aligned block of 1024 rows (0 to 1023, 1024 to 2047, ..., all dimensions but the last counted through in order) at most 32 rows name the same one
- cell: int32 [16, 16, 1024], P('mapx', 'mapy'), may hold values from 0 to 511
- directions: float32 [16, 64, 8192], P(None, 'mapx', ('mapy', 'layer')), may hold values from -6 to 6
- stiffness: float32 [64, 8192], P('mapx', ('mapy', 'layer')), may hold values from 0.02 to 0.2
Outputs:
- image: float32 [16, 2, 8, 128, 2048], P(None, None, 'layer', 'mapx', 'mapy')
- hessian: float32 [16, 64, 8192], P(None, 'mapx', ('mapy', 'layer'))
Inputs may be any that keep to these rules, and one draw needn't show every extreme that they name: Among the faces of one mesh block (aligned blocks of 1024 rows) no owner is named more than 32 times, a bound that some block reaches.
All inputs are finite; a program needn't handle non-finite values.
Results may differ from a plain program's by a relative error of at most 0.00002.
Values sent between devices are 32-bit elements; how exact they have to be, the bound alone decides.
No kernel may reach another device: no remote copies, remote signals or barrier semaphores. Data moves between devices by JAX's collectives and lax.ppermute only.
A program may use at most 32 MiB of HBM per device.

v0:
```python
import jax
import jax.numpy as jnp
from jax import lax
from jax.sharding import PartitionSpec as P


def with_halo(cells, sides, width):
    for axis, dim in sides:
        count = lax.axis_size(axis)
        ends = count - 1
        head = lax.slice_in_dim(cells, 0, width, axis=dim)
        tail = lax.slice_in_dim(cells, cells.shape[dim] - width, cells.shape[dim], axis=dim)
        cells = jnp.concatenate(
            [
                lax.ppermute(tail, axis, [(i, (i + 1) % count) for i in range(ends)]),
                cells,
                lax.ppermute(head, axis, [((i + 1) % count, i) for i in range(ends)]),
            ],
            axis=dim,
        )
    return cells


def broadcast(x, axis, root):
    mine = lax.axis_index(axis) == root
    return lax.psum(jnp.where(mine, x, jnp.zeros_like(x)), axis)


def stencil(padded, viscous):
    center = padded[..., 1:-1, 1:-1, 1:-1]
    visc = viscous[1:-1, 1:-1, 1:-1]
    weight_x = jnp.array([1.0, 0.25], jnp.float32)[:, None, None, None]
    weight_y = jnp.array([0.25, 1.0], jnp.float32)[:, None, None, None]
    total = 2.0 * 0.5 * (visc + viscous[2:, 1:-1, 1:-1]) * (center - padded[..., 2:, 1:-1, 1:-1])
    total = total + 2.0 * 0.5 * (visc + viscous[:-2, 1:-1, 1:-1]) * (
        center - padded[..., :-2, 1:-1, 1:-1]
    )
    total = total + weight_x * 0.5 * (visc + viscous[1:-1, 2:, 1:-1]) * (
        center - padded[..., 1:-1, 2:, 1:-1]
    )
    total = total + weight_x * 0.5 * (visc + viscous[1:-1, :-2, 1:-1]) * (
        center - padded[..., 1:-1, :-2, 1:-1]
    )
    total = total + weight_y * 0.5 * (visc + viscous[1:-1, 1:-1, 2:]) * (
        center - padded[..., 1:-1, 1:-1, 2:]
    )
    total = total + weight_y * 0.5 * (visc + viscous[1:-1, 1:-1, :-2]) * (
        center - padded[..., 1:-1, 1:-1, :-2]
    )
    return total


def laplace(padded):
    return (
        4.0 * padded[..., 1:-1, 1:-1]
        - padded[..., 2:, 1:-1]
        - padded[..., :-2, 1:-1]
        - padded[..., 1:-1, 2:]
        - padded[..., 1:-1, :-2]
    )


def map_border(field):
    return with_halo(field, (("mapx", 1), (("mapy", "layer"), 2)), 1)


def slot_places(keys, group_count, capacity, keep):
    onehot = (
        (keys[:, None] == jnp.arange(group_count, dtype=jnp.int32)[None, :]) & keep[:, None]
    ).astype(jnp.int32)
    before = jnp.cumsum(onehot, axis=0) - onehot
    slot_index = jnp.sum(before * onehot, axis=1)
    return jnp.where(keep, keys * capacity + slot_index, group_count * capacity)


def shards(velocity, viscosity, friction, owner, cell, directions, stiffness):
    probes = velocity.shape[0]
    depth, rows, cols = viscosity.shape
    stacked = jnp.concatenate([velocity.reshape(probes * 2, depth, rows, cols), viscosity[None]], 0)
    extended = with_halo(stacked, (("mapx", 2), ("mapy", 3), ("layer", 1)), 1)
    padded = extended[:-1].reshape(probes, 2, depth + 2, rows + 2, cols + 2)
    image = stencil(padded, extended[-1])
    face_count = rows * cols
    face_rows = (friction * (image[:, 0, 0] + image[:, 1, 0])).reshape(probes, face_count).T
    targets = owner.reshape(face_count)
    local_cells = cell.reshape(face_count).astype(jnp.float32)
    count_y = lax.axis_size("mapy")
    count_layer = lax.axis_size("layer")
    owner_count = count_y * count_layer
    capacity = 2 * face_count // owner_count
    my_layer = lax.axis_index("layer")
    spread = broadcast(face_rows, "layer", 0)
    keep = targets % count_layer == my_layer
    position = slot_places(targets // count_layer, count_y, capacity, keep)
    total_slots = count_y * capacity
    values = (
        jnp.zeros((total_slots + 1, probes), jnp.float32).at[position].set(spread)[:total_slots]
    )
    places = jnp.zeros((total_slots + 1,), jnp.float32).at[position].set(local_cells)[:total_slots]
    got_values, got_places = (
        lax.all_to_all(
            values.reshape(count_y, capacity, probes),
            "mapy",
            split_axis=0,
            concat_axis=0,
            tiled=True,
        ),
        lax.all_to_all(
            places.reshape(count_y, capacity), "mapy", split_axis=0, concat_axis=0, tiled=True
        ),
    )
    map_rows = directions.shape[1]
    map_cols = directions.shape[2]
    summed = jax.ops.segment_sum(
        got_values.reshape(-1, probes),
        got_places.reshape(-1).astype(jnp.int32),
        num_segments=map_rows * map_cols,
    )
    data = summed.T.reshape(probes, map_rows, map_cols)
    inner = stiffness[None] * laplace(map_border(directions))
    prior = laplace(map_border(inner))
    hessian = data + prior + 0.1 * directions
    return (image, hessian)


def solution(mesh):
    return jax.shard_map(
        shards,
        mesh=mesh,
        in_specs=(
            P(None, None, "layer", "mapx", "mapy"),
            P("layer", "mapx", "mapy"),
            P("mapx", "mapy"),
            P("mapx", "mapy", None, None),
            P("mapx", "mapy", None),
            P(None, "mapx", ("mapy", "layer")),
            P("mapx", ("mapy", "layer")),
        ),
        out_specs=(P(None, None, "layer", "mapx", "mapy"), P(None, "mapx", ("mapy", "layer"))),
        check_vma=False,
    )
```

profile of v0, /device:TPU:992, one launch (start us, length us, event | category | flops | bytes accessed | tf_op | source)
XLA Modules:
  0.0 271.0 jit_solution(4010867524704770683)
XLA Ops:
  7.2 1.1 pad_maximum_fusion.6
  8.3 1.9 collective-permute-start
  10.2 3.6 %collective-permute-start.1 = (f32[33,2,1,128]{3,2,1,0:T(1,128)S(1)}, f32[33,2,1,128]{3,2,1,0:T(1,128)S(1)}, u32[]{:S(2)}, u32[]{:S(2)}) collective-permute-start(f32[33,2,1,128]{3,2,1,0:T(1,128)S(1)} %get-tuple-element.9), channel_id=1, source_target_pairs={{64,0},{128,64},{192,128},{256,192},{320,256},{384,320},{448,384},... | collective-permute-start | bytes 101384 | tf_op jit(solution)/shard_map/ppermute | solution.py:17
  13.9 0.9 fusion.46
  14.7 1.9 collective-permute-start.6
  16.6 2.4 collective-permute-start.7
  21.9 4.5 %reduce-window.6 = s32[16,8,128]{2,1,0:T(8,128)S(1)} reduce-window(s32[16,8,128]{2,1,0:T(8,128)S(1)} %fusion.21, s32[]{:T(128)} %constant.47.clone.1), window={size=1x1x128 pad=0_0x0_0x127_0}, to_apply=%region_0.1 | reduce-window | flops 2080768 | bytes 131076 | tf_op jit(solution)/shard_map/reduce-window
  28.3 4.3 %scatter_custom_fusion = f32[513]{0:T(1024)S(1)} fusion(s32[1024]{0:T(1024)S(1)} %bitcast.81, f32[1024]{0:T(1024)S(1)} %bitcast.83, f32[]{:T(128)} %constant.46.clone.1), kind=kCustom, calls=%fused_computation.109 | custom fusion | bytes 2056 | tf_op jit(solution)/shard_map/scatter | solution.py:99
  33.3 20.5 %all-to-all-start = ((f32[16,1,32]{2,1,0:T(1,128)}), f32[16,1,32]{2,1,0:T(1,128)S(1)}, u32[]{:S(2)}, u32[]{:S(2)}) async-start(f32[16,1,32]{2,1,0:T(1,128)} %all_to_all.9), calls=%async_computation | async-start | bytes 16384 | tf_op jit(solution)/shard_map/all_to_all | solution.py:108
  54.7 16.6 %collective-permute-start.8 = (f32[16,6,1]{2,1,0:T(8,128)S(1)}, f32[16,6,1]{2,1,0:T(8,128)S(1)}, u32[]{:S(2)}, u32[]{:S(2)}) collective-permute-start(f32[16,6,1]{2,1,0:T(8,128)S(1)} %get-tuple-element.12), channel_id=1, source_target_pairs={{1,0},{2,1},{3,2},{4,3},{5,4},{6,5},{7,6},{8,7},{9,8},{10,9},{11,1... | collective-permute-start | bytes 1160 | tf_op jit(solution)/shard_map/ppermute | solution.py:17
  71.3 1.9 collective-permute-start.9
  73.3 1.1 pad_maximum_fusion.2
  74.9 1.9 collective-permute-start.2
  77.2 14.7 %collective-permute-start.3 = (f32[33,2,10,1]{0,1,3,2:T(2,128)S(1)}, f32[33,2,10,1]{0,1,3,2:T(2,128)S(1)}, u32[]{:S(2)}, u32[]{:S(2)}) collective-permute-start(f32[33,2,10,1]{0,1,3,2:T(2,128)S(1)} %copy.44), channel_id=1, source_target_pairs={{4,0},{8,4},{12,8},{16,12},{20,16},{24,20},{28,24},{32,28},{36,32}... | collective-permute-start | bytes 7928 | tf_op jit(solution)/shard_map/ppermute | solution.py:17
  91.9 9.3 %collective-permute-done.9 = f32[16,6,1]{2,1,0:T(8,128)S(1)} collective-permute-done((f32[16,6,1]{2,1,0:T(8,128)S(1)}, f32[16,6,1]{2,1,0:T(8,128)S(1)}, u32[]{:S(2)}, u32[]{:S(2)}) %collective-permute-start.9) | collective-permute-done | bytes 416 | tf_op jit(solution)/shard_map/ppermute | solution.py:15
  103.9 1.3 collective-permute-start.4
  105.6 1.3 collective-permute-start.5
  106.9 1.9 collective-permute-start.10
  108.8 2.6 collective-permute-start.11
  111.5 3.2 %collective-permute-done.5 = f32[33,1,10,130]{3,1,2,0:T(1,128)S(1)} collective-permute-done((f32[33,1,10,130]{3,1,2,0:T(1,128)S(1)}, f32[33,1,10,130]{3,1,2,0:T(1,128)S(1)}, u32[]{:S(2)}, u32[]{:S(2)}) %collective-permute-start.5) | collective-permute-done | bytes 171632 | tf_op jit(solution)/shard_map/ppermute | solution.py:17
  114.7 0.8 pad_maximum_fusion
  116.0 1.1 copy.52
  117.3 1.7 fusion.2
  119.3 1.0 fusion
  120.4 72.9 %all-reduce.2.cloned.1.call-done = f32[1024,16]{1,0:T(8,128)} async-done(((f32[1024,16]{1,0:T(8,128)}), f32[1024,16]{1,0:T(8,128)}) %all-reduce.2.cloned.1.call-update) | async-done | bytes 65552 | tf_op jit(solution)/shard_map/psum | solution.py:26
  193.4 3.5 %scatter_custom_fusion.1 = f32[513,16]{1,0:T(8,128)S(1)} fusion(s32[1024]{0:T(1024)S(1)} %bitcast.82, f32[1024,16]{1,0:T(8,128)} %all-reduce.2.cloned.1.call-done, f32[]{:T(128)} %constant.46.clone.1), kind=kCustom, calls=%fused_computation.25 | custom fusion | bytes 33344 | tf_op jit(solution)/shard_map/scatter | solution.py:97
  197.8 23.3 %all-to-all-start.1 = ((f32[16,1,512]{2,1,0:T(1,128)}), f32[16,1,512]{2,1,0:T(1,128)S(1)}, u32[]{:S(2)}, u32[]{:S(2)}) async-start(f32[16,1,512]{2,1,0:T(1,128)} %reshape.278), calls=%async_computation.1 | async-start | bytes 65536 | tf_op jit(solution)/shard_map/all_to_all | solution.py:101
  221.2 15.3 %collective-permute-start.12 = (f32[16,6,1]{2,1,0:T(8,128)S(1)}, f32[16,6,1]{2,1,0:T(8,128)S(1)}, u32[]{:S(2)}, u32[]{:S(2)}) collective-permute-start(f32[16,6,1]{2,1,0:T(8,128)S(1)} %get-tuple-element.10), channel_id=1, source_target_pairs={{1,0},{2,1},{3,2},{4,3},{5,4},{6,5},{7,6},{8,7},{9,8},{10,9},{11,1... | collective-permute-start | bytes 1160 | tf_op jit(solution)/shard_map/ppermute | solution.py:17
  236.6 1.9 collective-permute-start.13
  240.7 2.4 scatter_custom_fusion.2
  243.2 20.2 %collective-permute-done.13 = f32[16,6,1]{2,1,0:T(8,128)S(1)} collective-permute-done((f32[16,6,1]{2,1,0:T(8,128)S(1)}, f32[16,6,1]{2,1,0:T(8,128)S(1)}, u32[]{:S(2)}, u32[]{:S(2)}) %collective-permute-start.13) | collective-permute-done | bytes 416 | tf_op jit(solution)/shard_map/ppermute | solution.py:15
  263.4 0.8 fusion.24
  (80 shorter events, 14.4 us)
Async XLA Ops:
  8.3 65.0 %collective-permute-start = (f32[33,2,1,128]{3,2,1,0:T(1,128)S(1)}, f32[33,2,1,128]{3,2,1,0:T(1,128)S(1)}, u32[]{:S(2)}, u32[]{:S(2)}) collective-permute-start(f32[33,2,1,128]{3,2,1,0:T(1,128)S(1)} %get-tuple-element.8), channel_id=1, source_target_pairs={{0,64},{64,128},{128,192},{192,256},{256,320},{320,384},{384,448},... | collective-permute-start | bytes 101384 | tf_op jit(solution)/shard_map/ppermute | solution.py:15
  10.2 63.1 %collective-permute-start.1 = (f32[33,2,1,128]{3,2,1,0:T(1,128)S(1)}, f32[33,2,1,128]{3,2,1,0:T(1,128)S(1)}, u32[]{:S(2)}, u32[]{:S(2)}) collective-permute-start(f32[33,2,1,128]{3,2,1,0:T(1,128)S(1)} %get-tuple-element.9), channel_id=1, source_target_pairs={{64,0},{128,64},{192,128},{256,192},{320,256},{384,320},{448,384},... | collective-permute-start | bytes 101384 | tf_op jit(solution)/shard_map/ppermute | solution.py:17
  14.7 39.1 %collective-permute-start.6 = (f32[16,1,128]{2,1,0:T(1,128)S(1)}, f32[16,1,128]{2,1,0:T(1,128)S(1)}, u32[]{:S(2)}, u32[]{:S(2)}) collective-permute-start(f32[16,1,128]{2,1,0:T(1,128)S(1)} %get-tuple-element.23), channel_id=1, source_target_pairs={{64,0},{128,64},{192,128},{256,192},{320,256},{384,320},{448,384},... | collective-permute-start | bytes 24584 | tf_op jit(solution)/shard_map/ppermute | solution.py:17
  16.6 37.2 %collective-permute-start.7 = (f32[16,1,128]{2,1,0:T(1,128)S(1)}, f32[16,1,128]{2,1,0:T(1,128)S(1)}, u32[]{:S(2)}, u32[]{:S(2)}) collective-permute-start(f32[16,1,128]{2,1,0:T(1,128)S(1)} %get-tuple-element.22), channel_id=1, source_target_pairs={{0,64},{64,128},{128,192},{192,256},{256,320},{320,384},{384,448},... | collective-permute-start | bytes 24584 | tf_op jit(solution)/shard_map/ppermute | solution.py:15
  33.3 87.1 %all-to-all-start = ((f32[16,1,32]{2,1,0:T(1,128)}), f32[16,1,32]{2,1,0:T(1,128)S(1)}, u32[]{:S(2)}, u32[]{:S(2)}) async-start(f32[16,1,32]{2,1,0:T(1,128)} %all_to_all.9), calls=%async_computation | async-start | bytes 16384 | tf_op jit(solution)/shard_map/all_to_all | solution.py:108
  53.7 139.6 %all-reduce.2.cloned.1.call-start = ((), (), s32[]{:S(2)}) async-start(), calls=%async_computation.2 | async-start | bytes 1048576 | tf_op jit(solution)/shard_map/psum | solution.py:26
  54.6 46.6 %copy-start.1 = (f32[16,4,128]{2,1,0:T(4,128)S(1)}, f32[16,4,128]{2,1,0:T(4,128)}, u32[]{:S(2)}) copy-start(f32[16,4,128]{2,1,0:T(4,128)} %param.14) | copy-start | bytes 98308
  54.6 46.6 %copy-start.4 = (f32[4,128]{1,0:T(4,128)S(1)}, f32[4,128]{1,0:T(4,128)}, u32[]{:S(2)}) copy-start(f32[4,128]{1,0:T(4,128)} %param.15) | copy-start | bytes 6148
  54.7 37.2 %collective-permute-start.8 = (f32[16,6,1]{2,1,0:T(8,128)S(1)}, f32[16,6,1]{2,1,0:T(8,128)S(1)}, u32[]{:S(2)}, u32[]{:S(2)}) collective-permute-start(f32[16,6,1]{2,1,0:T(8,128)S(1)} %get-tuple-element.12), channel_id=1, source_target_pairs={{1,0},{2,1},{3,2},{4,3},{5,4},{6,5},{7,6},{8,7},{9,8},{10,9},{11,1... | collective-permute-start | bytes 1160 | tf_op jit(solution)/shard_map/ppermute | solution.py:17
  71.3 29.8 %collective-permute-start.9 = (f32[16,6,1]{2,1,0:T(8,128)S(1)}, f32[16,6,1]{2,1,0:T(8,128)S(1)}, u32[]{:S(2)}, u32[]{:S(2)}) collective-permute-start(f32[16,6,1]{2,1,0:T(8,128)S(1)} %get-tuple-element.13), channel_id=1, source_target_pairs={{0,1},{1,2},{2,3},{3,4},{4,5},{5,6},{6,7},{7,8},{8,9},{9,10},{10,1... | collective-permute-start | bytes 1160 | tf_op jit(solution)/shard_map/ppermute | solution.py:15
  74.4 28.3 %copy-start = (f32[16,2,2,8,128]{4,3,2,1,0:T(8,128)S(1)}, f32[16,2,2,8,128]{4,3,2,1,0:T(8,128)}, u32[]{:S(2)}) copy-start(f32[16,2,2,8,128]{4,3,2,1,0:T(8,128)} %param.9) | copy-start | bytes 786436
  74.4 28.3 %copy-start.2 = (f32[2,8,128]{2,1,0:T(8,128)S(1)}, f32[2,8,128]{2,1,0:T(8,128)}, u32[]{:S(2)}) copy-start(f32[2,8,128]{2,1,0:T(8,128)} %param.10) | copy-start | bytes 24580
  74.9 26.5 %collective-permute-start.2 = (f32[33,2,10,1]{0,1,3,2:T(2,128)S(1)}, f32[33,2,10,1]{0,1,3,2:T(2,128)S(1)}, u32[]{:S(2)}, u32[]{:S(2)}) collective-permute-start(f32[33,2,10,1]{0,1,3,2:T(2,128)S(1)} %copy.43), channel_id=1, source_target_pairs={{0,4},{4,8},{8,12},{12,16},{16,20},{20,24},{24,28},{28,32},{32,36}... | collective-permute-start | bytes 7928 | tf_op jit(solution)/shard_map/ppermute | solution.py:15
  77.2 24.9 %collective-permute-start.3 = (f32[33,2,10,1]{0,1,3,2:T(2,128)S(1)}, f32[33,2,10,1]{0,1,3,2:T(2,128)S(1)}, u32[]{:S(2)}, u32[]{:S(2)}) collective-permute-start(f32[33,2,10,1]{0,1,3,2:T(2,128)S(1)} %copy.44), channel_id=1, source_target_pairs={{4,0},{8,4},{12,8},{16,12},{20,16},{24,20},{28,24},{32,28},{36,32}... | collective-permute-start | bytes 7928 | tf_op jit(solution)/shard_map/ppermute | solution.py:17
  103.9 7.5 %collective-permute-start.4 = (f32[33,1,10,130]{3,1,2,0:T(1,128)S(1)}, f32[33,1,10,130]{3,1,2,0:T(1,128)S(1)}, u32[]{:S(2)}, u32[]{:S(2)}) collective-permute-start(f32[33,1,10,130]{3,1,2,0:T(1,128)S(1)} %copy.47), channel_id=1, source_target_pairs={{0,1},{1,2},{2,3},{4,5},{5,6},{6,7},{8,9},{9,10},{10,11},{12,13},{... | collective-permute-start | bytes 514808 | tf_op jit(solution)/shard_map/ppermute | solution.py:15
  105.6 9.1 %collective-permute-start.5 = (f32[33,1,10,130]{3,1,2,0:T(1,128)S(1)}, f32[33,1,10,130]{3,1,2,0:T(1,128)S(1)}, u32[]{:S(2)}, u32[]{:S(2)}) collective-permute-start(f32[33,1,10,130]{3,1,2,0:T(1,128)S(1)} %copy.48), channel_id=1, source_target_pairs={{1,0},{2,1},{3,2},{5,4},{6,5},{7,6},{9,8},{10,9},{11,10},{13,12},{... | collective-permute-start | bytes 514808 | tf_op jit(solution)/shard_map/ppermute | solution.py:17
  106.9 114.2 %collective-permute-start.10 = (f32[16,1,128]{2,1,0:T(1,128)S(1)}, f32[16,1,128]{2,1,0:T(1,128)S(1)}, u32[]{:S(2)}, u32[]{:S(2)}) collective-permute-start(f32[16,1,128]{2,1,0:T(1,128)S(1)} %get-tuple-element.21), channel_id=1, source_target_pairs={{64,0},{128,64},{192,128},{256,192},{320,256},{384,320},{448,384},... | collective-permute-start | bytes 24584 | tf_op jit(solution)/shard_map/ppermute | solution.py:17
  108.8 112.3 %collective-permute-start.11 = (f32[16,1,128]{2,1,0:T(1,128)S(1)}, f32[16,1,128]{2,1,0:T(1,128)S(1)}, u32[]{:S(2)}, u32[]{:S(2)}) collective-permute-start(f32[16,1,128]{2,1,0:T(1,128)S(1)} %get-tuple-element.20), channel_id=1, source_target_pairs={{0,64},{64,128},{128,192},{192,256},{256,320},{320,384},{384,448},... | collective-permute-start | bytes 24584 | tf_op jit(solution)/shard_map/ppermute | solution.py:15
  115.8 1.3 copy-start.5
  115.9 1.3 copy-start.6
  117.2 2.1 copy-start.3
  197.8 41.4 %all-to-all-start.1 = ((f32[16,1,512]{2,1,0:T(1,128)}), f32[16,1,512]{2,1,0:T(1,128)S(1)}, u32[]{:S(2)}, u32[]{:S(2)}) async-start(f32[16,1,512]{2,1,0:T(1,128)} %reshape.278), calls=%async_computation.1 | async-start | bytes 65536 | tf_op jit(solution)/shard_map/all_to_all | solution.py:101
  221.2 22.0 %collective-permute-start.12 = (f32[16,6,1]{2,1,0:T(8,128)S(1)}, f32[16,6,1]{2,1,0:T(8,128)S(1)}, u32[]{:S(2)}, u32[]{:S(2)}) collective-permute-start(f32[16,6,1]{2,1,0:T(8,128)S(1)} %get-tuple-element.10), channel_id=1, source_target_pairs={{1,0},{2,1},{3,2},{4,3},{5,4},{6,5},{7,6},{8,7},{9,8},{10,9},{11,1... | collective-permute-start | bytes 1160 | tf_op jit(solution)/shard_map/ppermute | solution.py:17
  236.6 26.8 %collective-permute-start.13 = (f32[16,6,1]{2,1,0:T(8,128)S(1)}, f32[16,6,1]{2,1,0:T(8,128)S(1)}, u32[]{:S(2)}, u32[]{:S(2)}) collective-permute-start(f32[16,6,1]{2,1,0:T(8,128)S(1)} %get-tuple-element.11), channel_id=1, source_target_pairs={{0,1},{1,2},{2,3},{3,4},{4,5},{5,6},{6,7},{7,8},{8,9},{9,10},{10,1... | collective-permute-start | bytes 1160 | tf_op jit(solution)/shard_map/ppermute | solution.py:15
Sparse Core Ops, SparseCore 0:
  120.4 72.8 all-reduce.1
where the time goes:
time: 272 us; the launch traced here: 271 us
  starting transfers between devices  113 us (42%)
  waiting for transfers between devices  106 us (39%)
  other arithmetic  20.6 us (8%)
  local copies, waits for them, and re-layouts  17 us (6%)
  between operations  14.6 us (5%)
    psum x1, waiting for transfers between devices, broadcast(): return lax.psum(jnp.where(mine, x, jnp.zeros_like(x)), axis)  72.9 us
    ppermute x7, starting transfers between devices, with_halo(): lax.ppermute(head, axis, [((i + 1) % count, i) for i in range(ends)])  55.5 us
    ppermute x7, waiting for transfers between devices, with_halo(): lax.ppermute(tail, axis, [(i, (i + 1) % count) for i in range(ends)])  29.5 us
    all_to_all x1, starting transfers between devices, shards(): lax.all_to_all(values.reshape(count_y, capacity, probes), 'mapy', split_a...  23.3 us
    all_to_all x1, starting transfers between devices, shards(): lax.all_to_all(places.reshape(count_y, capacity), 'mapy', split_axis=0, c...  20.5 us
    ppermute x7, starting transfers between devices, with_halo(): lax.ppermute(tail, axis, [(i, (i + 1) % count) for i in range(ends)])  14 us
  transfers between devices with their start and end apart: 17, of which 4 were waited for; matrix products, arithmetic and copies ran while one was open for 13% of the time, Pallas kernels for 0%

commit v1 on v0

--- a/solution.py
+++ b/solution.py
@@ -4,26 +4,31 @@
 from jax.sharding import PartitionSpec as P
 
 
-def with_halo(cells, sides, width):
-    for axis, dim in sides:
-        count = lax.axis_size(axis)
-        ends = count - 1
-        head = lax.slice_in_dim(cells, 0, width, axis=dim)
-        tail = lax.slice_in_dim(cells, cells.shape[dim] - width, cells.shape[dim], axis=dim)
-        cells = jnp.concatenate(
-            [
-                lax.ppermute(tail, axis, [(i, (i + 1) % count) for i in range(ends)]),
-                cells,
-                lax.ppermute(head, axis, [((i + 1) % count, i) for i in range(ends)]),
-            ],
-            axis=dim,
-        )
-    return cells
+def halo_pair(cells, axis, dim):
+    count = lax.axis_size(axis)
+    head = lax.slice_in_dim(cells, 0, 1, axis=dim)
+    tail = lax.slice_in_dim(cells, cells.shape[dim] - 1, cells.shape[dim], axis=dim)
+    low = lax.ppermute(tail, axis, [(i, i + 1) for i in range(count - 1)])
+    high = lax.ppermute(head, axis, [(i + 1, i) for i in range(count - 1)])
+    return low, high
 
 
-def broadcast(x, axis, root):
-    mine = lax.axis_index(axis) == root
-    return lax.psum(jnp.where(mine, x, jnp.zeros_like(x)), axis)
+def pad_others(part, lead, done):
+    widths = [(0, 0)] * part.ndim
+    for dim in done:
+        widths[dim] = (1, 1)
+    return jnp.pad(part, widths) if done else part
+
+
+def with_faces(cells, sides):
+    parts = [halo_pair(cells, axis, dim) for axis, dim in sides]
+    done = []
+    for (axis, dim), (low, high) in zip(sides, parts):
+        cells = jnp.concatenate(
+            [pad_others(low, 0, done), cells, pad_others(high, 0, done)], axis=dim
+        )
+        done.append(dim)
+    return cells
 
 
 def stencil(padded, viscous):
@@ -61,7 +66,16 @@
 
 
 def map_border(field):
-    return with_halo(field, (("mapx", 1), (("mapy", "layer"), 2)), 1)
+    return with_faces(field, (("mapx", 1), (("mapy", "layer"), 2)))
+
+
+def from_bottom(x, axis):
+    count = lax.axis_size(axis)
+    mine = lax.axis_index(axis) == 0
+    total = jnp.where(mine, x, jnp.zeros_like(x))
+    for to in range(1, count):
+        total = total + lax.ppermute(x, axis, [(0, to)])
+    return total
 
 
 def slot_places(keys, group_count, capacity, keep):
@@ -77,7 +91,7 @@
     probes = velocity.shape[0]
     depth, rows, cols = viscosity.shape
     stacked = jnp.concatenate([velocity.reshape(probes * 2, depth, rows, cols), viscosity[None]], 0)
-    extended = with_halo(stacked, (("mapx", 2), ("mapy", 3), ("layer", 1)), 1)
+    extended = with_faces(stacked, (("layer", 1), ("mapx", 2), ("mapy", 3)))
     padded = extended[:-1].reshape(probes, 2, depth + 2, rows + 2, cols + 2)
     image = stencil(padded, extended[-1])
     face_count = rows * cols
@@ -89,31 +103,26 @@
     owner_count = count_y * count_layer
     capacity = 2 * face_count // owner_count
     my_layer = lax.axis_index("layer")
-    spread = broadcast(face_rows, "layer", 0)
+    spread = from_bottom(face_rows, "layer")
     keep = targets % count_layer == my_layer
     position = slot_places(targets // count_layer, count_y, capacity, keep)
     total_slots = count_y * capacity
-    values = (
-        jnp.zeros((total_slots + 1, probes), jnp.float32).at[position].set(spread)[:total_slots]
+    rows_out = jnp.concatenate([spread, local_cells[:, None]], axis=1)
+    packed = (
+        jnp.zeros((total_slots + 1, probes + 1), jnp.float32).at[position].set(rows_out)[:total_slots]
     )
-    places = jnp.zeros((total_slots + 1,), jnp.float32).at[position].set(local_cells)[:total_slots]
-    got_values, got_places = (
-        lax.all_to_all(
-            values.reshape(count_y, capacity, probes),
-            "mapy",
-            split_axis=0,
-            concat_axis=0,
-            tiled=True,
-        ),
-        lax.all_to_all(
-            places.reshape(count_y, capacity), "mapy", split_axis=0, concat_axis=0, tiled=True
-        ),
-    )
+    got = lax.all_to_all(
+        packed.reshape(count_y, capacity, probes + 1),
+        "mapy",
+        split_axis=0,
+        concat_axis=0,
+        tiled=True,
+    ).reshape(-1, probes + 1)
     map_rows = directions.shape[1]
     map_cols = directions.shape[2]
     summed = jax.ops.segment_sum(
-        got_values.reshape(-1, probes),
-        got_places.reshape(-1).astype(jnp.int32),
+        got[:, :probes],
+        got[:, probes].astype(jnp.int32),
         num_segments=map_rows * map_cols,
     )
     data = summed.T.reshape(probes, map_rows, map_cols)

time: 272 us -> 177 us (0.65)
  the two profiles are of different devices: /device:TPU:992 before, /device:TPU:191 now
where the time goes in v1:
time: 177 us
  starting transfers between devices  108 us (61%)
  waiting for transfers between devices  42 us (24%)
  other arithmetic  17.8 us (10%)
  local copies, waits for them, and re-layouts  7.95 us (4%)
    ppermute x7, starting transfers between devices, halo_pair(): low = lax.ppermute(tail, axis, [(i, i + 1) for i in range(count - 1)])  57.8 us
    all_to_all x1, starting transfers between devices, shards(): lax.all_to_all(packed.reshape(count_y, capacity, probes + 1), 'mapy', spl...  30.9 us
    ppermute x7, waiting for transfers between devices, halo_pair(): high = lax.ppermute(head, axis, [(i + 1, i) for i in range(count - 1)])  27.2 us
    ppermute x7, starting transfers between devices, halo_pair(): high = lax.ppermute(head, axis, [(i + 1, i) for i in range(count - 1)])  16.3 us
    ppermute x7, waiting for transfers between devices, halo_pair(): low = lax.ppermute(tail, axis, [(i, i + 1) for i in range(count - 1)])  12.3 us
    another operation x3, other arithmetic  4.64 us
  transfers between devices with their start and end apart: 18, of which 5 were waited for; matrix products, arithmetic and copies ran while one was open for 11% of the time, Pallas kernels for 0%

profile of v1, /device:TPU:191, one launch (start us, length us, event | category | flops | bytes accessed | tf_op | source)
XLA Modules:
  0.0 176.5 jit_solution(8205275638192415671)
XLA Ops:
  0.7 1.2 fusion.5
  1.9 2.5 %collective-permute-start.5 = (f32[33,2,8,1]{3,2,1,0:T(8,128)S(1)}, f32[33,2,8,1]{3,2,1,0:T(8,128)S(1)}, u32[]{:S(2)}, u32[]{:S(2)}) collective-permute-start(f32[33,2,8,1]{3,2,1,0:T(8,128)S(1)} %get-tuple-element.5), channel_id=1, source_target_pairs={{4,0},{8,4},{12,8},{16,12},{20,16},{24,20},{28,24},{32,28},{36,32}... | collective-permute-start | bytes 6344 | tf_op jit(solution)/shard_map/ppermute | solution.py:12
  4.4 1.1 fusion.31
  5.5 2.9 %collective-permute-start.4 = (f32[33,2,1,128]{3,2,1,0:T(1,128)S(1)}, f32[33,2,1,128]{3,2,1,0:T(1,128)S(1)}, u32[]{:S(2)}, u32[]{:S(2)}) collective-permute-start(f32[33,2,1,128]{3,2,1,0:T(1,128)S(1)} %get-tuple-element.7), channel_id=1, source_target_pairs={{64,0},{128,64},{192,128},{256,192},{320,256},{384,320},{448,384},... | collective-permute-start | bytes 101384 | tf_op jit(solution)/shard_map/ppermute | solution.py:12
  8.3 3.4 %collective-permute-start.1 = (f32[33,2,1,128]{3,2,1,0:T(1,128)S(1)}, f32[33,2,1,128]{3,2,1,0:T(1,128)S(1)}, u32[]{:S(2)}, u32[]{:S(2)}) collective-permute-start(f32[33,2,1,128]{3,2,1,0:T(1,128)S(1)} %get-tuple-element.6), channel_id=1, source_target_pairs={{0,64},{64,128},{128,192},{192,256},{256,320},{320,384},{384,448},... | collective-permute-start | bytes 101384 | tf_op jit(solution)/shard_map/ppermute | solution.py:11
  11.8 14.5 %collective-permute-start = (f32[33,2,8,1]{3,2,1,0:T(8,128)S(1)}, f32[33,2,8,1]{3,2,1,0:T(8,128)S(1)}, u32[]{:S(2)}, u32[]{:S(2)}) collective-permute-start(f32[33,2,8,1]{3,2,1,0:T(8,128)S(1)} %get-tuple-element.4), channel_id=1, source_target_pairs={{0,4},{4,8},{8,12},{12,16},{16,20},{20,24},{24,28},{28,32},{32,36}... | collective-permute-start | bytes 6344 | tf_op jit(solution)/shard_map/ppermute | solution.py:11
  26.3 1.0 fusion.17
  27.3 2.4 %collective-permute-start.3 = (f32[33,1,8,128]{3,2,1,0:T(8,128)S(1)}, f32[33,1,8,128]{3,2,1,0:T(8,128)S(1)}, u32[]{:S(2)}, u32[]{:S(2)}) collective-permute-start(f32[33,1,8,128]{3,2,1,0:T(8,128)S(1)} %get-tuple-element.3), channel_id=1, source_target_pairs={{1,0},{2,1},{3,2},{5,4},{6,5},{7,6},{9,8},{10,9},{11,10},{13,12},{... | collective-permute-start | bytes 405512 | tf_op jit(solution)/shard_map/ppermute | solution.py:12
  32.5 0.9 fusion.55
  33.4 0.9 fusion.56
  34.3 4.5 %reduce-window.6 = s32[16,8,128]{2,1,0:T(8,128)S(1)} reduce-window(s32[16,8,128]{2,1,0:T(8,128)S(1)} %fusion.29, s32[]{:T(128)} %constant.47.clone.1), window={size=1x1x128 pad=0_0x0_0x127_0}, to_apply=%region_0.1 | reduce-window | flops 2080768 | bytes 131076 | tf_op jit(solution)/shard_map/reduce-window
  39.3 6.0 %collective-permute-done.5 = f32[33,2,8,1]{3,2,1,0:T(8,128)S(1)} collective-permute-done((f32[33,2,8,1]{3,2,1,0:T(8,128)S(1)}, f32[33,2,8,1]{3,2,1,0:T(8,128)S(1)}, u32[]{:S(2)}, u32[]{:S(2)}) %collective-permute-start.5) | collective-permute-done | bytes 2144 | tf_op jit(solution)/shard_map/ppermute | solution.py:12
  45.4 1.3 collective-permute-start.2
  46.7 12.2 %collective-permute-done = f32[33,2,8,1]{3,2,1,0:T(8,128)S(1)} collective-permute-done((f32[33,2,8,1]{3,2,1,0:T(8,128)S(1)}, f32[33,2,8,1]{3,2,1,0:T(8,128)S(1)}, u32[]{:S(2)}, u32[]{:S(2)}) %collective-permute-start) | collective-permute-done | bytes 2144 | tf_op jit(solution)/shard_map/ppermute | solution.py:11
  58.9 14.7 %collective-permute-start.12 = (f32[16,4,1]{2,1,0:T(4,128)S(1)}, f32[16,4,1]{2,1,0:T(4,128)S(1)}, u32[]{:S(2)}, u32[]{:S(2)}) collective-permute-start(f32[16,4,1]{2,1,0:T(4,128)S(1)} %get-tuple-element.19), channel_id=1, source_target_pairs={{0,1},{1,2},{2,3},{3,4},{4,5},{5,6},{6,7},{7,8},{8,9},{9,10},{10,1... | collective-permute-start | bytes 776 | tf_op jit(solution)/shard_map/ppermute | solution.py:11
  73.6 2.8 %collective-permute-start.9 = (f32[16,1,128]{2,1,0:T(1,128)S(1)}, f32[16,1,128]{2,1,0:T(1,128)S(1)}, u32[]{:S(2)}, u32[]{:S(2)}) collective-permute-start(f32[16,1,128]{2,1,0:T(1,128)S(1)} %get-tuple-element.21), channel_id=1, source_target_pairs={{64,0},{128,64},{192,128},{256,192},{320,256},{384,320},{448,384},... | collective-permute-start | bytes 24584 | tf_op jit(solution)/shard_map/ppermute | solution.py:12
  76.4 8.8 %collective-permute-start.10 = (f32[16,1,128]{2,1,0:T(1,128)S(1)}, f32[16,1,128]{2,1,0:T(1,128)S(1)}, u32[]{:S(2)}, u32[]{:S(2)}) collective-permute-start(f32[16,1,128]{2,1,0:T(1,128)S(1)} %get-tuple-element.20), channel_id=1, source_target_pairs={{0,64},{64,128},{128,192},{192,256},{256,320},{320,384},{384,448},... | collective-permute-start | bytes 24584 | tf_op jit(solution)/shard_map/ppermute | solution.py:11
  85.2 1.9 %collective-permute-start.11 = (f32[16,4,1]{2,1,0:T(4,128)S(1)}, f32[16,4,1]{2,1,0:T(4,128)S(1)}, u32[]{:S(2)}, u32[]{:S(2)}) collective-permute-start(f32[16,4,1]{2,1,0:T(4,128)S(1)} %get-tuple-element.18), channel_id=1, source_target_pairs={{1,0},{2,1},{3,2},{4,3},{5,4},{6,5},{7,6},{8,7},{9,8},{10,9},{11,1... | collective-permute-start | bytes 776 | tf_op jit(solution)/shard_map/ppermute | solution.py:12
  87.2 1.1 select_maximum_fusion
  89.6 1.3 collective-permute-start.8
  91.6 11.3 %collective-permute-done.11 = f32[16,4,1]{2,1,0:T(4,128)S(1)} collective-permute-done((f32[16,4,1]{2,1,0:T(4,128)S(1)}, f32[16,4,1]{2,1,0:T(4,128)S(1)}, u32[]{:S(2)}, u32[]{:S(2)}) %collective-permute-start.11) | collective-permute-done | bytes 288 | tf_op jit(solution)/shard_map/ppermute | solution.py:12
  104.0 3.1 %scatter_custom_fusion = f32[513,17]{1,0:T(8,128)S(1)} fusion(s32[1024]{0:T(1024)S(1)} %bitcast.90, f32[1024,17]{1,0:T(8,128)S(1)} %copy.32, f32[]{:T(128)} %constant.45.clone.1), kind=kCustom, calls=%fused_computation.46 | custom fusion | bytes 34888 | tf_op jit(solution)/shard_map/scatter | solution.py:112
  107.4 0.7 reshape.253
  108.1 30.9 %all-to-all-start = ((f32[16,1,544]{2,1,0:T(1,128)}), f32[16,1,544]{2,1,0:T(1,128)S(1)}, u32[]{:S(2)}, u32[]{:S(2)}) async-start(f32[16,1,544]{2,1,0:T(1,128)} %reshape.253), calls=%async_computation | async-start | bytes 81920 | tf_op jit(solution)/shard_map/all_to_all | solution.py:114
  139.0 10.3 %collective-permute-start.16 = (f32[16,4,1]{2,1,0:T(4,128)S(1)}, f32[16,4,1]{2,1,0:T(4,128)S(1)}, u32[]{:S(2)}, u32[]{:S(2)}) collective-permute-start(f32[16,4,1]{2,1,0:T(4,128)S(1)} %get-tuple-element.15), channel_id=1, source_target_pairs={{0,1},{1,2},{2,3},{3,4},{4,5},{5,6},{6,7},{7,8},{8,9},{9,10},{10,1... | collective-permute-start | bytes 776 | tf_op jit(solution)/shard_map/ppermute | solution.py:11
  149.4 1.9 %collective-permute-start.13 = (f32[16,1,128]{2,1,0:T(1,128)S(1)}, f32[16,1,128]{2,1,0:T(1,128)S(1)}, u32[]{:S(2)}, u32[]{:S(2)}) collective-permute-start(f32[16,1,128]{2,1,0:T(1,128)S(1)} %get-tuple-element.17), channel_id=1, source_target_pairs={{64,0},{128,64},{192,128},{256,192},{320,256},{384,320},{448,384},... | collective-permute-start | bytes 24584 | tf_op jit(solution)/shard_map/ppermute | solution.py:12
  151.3 4.8 %collective-permute-start.14 = (f32[16,1,128]{2,1,0:T(1,128)S(1)}, f32[16,1,128]{2,1,0:T(1,128)S(1)}, u32[]{:S(2)}, u32[]{:S(2)}) collective-permute-start(f32[16,1,128]{2,1,0:T(1,128)S(1)} %get-tuple-element.16), channel_id=1, source_target_pairs={{0,64},{64,128},{128,192},{192,256},{256,320},{320,384},{384,448},... | collective-permute-start | bytes 24584 | tf_op jit(solution)/shard_map/ppermute | solution.py:11
  156.1 1.9 %collective-permute-start.15 = (f32[16,4,1]{2,1,0:T(4,128)S(1)}, f32[16,4,1]{2,1,0:T(4,128)S(1)}, u32[]{:S(2)}, u32[]{:S(2)}) collective-permute-start(f32[16,4,1]{2,1,0:T(4,128)S(1)} %get-tuple-element.14), channel_id=1, source_target_pairs={{1,0},{2,1},{3,2},{4,3},{5,4},{6,5},{7,6},{8,7},{9,8},{10,9},{11,1... | collective-permute-start | bytes 776 | tf_op jit(solution)/shard_map/ppermute | solution.py:12
  158.0 2.6 %all-to-all-done = f32[16,1,544]{2,1,0:T(1,128)S(1)} async-done(((f32[16,1,544]{2,1,0:T(1,128)}), f32[16,1,544]{2,1,0:T(1,128)S(1)}, u32[]{:S(2)}, u32[]{:S(2)}) %all-to-all-start) | async-done | bytes 34848 | tf_op jit(solution)/shard_map/all_to_all | solution.py:114
  162.3 3.5 %scatter_custom_fusion.1 = f32[512,16]{1,0:T(8,128)S(1)} fusion(s32[512]{0:T(512)S(1)} %bitcast.91, f32[512,16]{1,0:T(8,128)S(1)} %copy.35, f32[]{:T(128)} %constant.45.clone.1), kind=kCustom, calls=%fused_computation.48 | custom fusion | flops 8192 | bytes 32772 | tf_op jit(solution)/shard_map/scatter-add | solution.py:123
  165.9 9.9 %collective-permute-done.15 = f32[16,4,1]{2,1,0:T(4,128)S(1)} collective-permute-done((f32[16,4,1]{2,1,0:T(4,128)S(1)}, f32[16,4,1]{2,1,0:T(4,128)S(1)}, u32[]{:S(2)}, u32[]{:S(2)}) %collective-permute-start.15) | collective-permute-done | bytes 288 | tf_op jit(solution)/shard_map/ppermute | solution.py:12
  175.7 0.8 fusion.35
  (73 shorter events, 8.3 us)
Async XLA Ops:
  0.6 86.6 %copy-start.3 = (f32[2,8,128]{2,1,0:T(8,128)S(1)}, f32[2,8,128]{2,1,0:T(8,128)}, u32[]{:S(2)}) copy-start(f32[2,8,128]{2,1,0:T(8,128)} %param.10) | copy-start | bytes 24580
  0.6 86.6 %copy-start = (f32[16,2,2,8,128]{4,3,2,1,0:T(8,128)S(1)}, f32[16,2,2,8,128]{4,3,2,1,0:T(8,128)}, u32[]{:S(2)}) copy-start(f32[16,2,2,8,128]{4,3,2,1,0:T(8,128)} %param.9) | copy-start | bytes 786436
  0.7 38.6 %copy-start.4 = (s32[1,1,1024,1]{2,3,1,0:T(1,128)S(1)}, s32[1,1,1024,1]{2,3,1,0:T(1,128)}, u32[]{:S(2)}) copy-start(s32[1,1,1024,1]{2,3,1,0:T(1,128)} %param.12) | copy-start | bytes 12292
  0.7 46.0 %copy-start.6 = (s32[1,1,1024]{2,1,0:T(1,128)S(1)}, s32[1,1,1024]{2,1,0:T(1,128)}, u32[]{:S(2)}) copy-start(s32[1,1,1024]{2,1,0:T(1,128)} %param.13) | copy-start | bytes 12292
  1.9 43.5 %collective-permute-start.5 = (f32[33,2,8,1]{3,2,1,0:T(8,128)S(1)}, f32[33,2,8,1]{3,2,1,0:T(8,128)S(1)}, u32[]{:S(2)}, u32[]{:S(2)}) collective-permute-start(f32[33,2,8,1]{3,2,1,0:T(8,128)S(1)} %get-tuple-element.5), channel_id=1, source_target_pairs={{4,0},{8,4},{12,8},{16,12},{20,16},{24,20},{28,24},{32,28},{36,32}... | collective-permute-start | bytes 6344 | tf_op jit(solution)/shard_map/ppermute | solution.py:12
  5.5 68.1 %collective-permute-start.4 = (f32[33,2,1,128]{3,2,1,0:T(1,128)S(1)}, f32[33,2,1,128]{3,2,1,0:T(1,128)S(1)}, u32[]{:S(2)}, u32[]{:S(2)}) collective-permute-start(f32[33,2,1,128]{3,2,1,0:T(1,128)S(1)} %get-tuple-element.7), channel_id=1, source_target_pairs={{64,0},{128,64},{192,128},{256,192},{320,256},{384,320},{448,384},... | collective-permute-start | bytes 101384 | tf_op jit(solution)/shard_map/ppermute | solution.py:12
  8.3 68.1 %collective-permute-start.1 = (f32[33,2,1,128]{3,2,1,0:T(1,128)S(1)}, f32[33,2,1,128]{3,2,1,0:T(1,128)S(1)}, u32[]{:S(2)}, u32[]{:S(2)}) collective-permute-start(f32[33,2,1,128]{3,2,1,0:T(1,128)S(1)} %get-tuple-element.6), channel_id=1, source_target_pairs={{0,64},{64,128},{128,192},{192,256},{256,320},{320,384},{384,448},... | collective-permute-start | bytes 101384 | tf_op jit(solution)/shard_map/ppermute | solution.py:11
  11.8 47.1 %collective-permute-start = (f32[33,2,8,1]{3,2,1,0:T(8,128)S(1)}, f32[33,2,8,1]{3,2,1,0:T(8,128)S(1)}, u32[]{:S(2)}, u32[]{:S(2)}) collective-permute-start(f32[33,2,8,1]{3,2,1,0:T(8,128)S(1)} %get-tuple-element.4), channel_id=1, source_target_pairs={{0,4},{4,8},{8,12},{12,16},{16,20},{20,24},{24,28},{28,32},{32,36}... | collective-permute-start | bytes 6344 | tf_op jit(solution)/shard_map/ppermute | solution.py:11
  27.3 57.9 %collective-permute-start.3 = (f32[33,1,8,128]{3,2,1,0:T(8,128)S(1)}, f32[33,1,8,128]{3,2,1,0:T(8,128)S(1)}, u32[]{:S(2)}, u32[]{:S(2)}) collective-permute-start(f32[33,1,8,128]{3,2,1,0:T(8,128)S(1)} %get-tuple-element.3), channel_id=1, source_target_pairs={{1,0},{2,1},{3,2},{5,4},{6,5},{7,6},{9,8},{10,9},{11,10},{13,12},{... | collective-permute-start | bytes 405512 | tf_op jit(solution)/shard_map/ppermute | solution.py:12
  45.4 41.8 %collective-permute-start.2 = (f32[33,1,8,128]{3,2,1,0:T(8,128)S(1)}, f32[33,1,8,128]{3,2,1,0:T(8,128)S(1)}, u32[]{:S(2)}, u32[]{:S(2)}) collective-permute-start(f32[33,1,8,128]{3,2,1,0:T(8,128)S(1)} %get-tuple-element.2), channel_id=1, source_target_pairs={{0,1},{1,2},{2,3},{4,5},{5,6},{6,7},{8,9},{9,10},{10,11},{12,13},{... | collective-permute-start | bytes 405512 | tf_op jit(solution)/shard_map/ppermute | solution.py:11
  58.9 32.0 %collective-permute-start.12 = (f32[16,4,1]{2,1,0:T(4,128)S(1)}, f32[16,4,1]{2,1,0:T(4,128)S(1)}, u32[]{:S(2)}, u32[]{:S(2)}) collective-permute-start(f32[16,4,1]{2,1,0:T(4,128)S(1)} %get-tuple-element.19), channel_id=1, source_target_pairs={{0,1},{1,2},{2,3},{3,4},{4,5},{5,6},{6,7},{7,8},{8,9},{9,10},{10,1... | collective-permute-start | bytes 776 | tf_op jit(solution)/shard_map/ppermute | solution.py:11
  73.6 29.9 %collective-permute-start.9 = (f32[16,1,128]{2,1,0:T(1,128)S(1)}, f32[16,1,128]{2,1,0:T(1,128)S(1)}, u32[]{:S(2)}, u32[]{:S(2)}) collective-permute-start(f32[16,1,128]{2,1,0:T(1,128)S(1)} %get-tuple-element.21), channel_id=1, source_target_pairs={{64,0},{128,64},{192,128},{256,192},{320,256},{384,320},{448,384},... | collective-permute-start | bytes 24584 | tf_op jit(solution)/shard_map/ppermute | solution.py:12
  76.4 27.1 %collective-permute-start.10 = (f32[16,1,128]{2,1,0:T(1,128)S(1)}, f32[16,1,128]{2,1,0:T(1,128)S(1)}, u32[]{:S(2)}, u32[]{:S(2)}) collective-permute-start(f32[16,1,128]{2,1,0:T(1,128)S(1)} %get-tuple-element.20), channel_id=1, source_target_pairs={{0,64},{64,128},{128,192},{192,256},{256,320},{320,384},{384,448},... | collective-permute-start | bytes 24584 | tf_op jit(solution)/shard_map/ppermute | solution.py:11
  85.2 17.6 %collective-permute-start.11 = (f32[16,4,1]{2,1,0:T(4,128)S(1)}, f32[16,4,1]{2,1,0:T(4,128)S(1)}, u32[]{:S(2)}, u32[]{:S(2)}) collective-permute-start(f32[16,4,1]{2,1,0:T(4,128)S(1)} %get-tuple-element.18), channel_id=1, source_target_pairs={{1,0},{2,1},{3,2},{4,3},{5,4},{6,5},{7,6},{8,7},{9,8},{10,9},{11,1... | collective-permute-start | bytes 776 | tf_op jit(solution)/shard_map/ppermute | solution.py:12
  88.3 0.7 copy-start.8
  88.3 0.7 copy-start.9
  88.5 1.0 copy-start.5
  88.5 15.0 %copy-start.1 = (f32[16,4,128]{2,1,0:T(4,128)S(1)}, f32[16,4,128]{2,1,0:T(4,128)}, u32[]{:S(2)}) copy-start(f32[16,4,128]{2,1,0:T(4,128)} %param.14) | copy-start | bytes 98308
  88.6 15.0 %copy-start.7 = (f32[4,128]{1,0:T(4,128)S(1)}, f32[4,128]{1,0:T(4,128)}, u32[]{:S(2)}) copy-start(f32[4,128]{1,0:T(4,128)} %param.15) | copy-start | bytes 6148
  89.5 72.7 %copy-start.2 = (f32[16,2,2,8,128]{4,3,2,1,0:T(8,128)}, f32[16,2,2,8,128]{4,3,2,1,0:T(8,128)S(1)}, u32[]{:S(2)}) copy-start(f32[16,2,2,8,128]{4,3,2,1,0:T(8,128)S(1)} %fusion.7) | copy-start | bytes 786436
  89.6 14.2 %collective-permute-start.8 = (f32[1024,16]{0,1:T(8,128)S(1)}, f32[1024,16]{0,1:T(8,128)S(1)}, u32[]{:S(2)}, u32[]{:S(2)}) collective-permute-start(f32[1024,16]{0,1:T(8,128)S(1)} %fusion.23), channel_id=1, source_target_pairs={{0,3},{4,7},{8,11},{12,15},{16,19},{20,23},{24,27},{28,31},{32,35}... | collective-permute-start | bytes 196616 | tf_op jit(solution)/shard_map/ppermute | solution.py:77
  90.9 12.9 %collective-permute-start.7 = (f32[1024,16]{0,1:T(8,128)S(1)}, f32[1024,16]{0,1:T(8,128)S(1)}, u32[]{:S(2)}, u32[]{:S(2)}) collective-permute-start(f32[1024,16]{0,1:T(8,128)S(1)} %fusion.23), channel_id=1, source_target_pairs={{0,2},{4,6},{8,10},{12,14},{16,18},{20,22},{24,26},{28,30},{32,34}... | collective-permute-start | bytes 196616 | tf_op jit(solution)/shard_map/ppermute | solution.py:77
  102.8 0.9 collective-permute-start.6
  108.1 52.5 %all-to-all-start = ((f32[16,1,544]{2,1,0:T(1,128)}), f32[16,1,544]{2,1,0:T(1,128)S(1)}, u32[]{:S(2)}, u32[]{:S(2)}) async-start(f32[16,1,544]{2,1,0:T(1,128)} %reshape.253), calls=%async_computation | async-start | bytes 81920 | tf_op jit(solution)/shard_map/all_to_all | solution.py:114
  139.0 26.8 %collective-permute-start.16 = (f32[16,4,1]{2,1,0:T(4,128)S(1)}, f32[16,4,1]{2,1,0:T(4,128)S(1)}, u32[]{:S(2)}, u32[]{:S(2)}) collective-permute-start(f32[16,4,1]{2,1,0:T(4,128)S(1)} %get-tuple-element.15), channel_id=1, source_target_pairs={{0,1},{1,2},{2,3},{3,4},{4,5},{5,6},{6,7},{7,8},{8,9},{9,10},{10,1... | collective-permute-start | bytes 776 | tf_op jit(solution)/shard_map/ppermute | solution.py:11
  149.4 26.3 %collective-permute-start.13 = (f32[16,1,128]{2,1,0:T(1,128)S(1)}, f32[16,1,128]{2,1,0:T(1,128)S(1)}, u32[]{:S(2)}, u32[]{:S(2)}) collective-permute-start(f32[16,1,128]{2,1,0:T(1,128)S(1)} %get-tuple-element.17), channel_id=1, source_target_pairs={{64,0},{128,64},{192,128},{256,192},{320,256},{384,320},{448,384},... | collective-permute-start | bytes 24584 | tf_op jit(solution)/shard_map/ppermute | solution.py:12
  151.3 24.4 %collective-permute-start.14 = (f32[16,1,128]{2,1,0:T(1,128)S(1)}, f32[16,1,128]{2,1,0:T(1,128)S(1)}, u32[]{:S(2)}, u32[]{:S(2)}) collective-permute-start(f32[16,1,128]{2,1,0:T(1,128)S(1)} %get-tuple-element.16), channel_id=1, source_target_pairs={{0,64},{64,128},{128,192},{192,256},{256,320},{320,384},{384,448},... | collective-permute-start | bytes 24584 | tf_op jit(solution)/shard_map/ppermute | solution.py:11
  156.1 19.6 %collective-permute-start.15 = (f32[16,4,1]{2,1,0:T(4,128)S(1)}, f32[16,4,1]{2,1,0:T(4,128)S(1)}, u32[]{:S(2)}, u32[]{:S(2)}) collective-permute-start(f32[16,4,1]{2,1,0:T(4,128)S(1)} %get-tuple-element.14), channel_id=1, source_target_pairs={{1,0},{2,1},{3,2},{4,3},{5,4},{6,5},{7,6},{8,7},{9,8},{10,9},{11,1... | collective-permute-start | bytes 776 | tf_op jit(solution)/shard_map/ppermute | solution.py:12

commit v2 on v1

--- a/solution.py
+++ b/solution.py
@@ -4,31 +4,25 @@
 from jax.sharding import PartitionSpec as P
 
 
-def halo_pair(cells, axis, dim):
-    count = lax.axis_size(axis)
-    head = lax.slice_in_dim(cells, 0, 1, axis=dim)
-    tail = lax.slice_in_dim(cells, cells.shape[dim] - 1, cells.shape[dim], axis=dim)
-    low = lax.ppermute(tail, axis, [(i, i + 1) for i in range(count - 1)])
-    high = lax.ppermute(head, axis, [(i + 1, i) for i in range(count - 1)])
-    return low, high
+def send(parts, axis, pairs):
+    flat = jnp.concatenate([p.reshape(-1) for p in parts])
+    got = lax.ppermute(flat, axis, pairs)
+    out, at = [], 0
+    for p in parts:
+        out.append(got[at : at + p.size].reshape(p.shape))
+        at += p.size
+    return out
 
 
-def pad_others(part, lead, done):
-    widths = [(0, 0)] * part.ndim
-    for dim in done:
-        widths[dim] = (1, 1)
-    return jnp.pad(part, widths) if done else part
+def steps(count):
+    return [(i, i + 1) for i in range(count - 1)], [(i + 1, i) for i in range(count - 1)]
 
 
-def with_faces(cells, sides):
-    parts = [halo_pair(cells, axis, dim) for axis, dim in sides]
-    done = []
-    for (axis, dim), (low, high) in zip(sides, parts):
-        cells = jnp.concatenate(
-            [pad_others(low, 0, done), cells, pad_others(high, 0, done)], axis=dim
-        )
-        done.append(dim)
-    return cells
+def pad_dims(part, dims):
+    widths = [(0, 0)] * part.ndim
+    for dim in dims:
+        widths[dim] = (1, 1)
+    return jnp.pad(part, widths)
 
 
 def stencil(padded, viscous):
@@ -65,10 +59,6 @@
     )
 
 
-def map_border(field):
-    return with_faces(field, (("mapx", 1), (("mapy", "layer"), 2)))
-
-
 def from_bottom(x, axis):
     count = lax.axis_size(axis)
     mine = lax.axis_index(axis) == 0
@@ -87,22 +77,83 @@
     return jnp.where(keep, keys * capacity + slot_index, group_count * capacity)
 
 
+def corner_pairs(rows, cols, step_row, step_col):
+    pairs = []
+    for a in range(rows):
+        for j in range(cols):
+            if 0 <= a - step_row < rows and 0 <= j - step_col < cols:
+                pairs.append(((a - step_row) * cols + (j - step_col), a * cols + j))
+    return pairs
+
+
 def shards(velocity, viscosity, friction, owner, cell, directions, stiffness):
     probes = velocity.shape[0]
     depth, rows, cols = viscosity.shape
+    column = ("mapy", "layer")
+    every = ("mapx", "mapy", "layer")
+    count_x = lax.axis_size("mapx")
+    count_col = lax.axis_size(column)
+    count_layer = lax.axis_size("layer")
+    my_layer = lax.axis_index("layer")
     stacked = jnp.concatenate([velocity.reshape(probes * 2, depth, rows, cols), viscosity[None]], 0)
-    extended = with_faces(stacked, (("layer", 1), ("mapx", 2), ("mapy", 3)))
+    fwd_x, bwd_x = steps(count_x)
+    fwd_c, bwd_c = steps(count_col)
+    fwd_y, bwd_y = steps(lax.axis_size("mapy"))
+    d, k = directions, stiffness
+    x_lo = send([stacked[:, :, -1:], d[:, -2:], k[-1:]], "mapx", fwd_x)
+    x_hi = send([stacked[:, :, :1], d[:, :2], k[:1]], "mapx", bwd_x)
+    c_lo = send([stacked[:, -1:], d[:, :, -2:], k[:, -1:]], column, fwd_c)
+    c_hi = send([stacked[:, :1], d[:, :, :2], k[:, :1]], column, bwd_c)
+    (y_lo,) = send([stacked[..., -1:]], "mapy", fwd_y)
+    (y_hi,) = send([stacked[..., :1]], "mapy", bwd_y)
+    corner = {}
+    for sr, sc, src in ((1, 1, d[:, -1, -1]), (1, -1, d[:, -1, 0]), (-1, 1, d[:, 0, -1]), (-1, -1, d[:, 0, 0])):
+        corner[sr, sc] = lax.ppermute(src, every, corner_pairs(count_x, count_col, sr, sc))[:, None, None]
+
+    z_lo = jnp.where(my_layer > 0, c_lo[0], jnp.zeros_like(c_lo[0]))
+    z_hi = jnp.where(my_layer < count_layer - 1, c_hi[0], jnp.zeros_like(c_hi[0]))
+    extended = jnp.concatenate([z_lo, stacked, z_hi], axis=1)
+    extended = jnp.concatenate([pad_dims(x_lo[0], (1,)), extended, pad_dims(x_hi[0], (1,))], axis=2)
+    extended = jnp.concatenate([pad_dims(y_lo, (1, 2)), extended, pad_dims(y_hi, (1, 2))], axis=3)
     padded = extended[:-1].reshape(probes, 2, depth + 2, rows + 2, cols + 2)
     image = stencil(padded, extended[-1])
+
+    zero2 = jnp.zeros((probes, 1, 2), jnp.float32)
+    zero1 = jnp.zeros((probes, 1, 1), jnp.float32)
+    top = jnp.concatenate(
+        [
+            jnp.concatenate([zero2, x_lo[1][:, :1], zero2], axis=2),
+            jnp.concatenate([zero1, corner[1, 1], x_lo[1][:, 1:], corner[1, -1], zero1], axis=2),
+        ],
+        axis=1,
+    )
+    bottom = jnp.concatenate(
+        [
+            jnp.concatenate([zero1, corner[-1, 1], x_hi[1][:, :1], corner[-1, -1], zero1], axis=2),
+            jnp.concatenate([zero2, x_hi[1][:, 1:], zero2], axis=2),
+        ],
+        axis=1,
+    )
+    middle = jnp.concatenate([c_lo[1], d, c_hi[1]], axis=2)
+    wide = jnp.concatenate([top, middle, bottom], axis=1)
+    ring = jnp.concatenate(
+        [
+            pad_dims(x_lo[2], (1,)),
+            jnp.concatenate([c_lo[2], k, c_hi[2]], axis=1),
+            pad_dims(x_hi[2], (1,)),
+        ],
+        axis=0,
+    )
+    inner = ring[None] * laplace(wide)
+    prior = laplace(inner)
+
     face_count = rows * cols
     face_rows = (friction * (image[:, 0, 0] + image[:, 1, 0])).reshape(probes, face_count).T
     targets = owner.reshape(face_count)
     local_cells = cell.reshape(face_count).astype(jnp.float32)
     count_y = lax.axis_size("mapy")
-    count_layer = lax.axis_size("layer")
     owner_count = count_y * count_layer
     capacity = 2 * face_count // owner_count
-    my_layer = lax.axis_index("layer")
     spread = from_bottom(face_rows, "layer")
     keep = targets % count_layer == my_layer
     position = slot_places(targets // count_layer, count_y, capacity, keep)
@@ -126,8 +177,6 @@
         num_segments=map_rows * map_cols,
     )
     data = summed.T.reshape(probes, map_rows, map_cols)
-    inner = stiffness[None] * laplace(map_border(directions))
-    prior = laplace(map_border(inner))
     hessian = data + prior + 0.1 * directions
     return (image, hessian)
 

time: 177 us -> 189 us (1.068)
  the two profiles are of different devices: /device:TPU:191 before, /device:TPU:56 now
where the time goes in v2:
time: 189 us; the launch traced here: 188 us
  starting transfers between devices  126 us (67%)
  waiting for transfers between devices  32 us (17%)
  local copies, waits for them, and re-layouts  14.9 us (8%)
  other arithmetic  13.6 us (7%)
    all_to_all x1, starting transfers between devices, shards(): lax.all_to_all(packed.reshape(count_y, capacity, probes + 1), 'mapy', spl...  91.9 us
    all_to_all x1, waiting for transfers between devices, shards(): lax.all_to_all(packed.reshape(count_y, capacity, probes + 1), 'mapy', spl...  23.9 us
    ppermute x6, starting transfers between devices, send(): got = lax.ppermute(flat, axis, pairs)  17 us
    ppermute x4, starting transfers between devices, shards(): lax.ppermute(src, every, corner_pairs(count_x, count_col, sr, sc))  15 us
    ppermute x3, waiting for transfers between devices, from_bottom(): total = total + lax.ppermute(x, axis, [(0, to)])  6.51 us
    another operation x3, other arithmetic  4.64 us
  transfers between devices with their start and end apart: 14, of which 4 were waited for; matrix products, arithmetic and copies ran while one was open for 8% of the time, Pallas kernels for 0%

profile of v2, /device:TPU:56, one launch (start us, length us, event | category | flops | bytes accessed | tf_op | source)
XLA Modules:
  0.0 188.4 jit_solution(732448839741195569)
XLA Ops:
  0.7 1.4 slice_reduce_fusion.2
  2.0 2.1 %collective-permute-start.10 = (f32[16]{0:T(128)S(1)}, f32[16]{0:T(128)S(1)}, u32[]{:S(2)}, u32[]{:S(2)}) collective-permute-start(f32[16]{0:T(128)S(1)} %get-tuple-element.2), channel_id=1, source_target_pairs={{1,64},{2,65},{3,66},{4,67},{5,68},{6,69},{7,70},{8,71},{9,72},{10... | collective-permute-start | bytes 200 | tf_op jit(solution)/shard_map/ppermute | solution.py:111
  4.1 6.5 %collective-permute-start.11 = (f32[16]{0:T(128)S(1)}, f32[16]{0:T(128)S(1)}, u32[]{:S(2)}, u32[]{:S(2)}) collective-permute-start(f32[16]{0:T(128)S(1)} %get-tuple-element.3), channel_id=1, source_target_pairs={{64,1},{65,2},{66,3},{67,4},{68,5},{69,6},{70,7},{71,8},{72,9},{73... | collective-permute-start | bytes 200 | tf_op jit(solution)/shard_map/ppermute | solution.py:111
  10.6 0.9 fusion.51
  11.5 0.8 slice_bitcast_fusion.6
  12.2 1.0 copy.140
  13.2 0.8 fusion.40
  14.1 1.9 %collective-permute-start.4 = (f32[12672]{0:T(1024)S(1)}, f32[12672]{0:T(1024)S(1)}, u32[]{:S(2)}, u32[]{:S(2)}) collective-permute-start(f32[12672]{0:T(1024)S(1)} %pad_maximum_fusion.16), channel_id=1, source_target_pairs={{64,0},{128,64},{192,128},{256,192},{320,256},{384,320},{448,384},... | collective-permute-start | bytes 152072 | tf_op jit(solution)/shard_map/ppermute | solution.py:9
  16.1 0.9 fusion.5
  17.5 3.4 %collective-permute-start = (f32[528]{0:T(1024)S(1)}, f32[528]{0:T(1024)S(1)}, u32[]{:S(2)}, u32[]{:S(2)}) collective-permute-start(f32[528]{0:T(1024)S(1)} %reshape.335), channel_id=1, source_target_pairs={{0,4},{4,8},{8,12},{12,16},{16,20},{20,24},{24,28},{28,32},{32,36}... | collective-permute-start | bytes 6344 | tf_op jit(solution)/shard_map/ppermute | solution.py:9
  21.5 1.3 collective-permute-start.5
  23.2 4.5 %reduce-window.6 = s32[16,8,128]{2,1,0:T(8,128)S(1)} reduce-window(s32[16,8,128]{2,1,0:T(8,128)S(1)} %fusion.38, s32[]{:T(128)} %constant.28.clone.1), window={size=1x1x128 pad=0_0x0_0x127_0}, to_apply=%region_0.1 | reduce-window | flops 2080768 | bytes 131076 | tf_op jit(solution)/shard_map/reduce-window
  28.7 3.0 %collective-permute-start.9 = (f32[16]{0:T(128)S(1)}, f32[16]{0:T(128)S(1)}, u32[]{:S(2)}, u32[]{:S(2)}) collective-permute-start(f32[16]{0:T(128)S(1)} %get-tuple-element.4), channel_id=1, source_target_pairs={{0,65},{1,66},{2,67},{3,68},{4,69},{5,70},{6,71},{7,72},{8,73},{9,... | collective-permute-start | bytes 200 | tf_op jit(solution)/shard_map/ppermute | solution.py:111
  31.8 3.5 %collective-permute-start.12 = (f32[16]{0:T(128)S(1)}, f32[16]{0:T(128)S(1)}, u32[]{:S(2)}, u32[]{:S(2)}) collective-permute-start(f32[16]{0:T(128)S(1)} %get-tuple-element.5), channel_id=1, source_target_pairs={{65,0},{66,1},{67,2},{68,3},{69,4},{70,5},{71,6},{72,7},{73,8},{74... | collective-permute-start | bytes 200 | tf_op jit(solution)/shard_map/ppermute | solution.py:111
  35.4 2.4 %collective-permute-start.1 = (f32[12672]{0:T(1024)S(1)}, f32[12672]{0:T(1024)S(1)}, u32[]{:S(2)}, u32[]{:S(2)}) collective-permute-start(f32[12672]{0:T(1024)S(1)} %pad_maximum_fusion.15), channel_id=1, source_target_pairs={{0,64},{64,128},{128,192},{192,256},{256,320},{320,384},{384,448},... | collective-permute-start | bytes 152072 | tf_op jit(solution)/shard_map/ppermute | solution.py:9
  37.9 0.9 collective-permute-done.12
  38.8 1.9 %collective-permute-start.3 = (f32[33924]{0:T(1024)S(1)}, f32[33924]{0:T(1024)S(1)}, u32[]{:S(2)}, u32[]{:S(2)}) collective-permute-start(f32[33924]{0:T(1024)S(1)} %pad_maximum_fusion.2), channel_id=1, source_target_pairs={{1,0},{2,1},{3,2},{4,3},{5,4},{6,5},{7,6},{8,7},{9,8},{10,9},{11,1... | collective-permute-start | bytes 407096 | tf_op jit(solution)/shard_map/ppermute | solution.py:9
  40.8 6.0 %collective-permute-start.2 = (f32[33924]{0:T(1024)S(1)}, f32[33924]{0:T(1024)S(1)}, u32[]{:S(2)}, u32[]{:S(2)}) collective-permute-start(f32[33924]{0:T(1024)S(1)} %pad_maximum_fusion.1), channel_id=1, source_target_pairs={{0,1},{1,2},{2,3},{3,4},{4,5},{5,6},{6,7},{7,8},{8,9},{9,10},{10,1... | collective-permute-start | bytes 407096 | tf_op jit(solution)/shard_map/ppermute | solution.py:9
  48.6 0.8 collective-permute-done.2
  49.4 1.1 select_maximum_fusion
  52.0 0.7 collective-permute-start.7
  52.6 0.7 collective-permute-start.6
  53.3 1.3 collective-permute-start.8
  55.3 6.5 %collective-permute-done.8 = f32[1024,16]{0,1:T(8,128)S(1)} collective-permute-done((f32[1024,16]{0,1:T(8,128)S(1)}, f32[1024,16]{0,1:T(8,128)S(1)}, u32[]{:S(2)}, u32[]{:S(2)}) %collective-permute-start.8) | collective-permute-done | bytes 65568 | tf_op jit(solution)/shard_map/ppermute | solution.py:67
  62.1 3.1 %scatter_custom_fusion = f32[513,17]{1,0:T(8,128)S(1)} fusion(s32[1024]{0:T(1024)S(1)} %bitcast.135, f32[1024,17]{1,0:T(8,128)S(1)} %copy.158, f32[]{:T(128)} %constant.23.clone.1), kind=kCustom, calls=%fused_computation.54 | custom fusion | bytes 34888 | tf_op jit(solution)/shard_map/scatter | solution.py:163
  65.4 0.7 reshape.395
  66.2 91.9 %all-to-all-start = ((f32[16,1,544]{2,1,0:T(1,128)}), f32[16,1,544]{2,1,0:T(1,128)S(1)}, u32[]{:S(2)}, u32[]{:S(2)}) async-start(f32[16,1,544]{2,1,0:T(1,128)} %reshape.395), calls=%async_computation | async-start | bytes 81920 | tf_op jit(solution)/shard_map/all_to_all | solution.py:165
  158.6 23.9 %all-to-all-done = f32[16,1,544]{2,1,0:T(1,128)S(1)} async-done(((f32[16,1,544]{2,1,0:T(1,128)}), f32[16,1,544]{2,1,0:T(1,128)S(1)}, u32[]{:S(2)}, u32[]{:S(2)}) %all-to-all-start) | async-done | bytes 34848 | tf_op jit(solution)/shard_map/all_to_all | solution.py:165
  182.5 0.5 broadcast.322
  183.0 0.7 reduce.12
  184.1 3.4 %scatter_custom_fusion.1 = f32[512,16]{1,0:T(8,128)S(1)} fusion(s32[512]{0:T(512)S(1)} %bitcast.136, f32[512,16]{1,0:T(8,128)S(1)} %copy.161, f32[]{:T(128)} %constant.23.clone.1), kind=kCustom, calls=%fused_computation.75 | custom fusion | flops 8192 | bytes 32772 | tf_op jit(solution)/shard_map/scatter-add | solution.py:174
  187.6 0.8 fusion.42
  (116 shorter events, 8.0 us)
Async XLA Ops:
  0.6 22.5 %copy-start = (f32[16,4,128]{2,1,0:T(4,128)S(1)}, f32[16,4,128]{2,1,0:T(4,128)}, u32[]{:S(2)}) copy-start(f32[16,4,128]{2,1,0:T(4,128)} %param.14) | copy-start | bytes 98308
  0.6 22.2 %copy-start.4 = (f32[4,128]{1,0:T(4,128)S(1)}, f32[4,128]{1,0:T(4,128)}, u32[]{:S(2)}) copy-start(f32[4,128]{1,0:T(4,128)} %param.15) | copy-start | bytes 6148
  0.7 22.5 %copy-start.2 = (f32[2,8,128]{2,1,0:T(8,128)S(1)}, f32[2,8,128]{2,1,0:T(8,128)}, u32[]{:S(2)}) copy-start(f32[2,8,128]{2,1,0:T(8,128)} %param.10) | copy-start | bytes 24580
  0.7 22.4 %copy-start.3 = (s32[1,1,1024,1]{2,3,1,0:T(1,128)S(1)}, s32[1,1,1024,1]{2,3,1,0:T(1,128)}, u32[]{:S(2)}) copy-start(s32[1,1,1024,1]{2,3,1,0:T(1,128)} %param.12) | copy-start | bytes 12292
  2.0 26.7 %collective-permute-start.10 = (f32[16]{0:T(128)S(1)}, f32[16]{0:T(128)S(1)}, u32[]{:S(2)}, u32[]{:S(2)}) collective-permute-start(f32[16]{0:T(128)S(1)} %get-tuple-element.2), channel_id=1, source_target_pairs={{1,64},{2,65},{3,66},{4,67},{5,68},{6,69},{7,70},{8,71},{9,72},{10... | collective-permute-start | bytes 200 | tf_op jit(solution)/shard_map/ppermute | solution.py:111
  4.1 27.6 %collective-permute-start.11 = (f32[16]{0:T(128)S(1)}, f32[16]{0:T(128)S(1)}, u32[]{:S(2)}, u32[]{:S(2)}) collective-permute-start(f32[16]{0:T(128)S(1)} %get-tuple-element.3), channel_id=1, source_target_pairs={{64,1},{65,2},{66,3},{67,4},{68,5},{69,6},{70,7},{71,8},{72,9},{73... | collective-permute-start | bytes 200 | tf_op jit(solution)/shard_map/ppermute | solution.py:111
  13.2 15.5 %copy-start.6 = (s32[1,1,1024]{2,1,0:T(1,128)S(1)}, s32[1,1,1024]{2,1,0:T(1,128)}, u32[]{:S(2)}) copy-start(s32[1,1,1024]{2,1,0:T(1,128)} %param.13) | copy-start | bytes 12292
  14.1 33.8 %collective-permute-start.4 = (f32[12672]{0:T(1024)S(1)}, f32[12672]{0:T(1024)S(1)}, u32[]{:S(2)}, u32[]{:S(2)}) collective-permute-start(f32[12672]{0:T(1024)S(1)} %pad_maximum_fusion.16), channel_id=1, source_target_pairs={{64,0},{128,64},{192,128},{256,192},{320,256},{384,320},{448,384},... | collective-permute-start | bytes 152072 | tf_op jit(solution)/shard_map/ppermute | solution.py:9
  17.5 29.8 %collective-permute-start = (f32[528]{0:T(1024)S(1)}, f32[528]{0:T(1024)S(1)}, u32[]{:S(2)}, u32[]{:S(2)}) collective-permute-start(f32[528]{0:T(1024)S(1)} %reshape.335), channel_id=1, source_target_pairs={{0,4},{4,8},{8,12},{12,16},{16,20},{20,24},{24,28},{28,32},{32,36}... | collective-permute-start | bytes 6344 | tf_op jit(solution)/shard_map/ppermute | solution.py:9
  21.5 19.2 %collective-permute-start.5 = (f32[528]{0:T(1024)S(1)}, f32[528]{0:T(1024)S(1)}, u32[]{:S(2)}, u32[]{:S(2)}) collective-permute-start(f32[528]{0:T(1024)S(1)} %reshape.351), channel_id=1, source_target_pairs={{4,0},{8,4},{12,8},{16,12},{20,16},{24,20},{28,24},{32,28},{36,32}... | collective-permute-start | bytes 6344 | tf_op jit(solution)/shard_map/ppermute | solution.py:9
  28.7 6.6 %collective-permute-start.9 = (f32[16]{0:T(128)S(1)}, f32[16]{0:T(128)S(1)}, u32[]{:S(2)}, u32[]{:S(2)}) collective-permute-start(f32[16]{0:T(128)S(1)} %get-tuple-element.4), channel_id=1, source_target_pairs={{0,65},{1,66},{2,67},{3,68},{4,69},{5,70},{6,71},{7,72},{8,73},{9,... | collective-permute-start | bytes 200 | tf_op jit(solution)/shard_map/ppermute | solution.py:111
  31.8 7.0 %collective-permute-start.12 = (f32[16]{0:T(128)S(1)}, f32[16]{0:T(128)S(1)}, u32[]{:S(2)}, u32[]{:S(2)}) collective-permute-start(f32[16]{0:T(128)S(1)} %get-tuple-element.5), channel_id=1, source_target_pairs={{65,0},{66,1},{67,2},{68,3},{69,4},{70,5},{71,6},{72,7},{73,8},{74... | collective-permute-start | bytes 200 | tf_op jit(solution)/shard_map/ppermute | solution.py:111
  35.4 12.7 %collective-permute-start.1 = (f32[12672]{0:T(1024)S(1)}, f32[12672]{0:T(1024)S(1)}, u32[]{:S(2)}, u32[]{:S(2)}) collective-permute-start(f32[12672]{0:T(1024)S(1)} %pad_maximum_fusion.15), channel_id=1, source_target_pairs={{0,64},{64,128},{128,192},{192,256},{256,320},{320,384},{384,448},... | collective-permute-start | bytes 152072 | tf_op jit(solution)/shard_map/ppermute | solution.py:9
  38.8 9.8 %collective-permute-start.3 = (f32[33924]{0:T(1024)S(1)}, f32[33924]{0:T(1024)S(1)}, u32[]{:S(2)}, u32[]{:S(2)}) collective-permute-start(f32[33924]{0:T(1024)S(1)} %pad_maximum_fusion.2), channel_id=1, source_target_pairs={{1,0},{2,1},{3,2},{4,3},{5,4},{6,5},{7,6},{8,7},{9,8},{10,9},{11,1... | collective-permute-start | bytes 407096 | tf_op jit(solution)/shard_map/ppermute | solution.py:9
  40.8 8.6 %collective-permute-start.2 = (f32[33924]{0:T(1024)S(1)}, f32[33924]{0:T(1024)S(1)}, u32[]{:S(2)}, u32[]{:S(2)}) collective-permute-start(f32[33924]{0:T(1024)S(1)} %pad_maximum_fusion.1), channel_id=1, source_target_pairs={{0,1},{1,2},{2,3},{3,4},{4,5},{5,6},{6,7},{7,8},{8,9},{9,10},{10,1... | collective-permute-start | bytes 407096 | tf_op jit(solution)/shard_map/ppermute | solution.py:9
  50.7 0.7 copy-start.7
  50.7 0.7 copy-start.8
  51.3 0.7 copy-start.5
  51.6 132.3 %copy-start.1 = (f32[16,2,2,8,128]{4,3,2,1,0:T(8,128)}, f32[16,2,2,8,128]{4,3,2,1,0:T(8,128)S(1)}, u32[]{:S(2)}) copy-start(f32[16,2,2,8,128]{4,3,2,1,0:T(8,128)S(1)} %fusion.7) | copy-start | bytes 786436
  52.0 3.3 %collective-permute-start.7 = (f32[1024,16]{0,1:T(8,128)S(1)}, f32[1024,16]{0,1:T(8,128)S(1)}, u32[]{:S(2)}, u32[]{:S(2)}) collective-permute-start(f32[1024,16]{0,1:T(8,128)S(1)} %fusion.32), channel_id=1, source_target_pairs={{0,2},{4,6},{8,10},{12,14},{16,18},{20,22},{24,26},{28,30},{32,34}... | collective-permute-start | bytes 196616 | tf_op jit(solution)/shard_map/ppermute | solution.py:67
  52.6 2.7 %collective-permute-start.6 = (f32[1024,16]{0,1:T(8,128)S(1)}, f32[1024,16]{0,1:T(8,128)S(1)}, u32[]{:S(2)}, u32[]{:S(2)}) collective-permute-start(f32[1024,16]{0,1:T(8,128)S(1)} %fusion.32), channel_id=1, source_target_pairs={{0,1},{4,5},{8,9},{12,13},{16,17},{20,21},{24,25},{28,29},{32,33},... | collective-permute-start | bytes 196616 | tf_op jit(solution)/shard_map/ppermute | solution.py:67
  53.3 8.5 %collective-permute-start.8 = (f32[1024,16]{0,1:T(8,128)S(1)}, f32[1024,16]{0,1:T(8,128)S(1)}, u32[]{:S(2)}, u32[]{:S(2)}) collective-permute-start(f32[1024,16]{0,1:T(8,128)S(1)} %fusion.32), channel_id=1, source_target_pairs={{0,3},{4,7},{8,11},{12,15},{16,19},{20,23},{24,27},{28,31},{32,35}... | collective-permute-start | bytes 196616 | tf_op jit(solution)/shard_map/ppermute | solution.py:67
  66.2 116.3 %all-to-all-start = ((f32[16,1,544]{2,1,0:T(1,128)}), f32[16,1,544]{2,1,0:T(1,128)S(1)}, u32[]{:S(2)}, u32[]{:S(2)}) async-start(f32[16,1,544]{2,1,0:T(1,128)} %reshape.395), calls=%async_computation | async-start | bytes 81920 | tf_op jit(solution)/shard_map/all_to_all | solution.py:165

commit v3 on v1

--- a/solution.py
+++ b/solution.py
@@ -126,6 +126,7 @@
         num_segments=map_rows * map_cols,
     )
     data = summed.T.reshape(probes, map_rows, map_cols)
+    directions, stiffness, got = lax.optimization_barrier((directions, stiffness, got))
     inner = stiffness[None] * laplace(map_border(directions))
     prior = laplace(map_border(inner))
     hessian = data + prior + 0.1 * directions

time: 177 us -> 197 us (1.11)
  blocking collectives: 0 us -> 62.8 us
  starting transfers between devices: 108 us -> 57.6 us
  waiting for transfers between devices: 42 us -> 51.2 us
  local copies, waits for them, and re-layouts: 7.95 us -> 5.68 us
    all_to_all x0 -> x1, blocking collectives: none -> 62.8 us  [shards(): lax.all_to_all(packed.reshape(count_y, capacity, probes + 1), 'mapy', spl...]
    all_to_all x1 -> x0, starting transfers between devices: 30.9 us -> none  [shards(): lax.all_to_all(packed.reshape(count_y, capacity, probes + 1), 'mapy', spl...]
    ppermute x7, starting transfers between devices: 57.8 us -> 35.5 us  [halo_pair(): low = lax.ppermute(tail, axis, [(i, i + 1) for i in range(count - 1)])]
    ppermute x7, waiting for transfers between devices: 27.2 us -> 35.4 us  [halo_pair(): high = lax.ppermute(head, axis, [(i + 1, i) for i in range(count - 1)])]
    ppermute x3, waiting for transfers between devices: 0.01 us -> 3.55 us  [from_bottom(): total = total + lax.ppermute(x, axis, [(0, to)])]
    ppermute x7, starting transfers between devices: 16.3 us -> 19.4 us  [halo_pair(): high = lax.ppermute(head, axis, [(i + 1, i) for i in range(count - 1)])]
    all_to_all x1 -> x0, waiting for transfers between devices: 2.55 us -> none  [shards(): lax.all_to_all(packed.reshape(count_y, capacity, probes + 1), 'mapy', spl...]
  transfers between devices with their start and end apart: 18 -> 17, of which waited for: 5 -> 5; matrix products, arithmetic and copies ran while one was open for 11% -> 7% of each run, Pallas kernels for 0% -> 0%
where the time goes in v3:
time: 197 us; the launch traced here: 196 us
  blocking collectives  62.8 us (32%)
  starting transfers between devices  57.6 us (29%)
  waiting for transfers between devices  51.2 us (26%)
  other arithmetic  17.4 us (9%)
  local copies, waits for them, and re-layouts  5.68 us (3%)
    all_to_all x1, blocking collectives, shards(): lax.all_to_all(packed.reshape(count_y, capacity, probes + 1), 'mapy', spl...  62.8 us
    ppermute x7, starting transfers between devices, halo_pair(): low = lax.ppermute(tail, axis, [(i, i + 1) for i in range(count - 1)])  35.5 us
    ppermute x7, waiting for transfers between devices, halo_pair(): high = lax.ppermute(head, axis, [(i + 1, i) for i in range(count - 1)])  35.4 us
    ppermute x7, starting transfers between devices, halo_pair(): high = lax.ppermute(head, axis, [(i + 1, i) for i in range(count - 1)])  19.4 us
    ppermute x7, waiting for transfers between devices, halo_pair(): low = lax.ppermute(tail, axis, [(i, i + 1) for i in range(count - 1)])  12.2 us
    another operation x3, other arithmetic  4.64 us
  transfers between devices with their start and end apart: 17, of which 5 were waited for; matrix products, arithmetic and copies ran while one was open for 7% of the time, Pallas kernels for 0%

profile of v3, /device:TPU:191, one launch (start us, length us, event | category | flops | bytes accessed | tf_op | source)
XLA Modules:
  0.0 195.9 jit_solution(16778547118585255798)
XLA Ops:
  0.7 1.2 fusion.5
  1.9 2.5 %collective-permute-start.5 = (f32[33,2,8,1]{3,2,1,0:T(8,128)S(1)}, f32[33,2,8,1]{3,2,1,0:T(8,128)S(1)}, u32[]{:S(2)}, u32[]{:S(2)}) collective-permute-start(f32[33,2,8,1]{3,2,1,0:T(8,128)S(1)} %get-tuple-element.9), channel_id=1, source_target_pairs={{4,0},{8,4},{12,8},{16,12},{20,16},{24,20},{28,24},{32,28},{36,32}... | collective-permute-start | bytes 6344 | tf_op jit(solution)/shard_map/ppermute | solution.py:12
  4.4 1.1 fusion.31
  5.5 2.9 %collective-permute-start.4 = (f32[33,2,1,128]{3,2,1,0:T(1,128)S(1)}, f32[33,2,1,128]{3,2,1,0:T(1,128)S(1)}, u32[]{:S(2)}, u32[]{:S(2)}) collective-permute-start(f32[33,2,1,128]{3,2,1,0:T(1,128)S(1)} %get-tuple-element.11), channel_id=1, source_target_pairs={{64,0},{128,64},{192,128},{256,192},{320,256},{384,320},{448,384},... | collective-permute-start | bytes 101384 | tf_op jit(solution)/shard_map/ppermute | solution.py:12
  8.3 3.4 %collective-permute-start.1 = (f32[33,2,1,128]{3,2,1,0:T(1,128)S(1)}, f32[33,2,1,128]{3,2,1,0:T(1,128)S(1)}, u32[]{:S(2)}, u32[]{:S(2)}) collective-permute-start(f32[33,2,1,128]{3,2,1,0:T(1,128)S(1)} %get-tuple-element.10), channel_id=1, source_target_pairs={{0,64},{64,128},{128,192},{192,256},{256,320},{320,384},{384,448},... | collective-permute-start | bytes 101384 | tf_op jit(solution)/shard_map/ppermute | solution.py:11
  11.8 14.5 %collective-permute-start = (f32[33,2,8,1]{3,2,1,0:T(8,128)S(1)}, f32[33,2,8,1]{3,2,1,0:T(8,128)S(1)}, u32[]{:S(2)}, u32[]{:S(2)}) collective-permute-start(f32[33,2,8,1]{3,2,1,0:T(8,128)S(1)} %get-tuple-element.8), channel_id=1, source_target_pairs={{0,4},{4,8},{8,12},{12,16},{16,20},{20,24},{24,28},{28,32},{32,36}... | collective-permute-start | bytes 6344 | tf_op jit(solution)/shard_map/ppermute | solution.py:11
  26.3 1.0 fusion.17
  27.3 2.4 %collective-permute-start.3 = (f32[33,1,8,128]{3,2,1,0:T(8,128)S(1)}, f32[33,1,8,128]{3,2,1,0:T(8,128)S(1)}, u32[]{:S(2)}, u32[]{:S(2)}) collective-permute-start(f32[33,1,8,128]{3,2,1,0:T(8,128)S(1)} %get-tuple-element.7), channel_id=1, source_target_pairs={{1,0},{2,1},{3,2},{5,4},{6,5},{7,6},{9,8},{10,9},{11,10},{13,12},{... | collective-permute-start | bytes 405512 | tf_op jit(solution)/shard_map/ppermute | solution.py:12
  30.4 0.7 fusion.48
  31.8 0.7 fusion.47
  32.5 4.5 %reduce-window.6 = s32[16,8,128]{2,1,0:T(8,128)S(1)} reduce-window(s32[16,8,128]{2,1,0:T(8,128)S(1)} %fusion.29, s32[]{:T(128)} %constant.47.clone.1), window={size=1x1x128 pad=0_0x0_0x127_0}, to_apply=%region_0.1 | reduce-window | flops 2080768 | bytes 131076 | tf_op jit(solution)/shard_map/reduce-window
  37.5 7.9 %collective-permute-done.5 = f32[33,2,8,1]{3,2,1,0:T(8,128)S(1)} collective-permute-done((f32[33,2,8,1]{3,2,1,0:T(8,128)S(1)}, f32[33,2,8,1]{3,2,1,0:T(8,128)S(1)}, u32[]{:S(2)}, u32[]{:S(2)}) %collective-permute-start.5) | collective-permute-done | bytes 2144 | tf_op jit(solution)/shard_map/ppermute | solution.py:12
  45.4 1.3 collective-permute-start.2
  46.7 12.2 %collective-permute-done = f32[33,2,8,1]{3,2,1,0:T(8,128)S(1)} collective-permute-done((f32[33,2,8,1]{3,2,1,0:T(8,128)S(1)}, f32[33,2,8,1]{3,2,1,0:T(8,128)S(1)}, u32[]{:S(2)}, u32[]{:S(2)}) %collective-permute-start) | collective-permute-done | bytes 2144 | tf_op jit(solution)/shard_map/ppermute | solution.py:11
  59.0 1.1 select_maximum_fusion
  61.4 1.4 collective-permute-start.8
  64.2 3.5 %collective-permute-done.8 = f32[1024,16]{0,1:T(8,128)S(1)} collective-permute-done((f32[1024,16]{0,1:T(8,128)S(1)}, f32[1024,16]{0,1:T(8,128)S(1)}, u32[]{:S(2)}, u32[]{:S(2)}) %collective-permute-start.8) | collective-permute-done | bytes 65568 | tf_op jit(solution)/shard_map/ppermute | solution.py:77
  68.0 3.1 %scatter_custom_fusion = f32[513,17]{1,0:T(8,128)S(1)} fusion(s32[1024]{0:T(1024)S(1)} %bitcast.90, f32[1024,17]{1,0:T(8,128)S(1)} %copy.32, f32[]{:T(128)} %constant.45.clone.1), kind=kCustom, calls=%fused_computation.46 | custom fusion | bytes 34888 | tf_op jit(solution)/shard_map/scatter | solution.py:112
  71.5 62.8 %all_to_all.5 = f32[16,1,544]{2,1,0:T(1,128)S(1)} all-to-all(f32[16,1,544]{2,1,0:T(1,128)S(1)} %reshape.253), channel_id=1, replica_groups=mesh['mapx'=16,'mapy'=16,'layer'=4] {'mapy'}, dimensions={0} | all-to-all | bytes 69632 | tf_op jit(solution)/shard_map/all_to_all | solution.py:114
  134.8 0.7 reduce
  135.9 6.2 %collective-permute-start.12 = (f32[16,4,1]{2,1,0:T(4,128)S(1)}, f32[16,4,1]{2,1,0:T(4,128)S(1)}, u32[]{:S(2)}, u32[]{:S(2)}) collective-permute-start(f32[16,4,1]{2,1,0:T(4,128)S(1)} %get-tuple-element.23), channel_id=1, source_target_pairs={{0,1},{1,2},{2,3},{3,4},{4,5},{5,6},{6,7},{7,8},{8,9},{9,10},{10,1... | collective-permute-start | bytes 776 | tf_op jit(solution)/shard_map/ppermute | solution.py:11
  142.1 4.5 %collective-permute-start.9 = (f32[16,1,128]{2,1,0:T(1,128)S(1)}, f32[16,1,128]{2,1,0:T(1,128)S(1)}, u32[]{:S(2)}, u32[]{:S(2)}) collective-permute-start(f32[16,1,128]{2,1,0:T(1,128)S(1)} %get-tuple-element.25), channel_id=1, source_target_pairs={{64,0},{128,64},{192,128},{256,192},{320,256},{384,320},{448,384},... | collective-permute-start | bytes 24584 | tf_op jit(solution)/shard_map/ppermute | solution.py:12
  146.6 4.4 %collective-permute-start.10 = (f32[16,1,128]{2,1,0:T(1,128)S(1)}, f32[16,1,128]{2,1,0:T(1,128)S(1)}, u32[]{:S(2)}, u32[]{:S(2)}) collective-permute-start(f32[16,1,128]{2,1,0:T(1,128)S(1)} %get-tuple-element.24), channel_id=1, source_target_pairs={{0,64},{64,128},{128,192},{192,256},{256,320},{320,384},{384,448},... | collective-permute-start | bytes 24584 | tf_op jit(solution)/shard_map/ppermute | solution.py:11
  151.1 1.9 collective-permute-start.11
  153.2 15.7 %collective-permute-done.11 = f32[16,4,1]{2,1,0:T(4,128)S(1)} collective-permute-done((f32[16,4,1]{2,1,0:T(4,128)S(1)}, f32[16,4,1]{2,1,0:T(4,128)S(1)}, u32[]{:S(2)}, u32[]{:S(2)}) %collective-permute-start.11) | collective-permute-done | bytes 288 | tf_op jit(solution)/shard_map/ppermute | solution.py:12
  169.1 1.9 collective-permute-start.13
  171.0 3.6 %collective-permute-start.14 = (f32[16,1,128]{2,1,0:T(1,128)S(1)}, f32[16,1,128]{2,1,0:T(1,128)S(1)}, u32[]{:S(2)}, u32[]{:S(2)}) collective-permute-start(f32[16,1,128]{2,1,0:T(1,128)S(1)} %get-tuple-element.20), channel_id=1, source_target_pairs={{0,64},{64,128},{128,192},{192,256},{256,320},{320,384},{384,448},... | collective-permute-start | bytes 24584 | tf_op jit(solution)/shard_map/ppermute | solution.py:11
  174.7 1.9 collective-permute-start.16
  176.7 3.4 %collective-permute-start.15 = (f32[16,4,1]{2,1,0:T(4,128)S(1)}, f32[16,4,1]{2,1,0:T(4,128)S(1)}, u32[]{:S(2)}, u32[]{:S(2)}) collective-permute-start(f32[16,4,1]{2,1,0:T(4,128)S(1)} %get-tuple-element.18), channel_id=1, source_target_pairs={{1,0},{2,1},{3,2},{4,3},{5,4},{6,5},{7,6},{8,7},{9,8},{10,9},{11,1... | collective-permute-start | bytes 776 | tf_op jit(solution)/shard_map/ppermute | solution.py:12
  180.0 3.0 %scatter_custom_fusion.1 = f32[512,16]{1,0:T(8,128)S(1)} fusion(s32[512]{0:T(512)S(1)} %bitcast.91, f32[512,16]{1,0:T(8,128)S(1)} %copy.35, f32[]{:T(128)} %constant.45.clone.1), kind=kCustom, calls=%fused_computation.48 | custom fusion | flops 8192 | bytes 32772 | tf_op jit(solution)/shard_map/scatter-add | solution.py:123
  183.2 11.9 %collective-permute-done.15 = f32[16,4,1]{2,1,0:T(4,128)S(1)} collective-permute-done((f32[16,4,1]{2,1,0:T(4,128)S(1)}, f32[16,4,1]{2,1,0:T(4,128)S(1)}, u32[]{:S(2)}, u32[]{:S(2)}) %collective-permute-start.15) | collective-permute-done | bytes 288 | tf_op jit(solution)/shard_map/ppermute | solution.py:12
  195.1 0.8 fusion.35
  (72 shorter events, 6.4 us)
Async XLA Ops:
  0.6 58.3 %copy-start.3 = (f32[2,8,128]{2,1,0:T(8,128)S(1)}, f32[2,8,128]{2,1,0:T(8,128)}, u32[]{:S(2)}) copy-start(f32[2,8,128]{2,1,0:T(8,128)} %param.10) | copy-start | bytes 24580
  0.6 58.3 %copy-start = (f32[16,2,2,8,128]{4,3,2,1,0:T(8,128)S(1)}, f32[16,2,2,8,128]{4,3,2,1,0:T(8,128)}, u32[]{:S(2)}) copy-start(f32[16,2,2,8,128]{4,3,2,1,0:T(8,128)} %param.9) | copy-start | bytes 786436
  0.7 46.0 %copy-start.4 = (s32[1,1,1024,1]{2,3,1,0:T(1,128)S(1)}, s32[1,1,1024,1]{2,3,1,0:T(1,128)}, u32[]{:S(2)}) copy-start(s32[1,1,1024,1]{2,3,1,0:T(1,128)} %param.12) | copy-start | bytes 12292
  1.9 43.5 %collective-permute-start.5 = (f32[33,2,8,1]{3,2,1,0:T(8,128)S(1)}, f32[33,2,8,1]{3,2,1,0:T(8,128)S(1)}, u32[]{:S(2)}, u32[]{:S(2)}) collective-permute-start(f32[33,2,8,1]{3,2,1,0:T(8,128)S(1)} %get-tuple-element.9), channel_id=1, source_target_pairs={{4,0},{8,4},{12,8},{16,12},{20,16},{24,20},{28,24},{32,28},{36,32}... | collective-permute-start | bytes 6344 | tf_op jit(solution)/shard_map/ppermute | solution.py:12
  5.5 53.5 %collective-permute-start.4 = (f32[33,2,1,128]{3,2,1,0:T(1,128)S(1)}, f32[33,2,1,128]{3,2,1,0:T(1,128)S(1)}, u32[]{:S(2)}, u32[]{:S(2)}) collective-permute-start(f32[33,2,1,128]{3,2,1,0:T(1,128)S(1)} %get-tuple-element.11), channel_id=1, source_target_pairs={{64,0},{128,64},{192,128},{256,192},{320,256},{384,320},{448,384},... | collective-permute-start | bytes 101384 | tf_op jit(solution)/shard_map/ppermute | solution.py:12
  8.3 50.6 %collective-permute-start.1 = (f32[33,2,1,128]{3,2,1,0:T(1,128)S(1)}, f32[33,2,1,128]{3,2,1,0:T(1,128)S(1)}, u32[]{:S(2)}, u32[]{:S(2)}) collective-permute-start(f32[33,2,1,128]{3,2,1,0:T(1,128)S(1)} %get-tuple-element.10), channel_id=1, source_target_pairs={{0,64},{64,128},{128,192},{192,256},{256,320},{320,384},{384,448},... | collective-permute-start | bytes 101384 | tf_op jit(solution)/shard_map/ppermute | solution.py:11
  11.8 47.1 %collective-permute-start = (f32[33,2,8,1]{3,2,1,0:T(8,128)S(1)}, f32[33,2,8,1]{3,2,1,0:T(8,128)S(1)}, u32[]{:S(2)}, u32[]{:S(2)}) collective-permute-start(f32[33,2,8,1]{3,2,1,0:T(8,128)S(1)} %get-tuple-element.8), channel_id=1, source_target_pairs={{0,4},{4,8},{8,12},{12,16},{16,20},{20,24},{24,28},{28,32},{32,36}... | collective-permute-start | bytes 6344 | tf_op jit(solution)/shard_map/ppermute | solution.py:11
  27.3 31.6 %collective-permute-start.3 = (f32[33,1,8,128]{3,2,1,0:T(8,128)S(1)}, f32[33,1,8,128]{3,2,1,0:T(8,128)S(1)}, u32[]{:S(2)}, u32[]{:S(2)}) collective-permute-start(f32[33,1,8,128]{3,2,1,0:T(8,128)S(1)} %get-tuple-element.7), channel_id=1, source_target_pairs={{1,0},{2,1},{3,2},{5,4},{6,5},{7,6},{9,8},{10,9},{11,10},{13,12},{... | collective-permute-start | bytes 405512 | tf_op jit(solution)/shard_map/ppermute | solution.py:12
  45.4 13.6 %collective-permute-start.2 = (f32[33,1,8,128]{3,2,1,0:T(8,128)S(1)}, f32[33,1,8,128]{3,2,1,0:T(8,128)S(1)}, u32[]{:S(2)}, u32[]{:S(2)}) collective-permute-start(f32[33,1,8,128]{3,2,1,0:T(8,128)S(1)} %get-tuple-element.6), channel_id=1, source_target_pairs={{0,1},{1,2},{2,3},{4,5},{5,6},{6,7},{8,9},{9,10},{10,11},{12,13},{... | collective-permute-start | bytes 405512 | tf_op jit(solution)/shard_map/ppermute | solution.py:11
  60.0 0.7 copy-start.8
  60.1 0.7 copy-start.9
  60.3 1.0 copy-start.5
  60.3 3.8 %copy-start.6 = (s32[1,1,1024]{2,1,0:T(1,128)S(1)}, s32[1,1,1024]{2,1,0:T(1,128)}, u32[]{:S(2)}) copy-start(s32[1,1,1024]{2,1,0:T(1,128)} %param.13) | copy-start | bytes 12292
  61.3 91.9 %copy-start.2 = (f32[16,2,2,8,128]{4,3,2,1,0:T(8,128)}, f32[16,2,2,8,128]{4,3,2,1,0:T(8,128)S(1)}, u32[]{:S(2)}) copy-start(f32[16,2,2,8,128]{4,3,2,1,0:T(8,128)S(1)} %fusion.7) | copy-start | bytes 786436
  61.3 74.5 %copy-start.1 = (f32[16,4,128]{2,1,0:T(4,128)S(1)}, f32[16,4,128]{2,1,0:T(4,128)}, u32[]{:S(2)}) copy-start(f32[16,4,128]{2,1,0:T(4,128)} %param.14) | copy-start | bytes 98308
  61.3 107.5 %copy-start.7 = (f32[4,128]{1,0:T(4,128)S(1)}, f32[4,128]{1,0:T(4,128)}, u32[]{:S(2)}) copy-start(f32[4,128]{1,0:T(4,128)} %param.15) | copy-start | bytes 6148
  61.4 6.4 %collective-permute-start.8 = (f32[1024,16]{0,1:T(8,128)S(1)}, f32[1024,16]{0,1:T(8,128)S(1)}, u32[]{:S(2)}, u32[]{:S(2)}) collective-permute-start(f32[1024,16]{0,1:T(8,128)S(1)} %fusion.23), channel_id=1, source_target_pairs={{0,3},{4,7},{8,11},{12,15},{16,19},{20,23},{24,27},{28,31},{32,35}... | collective-permute-start | bytes 196616 | tf_op jit(solution)/shard_map/ppermute | solution.py:77
  62.8 4.9 %collective-permute-start.7 = (f32[1024,16]{0,1:T(8,128)S(1)}, f32[1024,16]{0,1:T(8,128)S(1)}, u32[]{:S(2)}, u32[]{:S(2)}) collective-permute-start(f32[1024,16]{0,1:T(8,128)S(1)} %fusion.23), channel_id=1, source_target_pairs={{0,2},{4,6},{8,10},{12,14},{16,18},{20,22},{24,26},{28,30},{32,34}... | collective-permute-start | bytes 196616 | tf_op jit(solution)/shard_map/ppermute | solution.py:77
  63.5 4.3 %collective-permute-start.6 = (f32[1024,16]{0,1:T(8,128)S(1)}, f32[1024,16]{0,1:T(8,128)S(1)}, u32[]{:S(2)}, u32[]{:S(2)}) collective-permute-start(f32[1024,16]{0,1:T(8,128)S(1)} %fusion.23), channel_id=1, source_target_pairs={{0,1},{4,5},{8,9},{12,13},{16,17},{20,21},{24,25},{28,29},{32,33},... | collective-permute-start | bytes 196616 | tf_op jit(solution)/shard_map/ppermute | solution.py:77
  135.9 17.3 %collective-permute-start.12 = (f32[16,4,1]{2,1,0:T(4,128)S(1)}, f32[16,4,1]{2,1,0:T(4,128)S(1)}, u32[]{:S(2)}, u32[]{:S(2)}) collective-permute-start(f32[16,4,1]{2,1,0:T(4,128)S(1)} %get-tuple-element.23), channel_id=1, source_target_pairs={{0,1},{1,2},{2,3},{3,4},{4,5},{5,6},{6,7},{7,8},{8,9},{9,10},{10,1... | collective-permute-start | bytes 776 | tf_op jit(solution)/shard_map/ppermute | solution.py:11
  142.1 26.8 %collective-permute-start.9 = (f32[16,1,128]{2,1,0:T(1,128)S(1)}, f32[16,1,128]{2,1,0:T(1,128)S(1)}, u32[]{:S(2)}, u32[]{:S(2)}) collective-permute-start(f32[16,1,128]{2,1,0:T(1,128)S(1)} %get-tuple-element.25), channel_id=1, source_target_pairs={{64,0},{128,64},{192,128},{256,192},{320,256},{384,320},{448,384},... | collective-permute-start | bytes 24584 | tf_op jit(solution)/shard_map/ppermute | solution.py:12
  146.6 22.2 %collective-permute-start.10 = (f32[16,1,128]{2,1,0:T(1,128)S(1)}, f32[16,1,128]{2,1,0:T(1,128)S(1)}, u32[]{:S(2)}, u32[]{:S(2)}) collective-permute-start(f32[16,1,128]{2,1,0:T(1,128)S(1)} %get-tuple-element.24), channel_id=1, source_target_pairs={{0,64},{64,128},{128,192},{192,256},{256,320},{320,384},{384,448},... | collective-permute-start | bytes 24584 | tf_op jit(solution)/shard_map/ppermute | solution.py:11
  151.1 17.8 %collective-permute-start.11 = (f32[16,4,1]{2,1,0:T(4,128)S(1)}, f32[16,4,1]{2,1,0:T(4,128)S(1)}, u32[]{:S(2)}, u32[]{:S(2)}) collective-permute-start(f32[16,4,1]{2,1,0:T(4,128)S(1)} %get-tuple-element.22), channel_id=1, source_target_pairs={{1,0},{2,1},{3,2},{4,3},{5,4},{6,5},{7,6},{8,7},{9,8},{10,9},{11,1... | collective-permute-start | bytes 776 | tf_op jit(solution)/shard_map/ppermute | solution.py:12
  169.1 26.0 %collective-permute-start.13 = (f32[16,1,128]{2,1,0:T(1,128)S(1)}, f32[16,1,128]{2,1,0:T(1,128)S(1)}, u32[]{:S(2)}, u32[]{:S(2)}) collective-permute-start(f32[16,1,128]{2,1,0:T(1,128)S(1)} %get-tuple-element.21), channel_id=1, source_target_pairs={{64,0},{128,64},{192,128},{256,192},{320,256},{384,320},{448,384},... | collective-permute-start | bytes 24584 | tf_op jit(solution)/shard_map/ppermute | solution.py:12
  171.0 24.1 %collective-permute-start.14 = (f32[16,1,128]{2,1,0:T(1,128)S(1)}, f32[16,1,128]{2,1,0:T(1,128)S(1)}, u32[]{:S(2)}, u32[]{:S(2)}) collective-permute-start(f32[16,1,128]{2,1,0:T(1,128)S(1)} %get-tuple-element.20), channel_id=1, source_target_pairs={{0,64},{64,128},{128,192},{192,256},{256,320},{320,384},{384,448},... | collective-permute-start | bytes 24584 | tf_op jit(solution)/shard_map/ppermute | solution.py:11
  174.7 8.4 %collective-permute-start.16 = (f32[16,4,1]{2,1,0:T(4,128)S(1)}, f32[16,4,1]{2,1,0:T(4,128)S(1)}, u32[]{:S(2)}, u32[]{:S(2)}) collective-permute-start(f32[16,4,1]{2,1,0:T(4,128)S(1)} %get-tuple-element.19), channel_id=1, source_target_pairs={{0,1},{1,2},{2,3},{3,4},{4,5},{5,6},{6,7},{7,8},{8,9},{9,10},{10,1... | collective-permute-start | bytes 776 | tf_op jit(solution)/shard_map/ppermute | solution.py:11
  176.7 18.4 %collective-permute-start.15 = (f32[16,4,1]{2,1,0:T(4,128)S(1)}, f32[16,4,1]{2,1,0:T(4,128)S(1)}, u32[]{:S(2)}, u32[]{:S(2)}) collective-permute-start(f32[16,4,1]{2,1,0:T(4,128)S(1)} %get-tuple-element.18), channel_id=1, source_target_pairs={{1,0},{2,1},{3,2},{4,3},{5,4},{6,5},{7,6},{8,7},{9,8},{10,9},{11,1... | collective-permute-start | bytes 776 | tf_op jit(solution)/shard_map/ppermute | solution.py:12

commit v4 on v2

--- a/solution.py
+++ b/solution.py
@@ -77,20 +77,10 @@
     return jnp.where(keep, keys * capacity + slot_index, group_count * capacity)
 
 
-def corner_pairs(rows, cols, step_row, step_col):
-    pairs = []
-    for a in range(rows):
-        for j in range(cols):
-            if 0 <= a - step_row < rows and 0 <= j - step_col < cols:
-                pairs.append(((a - step_row) * cols + (j - step_col), a * cols + j))
-    return pairs
-
-
 def shards(velocity, viscosity, friction, owner, cell, directions, stiffness):
     probes = velocity.shape[0]
     depth, rows, cols = viscosity.shape
     column = ("mapy", "layer")
-    every = ("mapx", "mapy", "layer")
     count_x = lax.axis_size("mapx")
     count_col = lax.axis_size(column)
     count_layer = lax.axis_size("layer")
@@ -99,53 +89,33 @@
     fwd_x, bwd_x = steps(count_x)
     fwd_c, bwd_c = steps(count_col)
     fwd_y, bwd_y = steps(lax.axis_size("mapy"))
-    d, k = directions, stiffness
-    x_lo = send([stacked[:, :, -1:], d[:, -2:], k[-1:]], "mapx", fwd_x)
-    x_hi = send([stacked[:, :, :1], d[:, :2], k[:1]], "mapx", bwd_x)
-    c_lo = send([stacked[:, -1:], d[:, :, -2:], k[:, -1:]], column, fwd_c)
-    c_hi = send([stacked[:, :1], d[:, :, :2], k[:, :1]], column, bwd_c)
+    d = directions
+    fwd_l, bwd_l = steps(count_layer)
+    x_lo = send([stacked[:, :, -1:], d[:, -1:]], "mapx", fwd_x)
+    x_hi = send([stacked[:, :, :1], d[:, :1]], "mapx", bwd_x)
+    (z_lo,) = send([stacked[:, -1:]], "layer", fwd_l)
+    (z_hi,) = send([stacked[:, :1]], "layer", bwd_l)
     (y_lo,) = send([stacked[..., -1:]], "mapy", fwd_y)
     (y_hi,) = send([stacked[..., :1]], "mapy", bwd_y)
-    corner = {}
-    for sr, sc, src in ((1, 1, d[:, -1, -1]), (1, -1, d[:, -1, 0]), (-1, 1, d[:, 0, -1]), (-1, -1, d[:, 0, 0])):
-        corner[sr, sc] = lax.ppermute(src, every, corner_pairs(count_x, count_col, sr, sc))[:, None, None]
+    (c_lo,) = send([d[:, :, -1:]], column, fwd_c)
+    (c_hi,) = send([d[:, :, :1]], column, bwd_c)
 
-    z_lo = jnp.where(my_layer > 0, c_lo[0], jnp.zeros_like(c_lo[0]))
-    z_hi = jnp.where(my_layer < count_layer - 1, c_hi[0], jnp.zeros_like(c_hi[0]))
     extended = jnp.concatenate([z_lo, stacked, z_hi], axis=1)
     extended = jnp.concatenate([pad_dims(x_lo[0], (1,)), extended, pad_dims(x_hi[0], (1,))], axis=2)
     extended = jnp.concatenate([pad_dims(y_lo, (1, 2)), extended, pad_dims(y_hi, (1, 2))], axis=3)
     padded = extended[:-1].reshape(probes, 2, depth + 2, rows + 2, cols + 2)
     image = stencil(padded, extended[-1])
 
-    zero2 = jnp.zeros((probes, 1, 2), jnp.float32)
-    zero1 = jnp.zeros((probes, 1, 1), jnp.float32)
-    top = jnp.concatenate(
-        [
-            jnp.concatenate([zero2, x_lo[1][:, :1], zero2], axis=2),
-            jnp.concatenate([zero1, corner[1, 1], x_lo[1][:, 1:], corner[1, -1], zero1], axis=2),
-        ],
-        axis=1,
-    )
-    bottom = jnp.concatenate(
-        [
-            jnp.concatenate([zero1, corner[-1, 1], x_hi[1][:, :1], corner[-1, -1], zero1], axis=2),
-            jnp.concatenate([zero2, x_hi[1][:, 1:], zero2], axis=2),
-        ],
-        axis=1,
-    )
-    middle = jnp.concatenate([c_lo[1], d, c_hi[1]], axis=2)
-    wide = jnp.concatenate([top, middle, bottom], axis=1)
-    ring = jnp.concatenate(
-        [
-            pad_dims(x_lo[2], (1,)),
-            jnp.concatenate([c_lo[2], k, c_hi[2]], axis=1),
-            pad_dims(x_hi[2], (1,)),
-        ],
-        axis=0,
-    )
-    inner = ring[None] * laplace(wide)
-    prior = laplace(inner)
+    wide = jnp.concatenate([x_lo[1], d, x_hi[1]], axis=1)
+    wide = jnp.concatenate([pad_dims(c_lo, (1,)), wide, pad_dims(c_hi, (1,))], axis=2)
+    inner = stiffness[None] * laplace(wide)
+    (i_up,) = send([inner[:, -1:]], "mapx", fwd_x)
+    (i_down,) = send([inner[:, :1]], "mapx", bwd_x)
+    (i_left,) = send([inner[:, :, -1:]], column, fwd_c)
+    (i_right,) = send([inner[:, :, :1]], column, bwd_c)
+    ring = jnp.concatenate([i_up, inner, i_down], axis=1)
+    ring = jnp.concatenate([pad_dims(i_left, (1,)), ring, pad_dims(i_right, (1,))], axis=2)
+    prior = laplace(ring)
 
     face_count = rows * cols
     face_rows = (friction * (image[:, 0, 0] + image[:, 1, 0])).reshape(probes, face_count).T

time: 189 us -> 140 us (0.74)
  the two profiles are of different devices: /device:TPU:56 before, /device:TPU:896 now
where the time goes in v4:
time: 140 us; the launch traced here: 139 us
  starting transfers between devices  86.4 us (62%)
  waiting for transfers between devices  26.3 us (19%)
  other arithmetic  12.6 us (9%)
  local copies, waits for them, and re-layouts  12.3 us (9%)
    ppermute x12, starting transfers between devices, send(): got = lax.ppermute(flat, axis, pairs)  55.8 us
    ppermute x12, waiting for transfers between devices, send(): got = lax.ppermute(flat, axis, pairs)  24.6 us
    all_to_all x1, starting transfers between devices, shards(): lax.all_to_all(packed.reshape(count_y, capacity, probes + 1), 'mapy', spl...  18 us
    ppermute x3, starting transfers between devices, from_bottom(): total = total + lax.ppermute(x, axis, [(0, to)])  12.7 us
    another operation x3, other arithmetic  4.64 us
    scatter x1, local copies, waits for them, and re-layouts, shards(): jnp.zeros((total_slots + 1, probes + 1), jnp.float32).at[position]  3.13 us
    scatter-add x1, other arithmetic, shards(): jax.ops.segment_sum(got[:, :probes], got[:, probes].astype(jnp.int32), nu...  2.87 us
  transfers between devices with their start and end apart: 16, of which 5 were waited for; matrix products, arithmetic and copies ran while one was open for 10% of the time, Pallas kernels for 0%

profile of v4, /device:TPU:896, one launch (start us, length us, event | category | flops | bytes accessed | tf_op | source)
XLA Modules:
  0.0 138.9 jit_solution(10729195206454448350)
XLA Ops:
  0.7 1.0 copy.87
  1.7 0.8 fusion.33
  2.6 0.9 fusion.57
  3.4 1.9 %collective-permute-start.1 = (f32[10496]{0:T(1024)S(1)}, f32[10496]{0:T(1024)S(1)}, u32[]{:S(2)}, u32[]{:S(2)}) collective-permute-start(f32[10496]{0:T(1024)S(1)} %pad_maximum_fusion.2), channel_id=1, source_target_pairs={{0,64},{64,128},{128,192},{192,256},{256,320},{320,384},{384,448},... | collective-permute-start | bytes 125960 | tf_op jit(solution)/shard_map/ppermute | solution.py:9
  5.4 4.9 %collective-permute-start.4 = (f32[10496]{0:T(1024)S(1)}, f32[10496]{0:T(1024)S(1)}, u32[]{:S(2)}, u32[]{:S(2)}) collective-permute-start(f32[10496]{0:T(1024)S(1)} %pad_maximum_fusion.3), channel_id=1, source_target_pairs={{64,0},{128,64},{192,128},{256,192},{320,256},{384,320},{448,384},... | collective-permute-start | bytes 125960 | tf_op jit(solution)/shard_map/ppermute | solution.py:9
  10.3 0.9 fusion.5
  11.8 3.4 %collective-permute-start = (f32[528]{0:T(1024)S(1)}, f32[528]{0:T(1024)S(1)}, u32[]{:S(2)}, u32[]{:S(2)}) collective-permute-start(f32[528]{0:T(1024)S(1)} %reshape.333), channel_id=1, source_target_pairs={{0,4},{4,8},{8,12},{12,16},{16,20},{20,24},{24,28},{28,32},{32,36}... | collective-permute-start | bytes 6344 | tf_op jit(solution)/shard_map/ppermute | solution.py:9
  15.4 15.7 %collective-permute-start.9 = (f32[64]{0:T(128)S(1)}, f32[64]{0:T(128)S(1)}, u32[]{:S(2)}, u32[]{:S(2)}) collective-permute-start(f32[64]{0:T(128)S(1)} %reshape.353), channel_id=1, source_target_pairs={{1,0},{2,1},{3,2},{4,3},{5,4},{6,5},{7,6},{8,7},{9,8},{10,9},{11,1... | collective-permute-start | bytes 776 | tf_op jit(solution)/shard_map/ppermute | solution.py:9
  31.3 1.9 %collective-permute-start.10 = (f32[64]{0:T(128)S(1)}, f32[64]{0:T(128)S(1)}, u32[]{:S(2)}, u32[]{:S(2)}) collective-permute-start(f32[64]{0:T(128)S(1)} %reshape.355), channel_id=1, source_target_pairs={{0,1},{1,2},{2,3},{3,4},{4,5},{5,6},{6,7},{7,8},{8,9},{9,10},{10,1... | collective-permute-start | bytes 776 | tf_op jit(solution)/shard_map/ppermute | solution.py:9
  33.3 4.5 %reduce-window.6 = s32[16,8,128]{2,1,0:T(8,128)S(1)} reduce-window(s32[16,8,128]{2,1,0:T(8,128)S(1)} %fusion.31, s32[]{:T(128)} %constant.47.clone.1), window={size=1x1x128 pad=0_0x0_0x127_0}, to_apply=%region_0.1 | reduce-window | flops 2080768 | bytes 131076 | tf_op jit(solution)/shard_map/reduce-window
  38.9 1.9 %collective-permute-start.5 = (f32[528]{0:T(1024)S(1)}, f32[528]{0:T(1024)S(1)}, u32[]{:S(2)}, u32[]{:S(2)}) collective-permute-start(f32[528]{0:T(1024)S(1)} %reshape.343), channel_id=1, source_target_pairs={{4,0},{8,4},{12,8},{16,12},{20,16},{24,20},{28,24},{32,28},{36,32}... | collective-permute-start | bytes 6344 | tf_op jit(solution)/shard_map/ppermute | solution.py:9
  40.9 8.8 %collective-permute-done.10 = f32[64]{0:T(128)S(1)} collective-permute-done((f32[64]{0:T(128)S(1)}, f32[64]{0:T(128)S(1)}, u32[]{:S(2)}, u32[]{:S(2)}) %collective-permute-start.10) | collective-permute-done | bytes 288 | tf_op jit(solution)/shard_map/ppermute | solution.py:9
  49.7 1.3 collective-permute-start.2
  51.0 1.3 collective-permute-start.3
  54.0 3.9 %collective-permute-done.3 = f32[33792]{0:T(1024)S(1)} collective-permute-done((f32[33792]{0:T(1024)S(1)}, f32[33792]{0:T(1024)S(1)}, u32[]{:S(2)}, u32[]{:S(2)}) %collective-permute-start.3) | collective-permute-done | bytes 135200 | tf_op jit(solution)/shard_map/ppermute | solution.py:9
  57.9 1.1 select_maximum_fusion
  60.4 8.6 %collective-permute-start.6 = (f32[1024,16]{0,1:T(8,128)S(1)}, f32[1024,16]{0,1:T(8,128)S(1)}, u32[]{:S(2)}, u32[]{:S(2)}) collective-permute-start(f32[1024,16]{0,1:T(8,128)S(1)} %fusion.25), channel_id=1, source_target_pairs={{0,1},{4,5},{8,9},{12,13},{16,17},{20,21},{24,25},{28,29},{32,33},... | collective-permute-start | bytes 196616 | tf_op jit(solution)/shard_map/ppermute | solution.py:67
  69.1 2.7 %collective-permute-start.7 = (f32[1024,16]{0,1:T(8,128)S(1)}, f32[1024,16]{0,1:T(8,128)S(1)}, u32[]{:S(2)}, u32[]{:S(2)}) collective-permute-start(f32[1024,16]{0,1:T(8,128)S(1)} %fusion.25), channel_id=1, source_target_pairs={{0,2},{4,6},{8,10},{12,14},{16,18},{20,22},{24,26},{28,30},{32,34}... | collective-permute-start | bytes 196616 | tf_op jit(solution)/shard_map/ppermute | solution.py:67
  71.8 1.3 collective-permute-start.8
  73.7 1.3 collective-permute-done.8
  75.3 3.1 %scatter_custom_fusion = f32[513,17]{1,0:T(8,128)S(1)} fusion(s32[1024]{0:T(1024)S(1)} %bitcast.126, f32[1024,17]{1,0:T(8,128)S(1)} %copy.105, f32[]{:T(128)} %constant.45.clone.1), kind=kCustom, calls=%fused_computation.48 | custom fusion | bytes 34888 | tf_op jit(solution)/shard_map/scatter | solution.py:133
  78.6 0.7 reshape.393
  79.3 18.0 %all-to-all-start = ((f32[16,1,544]{2,1,0:T(1,128)}), f32[16,1,544]{2,1,0:T(1,128)S(1)}, u32[]{:S(2)}, u32[]{:S(2)}) async-start(f32[16,1,544]{2,1,0:T(1,128)} %reshape.393), calls=%async_computation | async-start | bytes 81920 | tf_op jit(solution)/shard_map/all_to_all | solution.py:135
  97.6 17.2 %collective-permute-start.13 = (f32[64]{0:T(128)S(1)}, f32[64]{0:T(128)S(1)}, u32[]{:S(2)}, u32[]{:S(2)}) collective-permute-start(f32[64]{0:T(128)S(1)} %reshape.361), channel_id=1, source_target_pairs={{1,0},{2,1},{3,2},{4,3},{5,4},{6,5},{7,6},{8,7},{9,8},{10,9},{11,1... | collective-permute-start | bytes 776 | tf_op jit(solution)/shard_map/ppermute | solution.py:9
  114.9 1.9 %collective-permute-start.14 = (f32[64]{0:T(128)S(1)}, f32[64]{0:T(128)S(1)}, u32[]{:S(2)}, u32[]{:S(2)}) collective-permute-start(f32[64]{0:T(128)S(1)} %reshape.363), channel_id=1, source_target_pairs={{0,1},{1,2},{2,3},{3,4},{4,5},{5,6},{6,7},{7,8},{8,9},{9,10},{10,1... | collective-permute-start | bytes 776 | tf_op jit(solution)/shard_map/ppermute | solution.py:9
  116.9 1.9 %collective-permute-start.11 = (f32[2048]{0:T(1024)S(1)}, f32[2048]{0:T(1024)S(1)}, u32[]{:S(2)}, u32[]{:S(2)}) collective-permute-start(f32[2048]{0:T(1024)S(1)} %bitcast.123), channel_id=1, source_target_pairs={{64,0},{128,64},{192,128},{256,192},{320,256},{384,320},{448,384},... | collective-permute-start | bytes 24584 | tf_op jit(solution)/shard_map/ppermute | solution.py:9
  118.8 2.4 %collective-permute-start.12 = (f32[2048]{0:T(1024)S(1)}, f32[2048]{0:T(1024)S(1)}, u32[]{:S(2)}, u32[]{:S(2)}) collective-permute-start(f32[2048]{0:T(1024)S(1)} %bitcast.122), channel_id=1, source_target_pairs={{0,64},{64,128},{128,192},{192,256},{256,320},{320,384},{384,448},... | collective-permute-start | bytes 24584 | tf_op jit(solution)/shard_map/ppermute | solution.py:9
  121.4 11.9 %collective-permute-done.14 = f32[64]{0:T(128)S(1)} collective-permute-done((f32[64]{0:T(128)S(1)}, f32[64]{0:T(128)S(1)}, u32[]{:S(2)}, u32[]{:S(2)}) %collective-permute-start.14) | collective-permute-done | bytes 288 | tf_op jit(solution)/shard_map/ppermute | solution.py:9
  133.5 0.5 broadcast.302
  134.0 0.7 reduce.8
  135.1 2.9 %scatter_custom_fusion.1 = f32[512,16]{1,0:T(8,128)S(1)} fusion(s32[512]{0:T(512)S(1)} %bitcast.127, f32[512,16]{1,0:T(8,128)S(1)} %copy.108, f32[]{:T(128)} %constant.45.clone.1), kind=kCustom, calls=%fused_computation.50 | custom fusion | flops 8192 | bytes 32772 | tf_op jit(solution)/shard_map/scatter-add | solution.py:144
  138.1 0.8 fusion.37
  (99 shorter events, 7.3 us)
Async XLA Ops:
  0.6 32.6 %copy-start.2 = (f32[2,8,128]{2,1,0:T(8,128)S(1)}, f32[2,8,128]{2,1,0:T(8,128)}, u32[]{:S(2)}) copy-start(f32[2,8,128]{2,1,0:T(8,128)} %param.10) | copy-start | bytes 24580
  0.6 14.5 %copy-start = (f32[16,4,128]{2,1,0:T(4,128)S(1)}, f32[16,4,128]{2,1,0:T(4,128)}, u32[]{:S(2)}) copy-start(f32[16,4,128]{2,1,0:T(4,128)} %param.14) | copy-start | bytes 98308
  0.7 32.6 %copy-start.3 = (s32[1,1,1024,1]{2,3,1,0:T(1,128)S(1)}, s32[1,1,1024,1]{2,3,1,0:T(1,128)}, u32[]{:S(2)}) copy-start(s32[1,1,1024,1]{2,3,1,0:T(1,128)} %param.12) | copy-start | bytes 12292
  0.7 51.6 %copy-start.5 = (s32[1,1,1024]{2,1,0:T(1,128)S(1)}, s32[1,1,1024]{2,1,0:T(1,128)}, u32[]{:S(2)}) copy-start(s32[1,1,1024]{2,1,0:T(1,128)} %param.13) | copy-start | bytes 12292
  3.4 50.3 %collective-permute-start.1 = (f32[10496]{0:T(1024)S(1)}, f32[10496]{0:T(1024)S(1)}, u32[]{:S(2)}, u32[]{:S(2)}) collective-permute-start(f32[10496]{0:T(1024)S(1)} %pad_maximum_fusion.2), channel_id=1, source_target_pairs={{0,64},{64,128},{128,192},{192,256},{256,320},{320,384},{384,448},... | collective-permute-start | bytes 125960 | tf_op jit(solution)/shard_map/ppermute | solution.py:9
  5.4 48.4 %collective-permute-start.4 = (f32[10496]{0:T(1024)S(1)}, f32[10496]{0:T(1024)S(1)}, u32[]{:S(2)}, u32[]{:S(2)}) collective-permute-start(f32[10496]{0:T(1024)S(1)} %pad_maximum_fusion.3), channel_id=1, source_target_pairs={{64,0},{128,64},{192,128},{256,192},{320,256},{384,320},{448,384},... | collective-permute-start | bytes 125960 | tf_op jit(solution)/shard_map/ppermute | solution.py:9
  11.8 39.2 %collective-permute-start = (f32[528]{0:T(1024)S(1)}, f32[528]{0:T(1024)S(1)}, u32[]{:S(2)}, u32[]{:S(2)}) collective-permute-start(f32[528]{0:T(1024)S(1)} %reshape.333), channel_id=1, source_target_pairs={{0,4},{4,8},{8,12},{12,16},{16,20},{20,24},{24,28},{28,32},{32,36}... | collective-permute-start | bytes 6344 | tf_op jit(solution)/shard_map/ppermute | solution.py:9
  15.4 23.5 %collective-permute-start.9 = (f32[64]{0:T(128)S(1)}, f32[64]{0:T(128)S(1)}, u32[]{:S(2)}, u32[]{:S(2)}) collective-permute-start(f32[64]{0:T(128)S(1)} %reshape.353), channel_id=1, source_target_pairs={{1,0},{2,1},{3,2},{4,3},{5,4},{6,5},{7,6},{8,7},{9,8},{10,9},{11,1... | collective-permute-start | bytes 776 | tf_op jit(solution)/shard_map/ppermute | solution.py:9
  31.3 18.4 %collective-permute-start.10 = (f32[64]{0:T(128)S(1)}, f32[64]{0:T(128)S(1)}, u32[]{:S(2)}, u32[]{:S(2)}) collective-permute-start(f32[64]{0:T(128)S(1)} %reshape.355), channel_id=1, source_target_pairs={{0,1},{1,2},{2,3},{3,4},{4,5},{5,6},{6,7},{7,8},{8,9},{9,10},{10,1... | collective-permute-start | bytes 776 | tf_op jit(solution)/shard_map/ppermute | solution.py:9
  38.9 14.3 %collective-permute-start.5 = (f32[528]{0:T(1024)S(1)}, f32[528]{0:T(1024)S(1)}, u32[]{:S(2)}, u32[]{:S(2)}) collective-permute-start(f32[528]{0:T(1024)S(1)} %reshape.343), channel_id=1, source_target_pairs={{4,0},{8,4},{12,8},{16,12},{20,16},{24,20},{28,24},{32,28},{36,32}... | collective-permute-start | bytes 6344 | tf_op jit(solution)/shard_map/ppermute | solution.py:9
  49.7 4.3 %collective-permute-start.2 = (f32[33792]{0:T(1024)S(1)}, f32[33792]{0:T(1024)S(1)}, u32[]{:S(2)}, u32[]{:S(2)}) collective-permute-start(f32[33792]{0:T(1024)S(1)} %get-tuple-element.13), channel_id=1, source_target_pairs={{0,1},{1,2},{2,3},{4,5},{5,6},{6,7},{8,9},{9,10},{10,11},{12,13},{... | collective-permute-start | bytes 405512 | tf_op jit(solution)/shard_map/ppermute | solution.py:9
  51.0 6.9 %collective-permute-start.3 = (f32[33792]{0:T(1024)S(1)}, f32[33792]{0:T(1024)S(1)}, u32[]{:S(2)}, u32[]{:S(2)}) collective-permute-start(f32[33792]{0:T(1024)S(1)} %get-tuple-element.14), channel_id=1, source_target_pairs={{1,0},{2,1},{3,2},{5,4},{6,5},{7,6},{9,8},{10,9},{11,10},{13,12},{... | collective-permute-start | bytes 405512 | tf_op jit(solution)/shard_map/ppermute | solution.py:9
  59.1 0.7 copy-start.7
  59.2 0.7 copy-start.8
  59.7 0.7 copy-start.4
  59.7 13.4 %copy-start.6 = (f32[4,128]{1,0:T(4,128)S(1)}, f32[4,128]{1,0:T(4,128)}, u32[]{:S(2)}) copy-start(f32[4,128]{1,0:T(4,128)} %param.15) | copy-start | bytes 6148
  60.0 75.1 %copy-start.1 = (f32[16,2,2,8,128]{4,3,2,1,0:T(8,128)}, f32[16,2,2,8,128]{4,3,2,1,0:T(8,128)S(1)}, u32[]{:S(2)}) copy-start(f32[16,2,2,8,128]{4,3,2,1,0:T(8,128)S(1)} %fusion.7) | copy-start | bytes 786436
  60.4 12.9 %collective-permute-start.6 = (f32[1024,16]{0,1:T(8,128)S(1)}, f32[1024,16]{0,1:T(8,128)S(1)}, u32[]{:S(2)}, u32[]{:S(2)}) collective-permute-start(f32[1024,16]{0,1:T(8,128)S(1)} %fusion.25), channel_id=1, source_target_pairs={{0,1},{4,5},{8,9},{12,13},{16,17},{20,21},{24,25},{28,29},{32,33},... | collective-permute-start | bytes 196616 | tf_op jit(solution)/shard_map/ppermute | solution.py:67
  69.1 4.6 %collective-permute-start.7 = (f32[1024,16]{0,1:T(8,128)S(1)}, f32[1024,16]{0,1:T(8,128)S(1)}, u32[]{:S(2)}, u32[]{:S(2)}) collective-permute-start(f32[1024,16]{0,1:T(8,128)S(1)} %fusion.25), channel_id=1, source_target_pairs={{0,2},{4,6},{8,10},{12,14},{16,18},{20,22},{24,26},{28,30},{32,34}... | collective-permute-start | bytes 196616 | tf_op jit(solution)/shard_map/ppermute | solution.py:67
  71.8 3.2 %collective-permute-start.8 = (f32[1024,16]{0,1:T(8,128)S(1)}, f32[1024,16]{0,1:T(8,128)S(1)}, u32[]{:S(2)}, u32[]{:S(2)}) collective-permute-start(f32[1024,16]{0,1:T(8,128)S(1)} %fusion.25), channel_id=1, source_target_pairs={{0,3},{4,7},{8,11},{12,15},{16,19},{20,23},{24,27},{28,31},{32,35}... | collective-permute-start | bytes 196616 | tf_op jit(solution)/shard_map/ppermute | solution.py:67
  79.3 54.1 %all-to-all-start = ((f32[16,1,544]{2,1,0:T(1,128)}), f32[16,1,544]{2,1,0:T(1,128)S(1)}, u32[]{:S(2)}, u32[]{:S(2)}) async-start(f32[16,1,544]{2,1,0:T(1,128)} %reshape.393), calls=%async_computation | async-start | bytes 81920 | tf_op jit(solution)/shard_map/all_to_all | solution.py:135
  97.6 23.6 %collective-permute-start.13 = (f32[64]{0:T(128)S(1)}, f32[64]{0:T(128)S(1)}, u32[]{:S(2)}, u32[]{:S(2)}) collective-permute-start(f32[64]{0:T(128)S(1)} %reshape.361), channel_id=1, source_target_pairs={{1,0},{2,1},{3,2},{4,3},{5,4},{6,5},{7,6},{8,7},{9,8},{10,9},{11,1... | collective-permute-start | bytes 776 | tf_op jit(solution)/shard_map/ppermute | solution.py:9
  114.9 18.4 %collective-permute-start.14 = (f32[64]{0:T(128)S(1)}, f32[64]{0:T(128)S(1)}, u32[]{:S(2)}, u32[]{:S(2)}) collective-permute-start(f32[64]{0:T(128)S(1)} %reshape.363), channel_id=1, source_target_pairs={{0,1},{1,2},{2,3},{3,4},{4,5},{5,6},{6,7},{7,8},{8,9},{9,10},{10,1... | collective-permute-start | bytes 776 | tf_op jit(solution)/shard_map/ppermute | solution.py:9
  116.9 21.3 %collective-permute-start.11 = (f32[2048]{0:T(1024)S(1)}, f32[2048]{0:T(1024)S(1)}, u32[]{:S(2)}, u32[]{:S(2)}) collective-permute-start(f32[2048]{0:T(1024)S(1)} %bitcast.123), channel_id=1, source_target_pairs={{64,0},{128,64},{192,128},{256,192},{320,256},{384,320},{448,384},... | collective-permute-start | bytes 24584 | tf_op jit(solution)/shard_map/ppermute | solution.py:9
  118.8 19.3 %collective-permute-start.12 = (f32[2048]{0:T(1024)S(1)}, f32[2048]{0:T(1024)S(1)}, u32[]{:S(2)}, u32[]{:S(2)}) collective-permute-start(f32[2048]{0:T(1024)S(1)} %bitcast.122), channel_id=1, source_target_pairs={{0,64},{64,128},{128,192},{192,256},{256,320},{320,384},{384,448},... | collective-permute-start | bytes 24584 | tf_op jit(solution)/shard_map/ppermute | solution.py:9

commit v5 on v4

--- a/solution.py
+++ b/solution.py
@@ -124,21 +124,29 @@
     count_y = lax.axis_size("mapy")
     owner_count = count_y * count_layer
     capacity = 2 * face_count // owner_count
-    spread = from_bottom(face_rows, "layer")
-    keep = targets % count_layer == my_layer
-    position = slot_places(targets // count_layer, count_y, capacity, keep)
-    total_slots = count_y * capacity
-    rows_out = jnp.concatenate([spread, local_cells[:, None]], axis=1)
-    packed = (
-        jnp.zeros((total_slots + 1, probes + 1), jnp.float32).at[position].set(rows_out)[:total_slots]
+    onehot = (targets[:, None] == jnp.arange(owner_count, dtype=jnp.int32)[None, :]).astype(
+        jnp.bfloat16
+    )
+    order = lax.broadcasted_iota(jnp.int32, (face_count, face_count), 0)
+    earlier = (order > lax.broadcasted_iota(jnp.int32, (face_count, face_count), 1)).astype(
+        jnp.bfloat16
+    )
+    before = jnp.dot(earlier, onehot, preferred_element_type=jnp.float32)
+    rank = jnp.sum(before * onehot.astype(jnp.float32), axis=1).astype(jnp.int32)
+    position = targets * capacity + rank
+    total_slots = owner_count * capacity
+    rows_out = jnp.concatenate([face_rows, local_cells[:, None]], axis=1)
+    packed = jnp.zeros((total_slots, probes + 1), jnp.float32).at[position].set(
+        rows_out, mode="drop"
     )
     got = lax.all_to_all(
-        packed.reshape(count_y, capacity, probes + 1),
-        "mapy",
+        packed.reshape(owner_count, capacity, probes + 1),
+        column,
         split_axis=0,
         concat_axis=0,
         tiled=True,
-    ).reshape(-1, probes + 1)
+    ).reshape(count_y, count_layer, capacity, probes + 1)[:, 0]
+    got = got.reshape(-1, probes + 1)
     map_rows = directions.shape[1]
     map_cols = directions.shape[2]
     summed = jax.ops.segment_sum(

time: 140 us -> 134 us (0.957)
  starting transfers between devices: 86.4 us -> 74.5 us
  waiting for transfers between devices: 26.3 us -> 34.6 us
  other arithmetic: 12.6 us -> 8.86 us
    ppermute x3 -> x0, starting transfers between devices: 12.7 us -> none  [from_bottom(): total = total + lax.ppermute(x, axis, [(0, to)])]
    ppermute x12, waiting for transfers between devices: 24.6 us -> 34.6 us  [send(): got = lax.ppermute(flat, axis, pairs)]
    all_to_all x1, starting transfers between devices: 18 us -> 23.3 us  [shards(): lax.all_to_all(packed.reshape(owner_count, capacity, probes + 1), column,...]
    another operation x3 -> x0, other arithmetic: 4.64 us -> none
    ppermute x12, starting transfers between devices: 55.8 us -> 51.2 us  [send(): got = lax.ppermute(flat, axis, pairs)]
    ppermute x3 -> x0, waiting for transfers between devices: 1.67 us -> none  [from_bottom(): total = total + lax.ppermute(x, axis, [(0, to)])]
    unnamed x23 -> x24, local copies, waits for them, and re-layouts: 2.78 us -> 3.25 us
  transfers between devices with their start and end apart: 16 -> 13, of which waited for: 5 -> 3; matrix products, arithmetic and copies ran while one was open for 10% -> 9% of each run, Pallas kernels for 0% -> 0%
where the time goes in v5:
time: 134 us; the launch traced here: 133 us
  starting transfers between devices  74.5 us (56%)
  waiting for transfers between devices  34.6 us (26%)
  local copies, waits for them, and re-layouts  13.3 us (10%)
  other arithmetic  8.86 us (7%)
    ppermute x12, starting transfers between devices, send(): got = lax.ppermute(flat, axis, pairs)  51.2 us
    ppermute x12, waiting for transfers between devices, send(): got = lax.ppermute(flat, axis, pairs)  34.6 us
    all_to_all x1, starting transfers between devices, shards(): lax.all_to_all(packed.reshape(owner_count, capacity, probes + 1), column,...  23.3 us
    scatter-add x1, other arithmetic, shards(): jax.ops.segment_sum(got[:, :probes], got[:, probes].astype(jnp.int32), nu...  3.63 us
    scatter x1, local copies, waits for them, and re-layouts, shards(): jnp.zeros((total_slots, probes + 1), jnp.float32).at[position]  3.34 us
    unnamed x24, local copies, waits for them, and re-layouts  3.25 us
  transfers between devices with their start and end apart: 13, of which 3 were waited for; matrix products, arithmetic and copies ran while one was open for 9% of the time, Pallas kernels for 0%

profile of v5, /device:TPU:896, one launch (start us, length us, event | category | flops | bytes accessed | tf_op | source)
XLA Modules:
  0.0 133.1 jit_solution(8467556779741627951)
XLA Ops:
  0.7 1.0 copy.57
  1.6 0.8 fusion.32
  2.5 0.9 fusion.50
  3.4 3.6 %collective-permute-start.4 = (f32[10496]{0:T(1024)S(1)}, f32[10496]{0:T(1024)S(1)}, u32[]{:S(2)}, u32[]{:S(2)}) collective-permute-start(f32[10496]{0:T(1024)S(1)} %pad_maximum_fusion.3), channel_id=1, source_target_pairs={{64,0},{128,64},{192,128},{256,192},{320,256},{384,320},{448,384},... | collective-permute-start | bytes 125960 | tf_op jit(solution)/shard_map/ppermute | solution.py:9
  7.0 1.9 %collective-permute-start.1 = (f32[10496]{0:T(1024)S(1)}, f32[10496]{0:T(1024)S(1)}, u32[]{:S(2)}, u32[]{:S(2)}) collective-permute-start(f32[10496]{0:T(1024)S(1)} %pad_maximum_fusion.2), channel_id=1, source_target_pairs={{0,64},{64,128},{128,192},{192,256},{256,320},{320,384},{384,448},... | collective-permute-start | bytes 125960 | tf_op jit(solution)/shard_map/ppermute | solution.py:9
  9.0 0.9 fusion.10
  9.9 0.5 copy.63
  10.5 10.6 %collective-permute-start.5 = (f32[528]{0:T(1024)S(1)}, f32[528]{0:T(1024)S(1)}, u32[]{:S(2)}, u32[]{:S(2)}) collective-permute-start(f32[528]{0:T(1024)S(1)} %reshape.206), channel_id=1, source_target_pairs={{4,0},{8,4},{12,8},{16,12},{20,16},{24,20},{28,24},{32,28},{36,32}... | collective-permute-start | bytes 6344 | tf_op jit(solution)/shard_map/ppermute | solution.py:9
  21.7 1.9 %collective-permute-start = (f32[528]{0:T(1024)S(1)}, f32[528]{0:T(1024)S(1)}, u32[]{:S(2)}, u32[]{:S(2)}) collective-permute-start(f32[528]{0:T(1024)S(1)} %reshape.196), channel_id=1, source_target_pairs={{0,4},{4,8},{8,12},{12,16},{16,20},{20,24},{24,28},{28,32},{32,36}... | collective-permute-start | bytes 6344 | tf_op jit(solution)/shard_map/ppermute | solution.py:9
  23.6 3.5 %collective-permute-start.2 = (f32[33792]{0:T(1024)S(1)}, f32[33792]{0:T(1024)S(1)}, u32[]{:S(2)}, u32[]{:S(2)}) collective-permute-start(f32[33792]{0:T(1024)S(1)} %get-tuple-element.13), channel_id=1, source_target_pairs={{0,1},{1,2},{2,3},{4,5},{5,6},{6,7},{8,9},{9,10},{10,11},{12,13},{... | collective-permute-start | bytes 405512 | tf_op jit(solution)/shard_map/ppermute | solution.py:9
  27.2 0.6 fusion.7
  27.8 1.3 collective-permute-start.3
  29.2 0.5 copy.64
  29.7 8.3 %collective-permute-done = f32[528]{0:T(1024)S(1)} collective-permute-done((f32[528]{0:T(1024)S(1)}, f32[528]{0:T(1024)S(1)}, u32[]{:S(2)}, u32[]{:S(2)}) %collective-permute-start) | collective-permute-done | bytes 2144 | tf_op jit(solution)/shard_map/ppermute | solution.py:9
  38.1 0.5 copy.90
  38.8 1.1 select_maximum_fusion
  40.2 0.5 fusion.48
  41.6 3.3 %scatter_custom_fusion = f32[2048,17]{1,0:T(8,128)S(1)} fusion(s32[1024]{0:T(1024)S(1)} %bitcast.87, f32[1024,17]{1,0:T(8,128)S(1)} %copy.73, f32[]{:T(128)} %constant.9.clone.1), kind=kCustom, calls=%fused_computation.25 | custom fusion | bytes 139268 | tf_op jit(solution)/shard_map/scatter | solution.py:139
  45.4 1.0 reshape.259
  46.4 23.3 %all-to-all-start = ((f32[64,1,544]{2,1,0:T(1,128)}), f32[64,1,544]{2,1,0:T(1,128)S(1)}, u32[]{:S(2)}, u32[]{:S(2)}) async-start(f32[64,1,544]{2,1,0:T(1,128)} %reshape.259), calls=%async_computation | async-start | bytes 327680 | tf_op jit(solution)/shard_map/all_to_all | solution.py:142
  70.0 16.3 %collective-permute-start.6 = (f32[64]{0:T(128)S(1)}, f32[64]{0:T(128)S(1)}, u32[]{:S(2)}, u32[]{:S(2)}) collective-permute-start(f32[64]{0:T(128)S(1)} %reshape.212), channel_id=1, source_target_pairs={{1,0},{2,1},{3,2},{4,3},{5,4},{6,5},{7,6},{8,7},{9,8},{10,9},{11,1... | collective-permute-start | bytes 776 | tf_op jit(solution)/shard_map/ppermute | solution.py:9
  86.4 1.9 %collective-permute-start.7 = (f32[64]{0:T(128)S(1)}, f32[64]{0:T(128)S(1)}, u32[]{:S(2)}, u32[]{:S(2)}) collective-permute-start(f32[64]{0:T(128)S(1)} %reshape.214), channel_id=1, source_target_pairs={{0,1},{1,2},{2,3},{3,4},{4,5},{5,6},{6,7},{7,8},{8,9},{9,10},{10,1... | collective-permute-start | bytes 776 | tf_op jit(solution)/shard_map/ppermute | solution.py:9
  88.5 16.3 %collective-permute-done.7 = f32[64]{0:T(128)S(1)} collective-permute-done((f32[64]{0:T(128)S(1)}, f32[64]{0:T(128)S(1)}, u32[]{:S(2)}, u32[]{:S(2)}) %collective-permute-start.7) | collective-permute-done | bytes 288 | tf_op jit(solution)/shard_map/ppermute | solution.py:9
  105.4 1.9 %collective-permute-start.10 = (f32[64]{0:T(128)S(1)}, f32[64]{0:T(128)S(1)}, u32[]{:S(2)}, u32[]{:S(2)}) collective-permute-start(f32[64]{0:T(128)S(1)} %reshape.220), channel_id=1, source_target_pairs={{1,0},{2,1},{3,2},{4,3},{5,4},{6,5},{7,6},{8,7},{9,8},{10,9},{11,1... | collective-permute-start | bytes 776 | tf_op jit(solution)/shard_map/ppermute | solution.py:9
  107.4 3.9 %collective-permute-start.11 = (f32[64]{0:T(128)S(1)}, f32[64]{0:T(128)S(1)}, u32[]{:S(2)}, u32[]{:S(2)}) collective-permute-start(f32[64]{0:T(128)S(1)} %reshape.222), channel_id=1, source_target_pairs={{0,1},{1,2},{2,3},{3,4},{4,5},{5,6},{6,7},{7,8},{8,9},{9,10},{10,1... | collective-permute-start | bytes 776 | tf_op jit(solution)/shard_map/ppermute | solution.py:9
  111.4 1.9 %collective-permute-start.8 = (f32[2048]{0:T(1024)S(1)}, f32[2048]{0:T(1024)S(1)}, u32[]{:S(2)}, u32[]{:S(2)}) collective-permute-start(f32[2048]{0:T(1024)S(1)} %bitcast.82), channel_id=1, source_target_pairs={{64,0},{128,64},{192,128},{256,192},{320,256},{384,320},{448,384},... | collective-permute-start | bytes 24584 | tf_op jit(solution)/shard_map/ppermute | solution.py:9
  113.3 2.4 %collective-permute-start.9 = (f32[2048]{0:T(1024)S(1)}, f32[2048]{0:T(1024)S(1)}, u32[]{:S(2)}, u32[]{:S(2)}) collective-permute-start(f32[2048]{0:T(1024)S(1)} %bitcast.81), channel_id=1, source_target_pairs={{0,64},{64,128},{128,192},{192,256},{256,320},{320,384},{384,448},... | collective-permute-start | bytes 24584 | tf_op jit(solution)/shard_map/ppermute | solution.py:9
  115.9 9.9 %collective-permute-done.11 = f32[64]{0:T(128)S(1)} collective-permute-done((f32[64]{0:T(128)S(1)}, f32[64]{0:T(128)S(1)}, u32[]{:S(2)}, u32[]{:S(2)}) %collective-permute-start.11) | collective-permute-done | bytes 288 | tf_op jit(solution)/shard_map/ppermute | solution.py:9
  126.0 0.5 broadcast.146
  126.5 1.0 reduce.12
  128.5 3.6 %scatter_custom_fusion.1 = f32[512,16]{1,0:T(8,128)S(1)} fusion(s32[512]{0:T(512)S(1)} %bitcast.88, f32[512,16]{1,0:T(8,128)S(1)} %copy.89, f32[]{:T(128)} %constant.9.clone.1), kind=kCustom, calls=%fused_computation.58 | custom fusion | flops 8192 | bytes 32772 | tf_op jit(solution)/shard_map/scatter-add | solution.py:152
  132.3 0.8 fusion.36
  (81 shorter events, 5.4 us)
Async XLA Ops:
  0.6 23.0 %copy-start.2 = (f32[2,8,128]{2,1,0:T(8,128)S(1)}, f32[2,8,128]{2,1,0:T(8,128)}, u32[]{:S(2)}) copy-start(f32[2,8,128]{2,1,0:T(8,128)} %param.10) | copy-start | bytes 24580
  0.6 26.5 %copy-start.3 = (s32[1,1,1024,1]{2,3,1,0:T(1,128)S(1)}, s32[1,1,1024,1]{2,3,1,0:T(1,128)}, u32[]{:S(2)}) copy-start(s32[1,1,1024,1]{2,3,1,0:T(1,128)} %param.12) | copy-start | bytes 12292
  2.5 26.6 %copy-start.5 = (s32[1,1,1024]{2,1,0:T(1,128)S(1)}, s32[1,1,1024]{2,1,0:T(1,128)}, u32[]{:S(2)}) copy-start(s32[1,1,1024]{2,1,0:T(1,128)} %param.13) | copy-start | bytes 12292
  3.4 35.2 %collective-permute-start.4 = (f32[10496]{0:T(1024)S(1)}, f32[10496]{0:T(1024)S(1)}, u32[]{:S(2)}, u32[]{:S(2)}) collective-permute-start(f32[10496]{0:T(1024)S(1)} %pad_maximum_fusion.3), channel_id=1, source_target_pairs={{64,0},{128,64},{192,128},{256,192},{320,256},{384,320},{448,384},... | collective-permute-start | bytes 125960 | tf_op jit(solution)/shard_map/ppermute | solution.py:9
  7.0 31.6 %collective-permute-start.1 = (f32[10496]{0:T(1024)S(1)}, f32[10496]{0:T(1024)S(1)}, u32[]{:S(2)}, u32[]{:S(2)}) collective-permute-start(f32[10496]{0:T(1024)S(1)} %pad_maximum_fusion.2), channel_id=1, source_target_pairs={{0,64},{64,128},{128,192},{192,256},{256,320},{320,384},{384,448},... | collective-permute-start | bytes 125960 | tf_op jit(solution)/shard_map/ppermute | solution.py:9
  10.5 17.3 %collective-permute-start.5 = (f32[528]{0:T(1024)S(1)}, f32[528]{0:T(1024)S(1)}, u32[]{:S(2)}, u32[]{:S(2)}) collective-permute-start(f32[528]{0:T(1024)S(1)} %reshape.206), channel_id=1, source_target_pairs={{4,0},{8,4},{12,8},{16,12},{20,16},{24,20},{28,24},{32,28},{36,32}... | collective-permute-start | bytes 6344 | tf_op jit(solution)/shard_map/ppermute | solution.py:9
  21.7 16.3 %collective-permute-start = (f32[528]{0:T(1024)S(1)}, f32[528]{0:T(1024)S(1)}, u32[]{:S(2)}, u32[]{:S(2)}) collective-permute-start(f32[528]{0:T(1024)S(1)} %reshape.196), channel_id=1, source_target_pairs={{0,4},{4,8},{8,12},{12,16},{16,20},{20,24},{24,28},{28,32},{32,36}... | collective-permute-start | bytes 6344 | tf_op jit(solution)/shard_map/ppermute | solution.py:9
  23.6 15.1 %collective-permute-start.2 = (f32[33792]{0:T(1024)S(1)}, f32[33792]{0:T(1024)S(1)}, u32[]{:S(2)}, u32[]{:S(2)}) collective-permute-start(f32[33792]{0:T(1024)S(1)} %get-tuple-element.13), channel_id=1, source_target_pairs={{0,1},{1,2},{2,3},{4,5},{5,6},{6,7},{8,9},{9,10},{10,11},{12,13},{... | collective-permute-start | bytes 405512 | tf_op jit(solution)/shard_map/ppermute | solution.py:9
  27.8 11.0 %collective-permute-start.3 = (f32[33792]{0:T(1024)S(1)}, f32[33792]{0:T(1024)S(1)}, u32[]{:S(2)}, u32[]{:S(2)}) collective-permute-start(f32[33792]{0:T(1024)S(1)} %get-tuple-element.14), channel_id=1, source_target_pairs={{1,0},{2,1},{3,2},{5,4},{6,5},{7,6},{9,8},{10,9},{11,10},{13,12},{... | collective-permute-start | bytes 405512 | tf_op jit(solution)/shard_map/ppermute | solution.py:9
  40.0 0.7 copy-start.7
  40.1 0.7 copy-start.8
  40.6 0.7 copy-start.4
  41.0 5.5 %copy-start.1 = (f32[16,2,2,8,128]{4,3,2,1,0:T(8,128)}, f32[16,2,2,8,128]{4,3,2,1,0:T(8,128)S(1)}, u32[]{:S(2)}) copy-start(f32[16,2,2,8,128]{4,3,2,1,0:T(8,128)S(1)} %fusion.12) | copy-start | bytes 786436
  41.6 28.2 %copy-start = (f32[16,4,128]{2,1,0:T(4,128)S(1)}, f32[16,4,128]{2,1,0:T(4,128)}, u32[]{:S(2)}) copy-start(f32[16,4,128]{2,1,0:T(4,128)} %param.14) | copy-start | bytes 98308
  41.6 63.4 %copy-start.6 = (f32[4,128]{1,0:T(4,128)S(1)}, f32[4,128]{1,0:T(4,128)}, u32[]{:S(2)}) copy-start(f32[4,128]{1,0:T(4,128)} %param.15) | copy-start | bytes 6148
  46.4 79.6 %all-to-all-start = ((f32[64,1,544]{2,1,0:T(1,128)}), f32[64,1,544]{2,1,0:T(1,128)S(1)}, u32[]{:S(2)}, u32[]{:S(2)}) async-start(f32[64,1,544]{2,1,0:T(1,128)} %reshape.259), calls=%async_computation | async-start | bytes 327680 | tf_op jit(solution)/shard_map/all_to_all | solution.py:142
  70.0 18.3 %collective-permute-start.6 = (f32[64]{0:T(128)S(1)}, f32[64]{0:T(128)S(1)}, u32[]{:S(2)}, u32[]{:S(2)}) collective-permute-start(f32[64]{0:T(128)S(1)} %reshape.212), channel_id=1, source_target_pairs={{1,0},{2,1},{3,2},{4,3},{5,4},{6,5},{7,6},{8,7},{9,8},{10,9},{11,1... | collective-permute-start | bytes 776 | tf_op jit(solution)/shard_map/ppermute | solution.py:9
  86.4 18.4 %collective-permute-start.7 = (f32[64]{0:T(128)S(1)}, f32[64]{0:T(128)S(1)}, u32[]{:S(2)}, u32[]{:S(2)}) collective-permute-start(f32[64]{0:T(128)S(1)} %reshape.214), channel_id=1, source_target_pairs={{0,1},{1,2},{2,3},{3,4},{4,5},{5,6},{6,7},{7,8},{8,9},{9,10},{10,1... | collective-permute-start | bytes 776 | tf_op jit(solution)/shard_map/ppermute | solution.py:9
  105.4 10.3 %collective-permute-start.10 = (f32[64]{0:T(128)S(1)}, f32[64]{0:T(128)S(1)}, u32[]{:S(2)}, u32[]{:S(2)}) collective-permute-start(f32[64]{0:T(128)S(1)} %reshape.220), channel_id=1, source_target_pairs={{1,0},{2,1},{3,2},{4,3},{5,4},{6,5},{7,6},{8,7},{9,8},{10,9},{11,1... | collective-permute-start | bytes 776 | tf_op jit(solution)/shard_map/ppermute | solution.py:9
  107.4 18.4 %collective-permute-start.11 = (f32[64]{0:T(128)S(1)}, f32[64]{0:T(128)S(1)}, u32[]{:S(2)}, u32[]{:S(2)}) collective-permute-start(f32[64]{0:T(128)S(1)} %reshape.222), channel_id=1, source_target_pairs={{0,1},{1,2},{2,3},{3,4},{4,5},{5,6},{6,7},{7,8},{8,9},{9,10},{10,1... | collective-permute-start | bytes 776 | tf_op jit(solution)/shard_map/ppermute | solution.py:9
  111.4 20.9 %collective-permute-start.8 = (f32[2048]{0:T(1024)S(1)}, f32[2048]{0:T(1024)S(1)}, u32[]{:S(2)}, u32[]{:S(2)}) collective-permute-start(f32[2048]{0:T(1024)S(1)} %bitcast.82), channel_id=1, source_target_pairs={{64,0},{128,64},{192,128},{256,192},{320,256},{384,320},{448,384},... | collective-permute-start | bytes 24584 | tf_op jit(solution)/shard_map/ppermute | solution.py:9
  113.3 18.9 %collective-permute-start.9 = (f32[2048]{0:T(1024)S(1)}, f32[2048]{0:T(1024)S(1)}, u32[]{:S(2)}, u32[]{:S(2)}) collective-permute-start(f32[2048]{0:T(1024)S(1)} %bitcast.81), channel_id=1, source_target_pairs={{0,64},{64,128},{128,192},{192,256},{256,320},{320,384},{384,448},... | collective-permute-start | bytes 24584 | tf_op jit(solution)/shard_map/ppermute | solution.py:9

commit v6 on v5

--- a/solution.py
+++ b/solution.py
@@ -89,16 +89,14 @@
     fwd_x, bwd_x = steps(count_x)
     fwd_c, bwd_c = steps(count_col)
     fwd_y, bwd_y = steps(lax.axis_size("mapy"))
-    d = directions
+    d, k = directions, stiffness
     fwd_l, bwd_l = steps(count_layer)
-    x_lo = send([stacked[:, :, -1:], d[:, -1:]], "mapx", fwd_x)
-    x_hi = send([stacked[:, :, :1], d[:, :1]], "mapx", bwd_x)
+    x_lo = send([stacked[:, :, -1:], d[:, -2:], k[-1:]], "mapx", fwd_x)
+    x_hi = send([stacked[:, :, :1], d[:, :2], k[:1]], "mapx", bwd_x)
     (z_lo,) = send([stacked[:, -1:]], "layer", fwd_l)
     (z_hi,) = send([stacked[:, :1]], "layer", bwd_l)
     (y_lo,) = send([stacked[..., -1:]], "mapy", fwd_y)
     (y_hi,) = send([stacked[..., :1]], "mapy", bwd_y)
-    (c_lo,) = send([d[:, :, -1:]], column, fwd_c)
-    (c_hi,) = send([d[:, :, :1]], column, bwd_c)
 
     extended = jnp.concatenate([z_lo, stacked, z_hi], axis=1)
     extended = jnp.concatenate([pad_dims(x_lo[0], (1,)), extended, pad_dims(x_hi[0], (1,))], axis=2)
@@ -106,16 +104,9 @@
     padded = extended[:-1].reshape(probes, 2, depth + 2, rows + 2, cols + 2)
     image = stencil(padded, extended[-1])
 
-    wide = jnp.concatenate([x_lo[1], d, x_hi[1]], axis=1)
-    wide = jnp.concatenate([pad_dims(c_lo, (1,)), wide, pad_dims(c_hi, (1,))], axis=2)
-    inner = stiffness[None] * laplace(wide)
-    (i_up,) = send([inner[:, -1:]], "mapx", fwd_x)
-    (i_down,) = send([inner[:, :1]], "mapx", bwd_x)
-    (i_left,) = send([inner[:, :, -1:]], column, fwd_c)
-    (i_right,) = send([inner[:, :, :1]], column, bwd_c)
-    ring = jnp.concatenate([i_up, inner, i_down], axis=1)
-    ring = jnp.concatenate([pad_dims(i_left, (1,)), ring, pad_dims(i_right, (1,))], axis=2)
-    prior = laplace(ring)
+    tall = jnp.concatenate([x_lo[1], d, x_hi[1]], axis=1)
+    tall_k = jnp.concatenate([x_lo[2], k, x_hi[2]], axis=0)
+    strip_parts = [(tall[:, :, -2:], tall_k[:, -1:]), (tall[:, :, :2], tall_k[:, :1])]
 
     face_count = rows * cols
     face_rows = (friction * (image[:, 0, 0] + image[:, 1, 0])).reshape(probes, face_count).T
@@ -139,14 +130,40 @@
     packed = jnp.zeros((total_slots, probes + 1), jnp.float32).at[position].set(
         rows_out, mode="drop"
     )
-    got = lax.all_to_all(
-        packed.reshape(owner_count, capacity, probes + 1),
-        column,
-        split_axis=0,
-        concat_axis=0,
-        tiled=True,
-    ).reshape(count_y, count_layer, capacity, probes + 1)[:, 0]
+    me = lax.axis_index(column)
+    strips = [jnp.concatenate([a.reshape(-1), b.reshape(-1)]) for a, b in strip_parts]
+    strip_size = strips[0].size
+    extra_rows = -(-strip_size // (probes + 1))
+    strips = [
+        jnp.pad(x, (0, extra_rows * (probes + 1) - strip_size)).reshape(extra_rows, probes + 1)
+        for x in strips
+    ]
+    dest = lax.broadcasted_iota(jnp.int32, (owner_count, 1, 1), 0)
+    extra = jnp.where(dest == me + 1, strips[0][None], 0.0) + jnp.where(
+        dest == me - 1, strips[1][None], 0.0
+    )
+    packed = jnp.concatenate([packed.reshape(owner_count, capacity, probes + 1), extra], axis=1)
+    received = lax.all_to_all(packed, column, split_axis=0, concat_axis=0, tiled=True)
+    got = received[:, :capacity].reshape(count_y, count_layer, capacity, probes + 1)[:, 0]
     got = got.reshape(-1, probes + 1)
+    side_lo = lax.dynamic_index_in_dim(received, jnp.maximum(me - 1, 0), 0, keepdims=False)
+    side_hi = lax.dynamic_index_in_dim(
+        received, jnp.minimum(me + 1, owner_count - 1), 0, keepdims=False
+    )
+    side_lo = jnp.where(me > 0, side_lo[capacity:], 0.0).reshape(-1)[:strip_size]
+    side_hi = jnp.where(me < owner_count - 1, side_hi[capacity:], 0.0).reshape(-1)[:strip_size]
+    wide_shape, k_shape = strip_parts[0][0].shape, strip_parts[0][1].shape
+    wide_size = strip_parts[0][0].size
+    wide = jnp.concatenate(
+        [side_lo[:wide_size].reshape(wide_shape), tall, side_hi[:wide_size].reshape(wide_shape)],
+        axis=2,
+    )
+    ring = jnp.concatenate(
+        [side_lo[wide_size:].reshape(k_shape), tall_k, side_hi[wide_size:].reshape(k_shape)],
+        axis=1,
+    )
+    inner = ring[None] * laplace(wide)
+    prior = laplace(inner)
     map_rows = directions.shape[1]
     map_cols = directions.shape[2]
     summed = jax.ops.segment_sum(

time: 134 us -> 131 us (0.978)
  the two profiles are of different devices: /device:TPU:896 before, /device:TPU:32 now
where the time goes in v6:
time: 131 us; the launch traced here: 130 us
  starting transfers between devices  58.3 us (45%)
  waiting for transfers between devices  46.3 us (35%)
  local copies, waits for them, and re-layouts  14.2 us (11%)
  other arithmetic  9.54 us (7%)
    all_to_all x1, starting transfers between devices, shards(): lax.all_to_all(packed, column, split_axis=0, concat_axis=0, tiled=True)  43.3 us
    all_to_all x1, waiting for transfers between devices, shards(): lax.all_to_all(packed, column, split_axis=0, concat_axis=0, tiled=True)  42.1 us
    ppermute x6, starting transfers between devices, send(): got = lax.ppermute(flat, axis, pairs)  14.9 us
    ppermute x6, waiting for transfers between devices, send(): got = lax.ppermute(flat, axis, pairs)  4.2 us
    unnamed x23, local copies, waits for them, and re-layouts  3.43 us
    scatter x1, local copies, waits for them, and re-layouts, shards(): jnp.zeros((total_slots, probes + 1), jnp.float32).at[position]  3.34 us
    scatter-add x1, other arithmetic, shards(): jax.ops.segment_sum(got[:, :probes], got[:, probes].astype(jnp.int32), nu...  3.23 us
  transfers between devices with their start and end apart: 7, of which 2 were waited for; matrix products, arithmetic and copies ran while one was open for 4% of the time, Pallas kernels for 0%

profile of v6, /device:TPU:32, one launch (start us, length us, event | category | flops | bytes accessed | tf_op | source)
XLA Modules:
  0.0 130.2 jit_solution(6135540233734362132)
XLA Ops:
  0.7 1.0 copy.106
  1.6 0.8 fusion.35
  2.5 0.9 fusion.40
  3.4 0.8 slice_bitcast_fusion.6
  4.2 1.9 %collective-permute-start.4 = (f32[12672]{0:T(1024)S(1)}, f32[12672]{0:T(1024)S(1)}, u32[]{:S(2)}, u32[]{:S(2)}) collective-permute-start(f32[12672]{0:T(1024)S(1)} %pad_maximum_fusion.12), channel_id=1, source_target_pairs={{64,0},{128,64},{192,128},{256,192},{320,256},{384,320},{448,384},... | collective-permute-start | bytes 152072 | tf_op jit(solution)/shard_map/ppermute | solution.py:9
  6.2 2.4 %collective-permute-start.1 = (f32[12672]{0:T(1024)S(1)}, f32[12672]{0:T(1024)S(1)}, u32[]{:S(2)}, u32[]{:S(2)}) collective-permute-start(f32[12672]{0:T(1024)S(1)} %pad_maximum_fusion.11), channel_id=1, source_target_pairs={{0,64},{64,128},{128,192},{192,256},{256,320},{320,384},{384,448},... | collective-permute-start | bytes 152072 | tf_op jit(solution)/shard_map/ppermute | solution.py:9
  8.6 0.9 fusion.10
  9.5 0.5 copy.112
  10.1 1.3 collective-permute-start.5
  11.4 0.5 copy.107
  12.0 4.5 %collective-permute-start = (f32[528]{0:T(1024)S(1)}, f32[528]{0:T(1024)S(1)}, u32[]{:S(2)}, u32[]{:S(2)}) collective-permute-start(f32[528]{0:T(1024)S(1)} %reshape.202), channel_id=1, source_target_pairs={{0,4},{4,8},{8,12},{12,16},{16,20},{20,24},{24,28},{28,32},{32,36}... | collective-permute-start | bytes 6344 | tf_op jit(solution)/shard_map/ppermute | solution.py:9
  16.5 3.5 %collective-permute-start.2 = (f32[33792]{0:T(1024)S(1)}, f32[33792]{0:T(1024)S(1)}, u32[]{:S(2)}, u32[]{:S(2)}) collective-permute-start(f32[33792]{0:T(1024)S(1)} %get-tuple-element.13), channel_id=1, source_target_pairs={{0,1},{1,2},{2,3},{4,5},{5,6},{6,7},{8,9},{9,10},{10,11},{12,13},{... | collective-permute-start | bytes 405512 | tf_op jit(solution)/shard_map/ppermute | solution.py:9
  20.1 0.6 fusion.7
  20.7 1.3 collective-permute-start.3
  22.2 0.5 copy.113
  22.7 0.5 copy.142
  24.6 4.2 %collective-permute-done.3 = f32[33792]{0:T(1024)S(1)} collective-permute-done((f32[33792]{0:T(1024)S(1)}, f32[33792]{0:T(1024)S(1)}, u32[]{:S(2)}, u32[]{:S(2)}) %collective-permute-start.3) | collective-permute-done | bytes 135200 | tf_op jit(solution)/shard_map/ppermute | solution.py:9
  28.8 1.1 select_maximum_fusion
  30.2 0.5 fusion.38
  31.0 0.3 copy-done.5
  31.6 3.3 %scatter_custom_fusion = f32[2048,17]{1,0:T(8,128)S(1)} fusion(s32[1024]{0:T(1024)S(1)} %bitcast.98, f32[1024,17]{1,0:T(8,128)S(1)} %copy.122, f32[]{:T(128)} %constant.17.clone.1), kind=kCustom, calls=%fused_computation.27 | custom fusion | bytes 139268 | tf_op jit(solution)/shard_map/scatter | solution.py:130
  35.0 0.5 copy.125
  35.4 0.3 fusion.41
  35.7 1.2 reshape.254
  37.0 43.3 %all-to-all-start = ((f32[64,1,816]{2,1,0:T(1,128)}), f32[64,1,816]{2,1,0:T(1,128)S(1)}, u32[]{:S(2)}, u32[]{:S(2)}) async-start(f32[64,1,816]{2,1,0:T(1,128)} %reshape.254), calls=%async_computation | async-start | bytes 458752 | tf_op jit(solution)/shard_map/all_to_all | solution.py:146
  80.4 42.1 %all-to-all-done = f32[64,1,816]{2,1,0:T(1,128)S(1)} async-done(((f32[64,1,816]{2,1,0:T(1,128)}), f32[64,1,816]{2,1,0:T(1,128)S(1)}, u32[]{:S(2)}, u32[]{:S(2)}) %all-to-all-start) | async-done | bytes 208928 | tf_op jit(solution)/shard_map/all_to_all | solution.py:146
  122.5 0.5 broadcast.147
  123.0 1.2 reduce.4
  124.2 0.2 reshape.255
  125.6 3.2 %scatter_custom_fusion.1 = f32[512,16]{1,0:T(8,128)S(1)} fusion(s32[512]{0:T(512)S(1)} %bitcast.99, f32[512,16]{1,0:T(8,128)S(1)} %copy.127, f32[]{:T(128)} %constant.17.clone.1), kind=kCustom, calls=%fused_computation.72 | custom fusion | flops 8192 | bytes 32772 | tf_op jit(solution)/shard_map/scatter-add | solution.py:169
  129.2 0.3 fusion.28
  129.5 0.8 fusion.37
  (90 shorter events, 4.2 us)
Async XLA Ops:
  0.6 15.9 %copy-start.2 = (f32[2,8,128]{2,1,0:T(8,128)S(1)}, f32[2,8,128]{2,1,0:T(8,128)}, u32[]{:S(2)}) copy-start(f32[2,8,128]{2,1,0:T(8,128)} %param.10) | copy-start | bytes 24580
  0.6 19.4 %copy-start.6 = (s32[1,1,1024]{2,1,0:T(1,128)S(1)}, s32[1,1,1024]{2,1,0:T(1,128)}, u32[]{:S(2)}) copy-start(s32[1,1,1024]{2,1,0:T(1,128)} %param.13) | copy-start | bytes 12292
  0.7 19.4 %copy-start.4 = (s32[1,1,1024,1]{2,3,1,0:T(1,128)S(1)}, s32[1,1,1024,1]{2,3,1,0:T(1,128)}, u32[]{:S(2)}) copy-start(s32[1,1,1024,1]{2,3,1,0:T(1,128)} %param.12) | copy-start | bytes 12292
  4.2 19.0 %collective-permute-start.4 = (f32[12672]{0:T(1024)S(1)}, f32[12672]{0:T(1024)S(1)}, u32[]{:S(2)}, u32[]{:S(2)}) collective-permute-start(f32[12672]{0:T(1024)S(1)} %pad_maximum_fusion.12), channel_id=1, source_target_pairs={{64,0},{128,64},{192,128},{256,192},{320,256},{384,320},{448,384},... | collective-permute-start | bytes 152072 | tf_op jit(solution)/shard_map/ppermute | solution.py:9
  6.2 17.1 %collective-permute-start.1 = (f32[12672]{0:T(1024)S(1)}, f32[12672]{0:T(1024)S(1)}, u32[]{:S(2)}, u32[]{:S(2)}) collective-permute-start(f32[12672]{0:T(1024)S(1)} %pad_maximum_fusion.11), channel_id=1, source_target_pairs={{0,64},{64,128},{128,192},{192,256},{256,320},{320,384},{384,448},... | collective-permute-start | bytes 152072 | tf_op jit(solution)/shard_map/ppermute | solution.py:9
  9.5 13.9 %copy-start = (f32[16,4,128]{2,1,0:T(4,128)S(1)}, f32[16,4,128]{2,1,0:T(4,128)}, u32[]{:S(2)}) copy-start(f32[16,4,128]{2,1,0:T(4,128)} %param.14) | copy-start | bytes 98308
  10.1 10.7 %collective-permute-start.5 = (f32[528]{0:T(1024)S(1)}, f32[528]{0:T(1024)S(1)}, u32[]{:S(2)}, u32[]{:S(2)}) collective-permute-start(f32[528]{0:T(1024)S(1)} %reshape.216), channel_id=1, source_target_pairs={{4,0},{8,4},{12,8},{16,12},{20,16},{24,20},{28,24},{32,28},{36,32}... | collective-permute-start | bytes 6344 | tf_op jit(solution)/shard_map/ppermute | solution.py:9
  11.4 12.5 %copy-start.3 = (f32[4,128]{1,0:T(4,128)S(1)}, f32[4,128]{1,0:T(4,128)}, u32[]{:S(2)}) copy-start(f32[4,128]{1,0:T(4,128)} %param.15) | copy-start | bytes 6148
  12.0 10.7 %collective-permute-start = (f32[528]{0:T(1024)S(1)}, f32[528]{0:T(1024)S(1)}, u32[]{:S(2)}, u32[]{:S(2)}) collective-permute-start(f32[528]{0:T(1024)S(1)} %reshape.202), channel_id=1, source_target_pairs={{0,4},{4,8},{8,12},{12,16},{16,20},{20,24},{24,28},{28,32},{32,36}... | collective-permute-start | bytes 6344 | tf_op jit(solution)/shard_map/ppermute | solution.py:9
  16.5 8.1 %collective-permute-start.2 = (f32[33792]{0:T(1024)S(1)}, f32[33792]{0:T(1024)S(1)}, u32[]{:S(2)}, u32[]{:S(2)}) collective-permute-start(f32[33792]{0:T(1024)S(1)} %get-tuple-element.13), channel_id=1, source_target_pairs={{0,1},{1,2},{2,3},{4,5},{5,6},{6,7},{8,9},{9,10},{10,11},{12,13},{... | collective-permute-start | bytes 405512 | tf_op jit(solution)/shard_map/ppermute | solution.py:9
  20.7 8.1 %collective-permute-start.3 = (f32[33792]{0:T(1024)S(1)}, f32[33792]{0:T(1024)S(1)}, u32[]{:S(2)}, u32[]{:S(2)}) collective-permute-start(f32[33792]{0:T(1024)S(1)} %get-tuple-element.14), channel_id=1, source_target_pairs={{1,0},{2,1},{3,2},{5,4},{6,5},{7,6},{9,8},{10,9},{11,10},{13,12},{... | collective-permute-start | bytes 405512 | tf_op jit(solution)/shard_map/ppermute | solution.py:9
  30.1 0.7 copy-start.7
  30.1 0.7 copy-start.8
  30.7 0.7 copy-start.5
  31.0 4.7 %copy-start.1 = (f32[16,2,2,8,128]{4,3,2,1,0:T(8,128)}, f32[16,2,2,8,128]{4,3,2,1,0:T(8,128)S(1)}, u32[]{:S(2)}) copy-start(f32[16,2,2,8,128]{4,3,2,1,0:T(8,128)S(1)} %fusion.12) | copy-start | bytes 786436
  37.0 85.5 %all-to-all-start = ((f32[64,1,816]{2,1,0:T(1,128)}), f32[64,1,816]{2,1,0:T(1,128)S(1)}, u32[]{:S(2)}, u32[]{:S(2)}) async-start(f32[64,1,816]{2,1,0:T(1,128)} %reshape.254), calls=%async_computation | async-start | bytes 458752 | tf_op jit(solution)/shard_map/all_to_all | solution.py:146

commit v7 on v6

--- a/solution.py
+++ b/solution.py
@@ -90,6 +90,7 @@
     fwd_c, bwd_c = steps(count_col)
     fwd_y, bwd_y = steps(lax.axis_size("mapy"))
     d, k = directions, stiffness
+    rmap = d.shape[1]
     fwd_l, bwd_l = steps(count_layer)
     x_lo = send([stacked[:, :, -1:], d[:, -2:], k[-1:]], "mapx", fwd_x)
     x_hi = send([stacked[:, :, :1], d[:, :2], k[:1]], "mapx", bwd_x)
@@ -106,7 +107,10 @@
 
     tall = jnp.concatenate([x_lo[1], d, x_hi[1]], axis=1)
     tall_k = jnp.concatenate([x_lo[2], k, x_hi[2]], axis=0)
-    strip_parts = [(tall[:, :, -2:], tall_k[:, -1:]), (tall[:, :, :2], tall_k[:, :1])]
+    strip_parts = [
+        (tall[:, 1 : rmap + 3, -1], tall[:, 2 : rmap + 2, -2], tall_k[1 : rmap + 1, -1]),
+        (tall[:, 1 : rmap + 3, 0], tall[:, 2 : rmap + 2, 1], tall_k[1 : rmap + 1, 0]),
+    ]
 
     face_count = rows * cols
     face_rows = (friction * (image[:, 0, 0] + image[:, 1, 0])).reshape(probes, face_count).T
@@ -127,11 +131,12 @@
     position = targets * capacity + rank
     total_slots = owner_count * capacity
     rows_out = jnp.concatenate([face_rows, local_cells[:, None]], axis=1)
-    packed = jnp.zeros((total_slots, probes + 1), jnp.float32).at[position].set(
-        rows_out, mode="drop"
-    )
+    chooser = (
+        lax.broadcasted_iota(jnp.int32, (total_slots, face_count), 0) == position[None, :]
+    ).astype(jnp.float32)
+    packed = jnp.dot(chooser, rows_out, precision=lax.Precision.HIGHEST)
     me = lax.axis_index(column)
-    strips = [jnp.concatenate([a.reshape(-1), b.reshape(-1)]) for a, b in strip_parts]
+    strips = [jnp.concatenate([p.reshape(-1) for p in parts]) for parts in strip_parts]
     strip_size = strips[0].size
     extra_rows = -(-strip_size // (probes + 1))
     strips = [
@@ -152,26 +157,31 @@
     )
     side_lo = jnp.where(me > 0, side_lo[capacity:], 0.0).reshape(-1)[:strip_size]
     side_hi = jnp.where(me < owner_count - 1, side_hi[capacity:], 0.0).reshape(-1)[:strip_size]
-    wide_shape, k_shape = strip_parts[0][0].shape, strip_parts[0][1].shape
-    wide_size = strip_parts[0][0].size
-    wide = jnp.concatenate(
-        [side_lo[:wide_size].reshape(wide_shape), tall, side_hi[:wide_size].reshape(wide_shape)],
-        axis=2,
-    )
-    ring = jnp.concatenate(
-        [side_lo[wide_size:].reshape(k_shape), tall_k, side_hi[wide_size:].reshape(k_shape)],
-        axis=1,
-    )
+    sizes = [p.size for p in strip_parts[0]]
+
+    def unpack(side):
+        near = side[: sizes[0]].reshape(probes, rmap + 2)
+        far = side[sizes[0] : sizes[0] + sizes[1]].reshape(probes, rmap)
+        kk = side[sizes[0] + sizes[1] :]
+        near = jnp.pad(near, ((0, 0), (1, 1)))[:, :, None]
+        far = jnp.pad(far, ((0, 0), (2, 2)))[:, :, None]
+        kk = jnp.pad(kk, (1, 1))[:, None]
+        return near, far, kk
+
+    lo_near, lo_far, lo_k = unpack(side_lo)
+    hi_near, hi_far, hi_k = unpack(side_hi)
+    wide = jnp.concatenate([lo_far, lo_near, tall, hi_near, hi_far], axis=2)
+    ring = jnp.concatenate([lo_k, tall_k, hi_k], axis=1)
     inner = ring[None] * laplace(wide)
     prior = laplace(inner)
     map_rows = directions.shape[1]
     map_cols = directions.shape[2]
-    summed = jax.ops.segment_sum(
-        got[:, :probes],
-        got[:, probes].astype(jnp.int32),
-        num_segments=map_rows * map_cols,
-    )
-    data = summed.T.reshape(probes, map_rows, map_cols)
+    places = got[:, probes].astype(jnp.int32)
+    spots = (
+        places[:, None] == lax.broadcasted_iota(jnp.int32, (1, map_rows * map_cols), 1)
+    ).astype(jnp.float32)
+    summed = jnp.dot(got[:, :probes].T, spots, precision=lax.Precision.HIGHEST)
+    data = summed.reshape(probes, map_rows, map_cols)
     hessian = data + prior + 0.1 * directions
     return (image, hessian)
 

time: 131 us -> 127 us (0.969)
  matrix products: 0.59 us -> 4.85 us
  other arithmetic: 9.54 us -> 6.1 us
  waiting for transfers between devices: 46.3 us -> 43.7 us
  local copies, waits for them, and re-layouts: 14.2 us -> 12.4 us
    dot_general x0 -> x2, matrix products: none -> 4.25 us  [the longest x1 3.77 us: shards(): packed = jnp.dot(chooser, rows_out, precision=lax.Precision.HIGHEST)]
    scatter x1 -> x0, local copies, waits for them, and re-layouts: 3.34 us -> none  [shards(): jnp.zeros((total_slots, probes + 1), jnp.float32).at[position]]
    scatter-add x1 -> x0, other arithmetic: 3.23 us -> none  [shards(): jax.ops.segment_sum(got[:, :probes], got[:, probes].astype(jnp.int32), nu...]
    all_to_all x1, waiting for transfers between devices: 42.1 us -> 39.2 us  [shards(): lax.all_to_all(packed, column, split_axis=0, concat_axis=0, tiled=True)]
    unnamed x23 -> x26, local copies, waits for them, and re-layouts: 3.43 us -> 3.59 us
where the time goes in v7:
time: 127 us
  starting transfers between devices  58.3 us (46%)
  waiting for transfers between devices  43.7 us (34%)
  local copies, waits for them, and re-layouts  12.4 us (10%)
  other arithmetic  6.1 us (5%)
  matrix products  4.85 us (4%)
    all_to_all x1, starting transfers between devices, shards(): lax.all_to_all(packed, column, split_axis=0, concat_axis=0, tiled=True)  43.3 us
    all_to_all x1, waiting for transfers between devices, shards(): lax.all_to_all(packed, column, split_axis=0, concat_axis=0, tiled=True)  39.2 us
    ppermute x6, starting transfers between devices, send(): got = lax.ppermute(flat, axis, pairs)  14.9 us
    ppermute x6, waiting for transfers between devices, send(): got = lax.ppermute(flat, axis, pairs)  4.45 us
    dot_general x1, matrix products, shards(): packed = jnp.dot(chooser, rows_out, precision=lax.Precision.HIGHEST)  3.77 us
    unnamed x26, local copies, waits for them, and re-layouts  3.59 us
  transfers between devices with their start and end apart: 7, of which 2 were waited for; matrix products, arithmetic and copies ran while one was open for 4% of the time, Pallas kernels for 0%

profile of v7, /device:TPU:32, one launch (start us, length us, event | category | flops | bytes accessed | tf_op | source)
XLA Modules:
  0.0 126.5 jit_solution(14658940090456789802)
XLA Ops:
  0.7 1.0 copy.113
  1.7 0.8 fusion.39
  2.6 0.9 fusion.45
  3.4 0.8 slice_bitcast_fusion.4
  4.2 1.9 %collective-permute-start.4 = (f32[12672]{0:T(1024)S(1)}, f32[12672]{0:T(1024)S(1)}, u32[]{:S(2)}, u32[]{:S(2)}) collective-permute-start(f32[12672]{0:T(1024)S(1)} %pad_maximum_fusion.12), channel_id=1, source_target_pairs={{64,0},{128,64},{192,128},{256,192},{320,256},{384,320},{448,384},... | collective-permute-start | bytes 152072 | tf_op jit(solution)/shard_map/ppermute | solution.py:9
  6.2 2.4 %collective-permute-start.1 = (f32[12672]{0:T(1024)S(1)}, f32[12672]{0:T(1024)S(1)}, u32[]{:S(2)}, u32[]{:S(2)}) collective-permute-start(f32[12672]{0:T(1024)S(1)} %pad_maximum_fusion.11), channel_id=1, source_target_pairs={{0,64},{64,128},{128,192},{192,256},{256,320},{320,384},{384,448},... | collective-permute-start | bytes 152072 | tf_op jit(solution)/shard_map/ppermute | solution.py:9
  8.6 0.9 fusion.12
  9.5 0.5 copy.119
  10.1 1.3 %collective-permute-start.5 = (f32[528]{0:T(1024)S(1)}, f32[528]{0:T(1024)S(1)}, u32[]{:S(2)}, u32[]{:S(2)}) collective-permute-start(f32[528]{0:T(1024)S(1)} %reshape.177), channel_id=1, source_target_pairs={{4,0},{8,4},{12,8},{16,12},{20,16},{24,20},{28,24},{32,28},{36,32}... | collective-permute-start | bytes 6344 | tf_op jit(solution)/shard_map/ppermute | solution.py:9
  11.4 0.5 copy.114
  12.0 4.5 %collective-permute-start = (f32[528]{0:T(1024)S(1)}, f32[528]{0:T(1024)S(1)}, u32[]{:S(2)}, u32[]{:S(2)}) collective-permute-start(f32[528]{0:T(1024)S(1)} %reshape.163), channel_id=1, source_target_pairs={{0,4},{4,8},{8,12},{12,16},{16,20},{20,24},{24,28},{28,32},{32,36}... | collective-permute-start | bytes 6344 | tf_op jit(solution)/shard_map/ppermute | solution.py:9
  16.6 3.5 %collective-permute-start.2 = (f32[33792]{0:T(1024)S(1)}, f32[33792]{0:T(1024)S(1)}, u32[]{:S(2)}, u32[]{:S(2)}) collective-permute-start(f32[33792]{0:T(1024)S(1)} %get-tuple-element.17), channel_id=1, source_target_pairs={{0,1},{1,2},{2,3},{4,5},{5,6},{6,7},{8,9},{9,10},{10,11},{12,13},{... | collective-permute-start | bytes 405512 | tf_op jit(solution)/shard_map/ppermute | solution.py:9
  20.5 0.6 fusion.9
  21.3 1.3 %collective-permute-start.3 = (f32[33792]{0:T(1024)S(1)}, f32[33792]{0:T(1024)S(1)}, u32[]{:S(2)}, u32[]{:S(2)}) collective-permute-start(f32[33792]{0:T(1024)S(1)} %get-tuple-element.18), channel_id=1, source_target_pairs={{1,0},{2,1},{3,2},{5,4},{6,5},{7,6},{9,8},{10,9},{11,10},{13,12},{... | collective-permute-start | bytes 405512 | tf_op jit(solution)/shard_map/ppermute | solution.py:9
  22.7 0.5 copy.120
  23.3 0.5 copy.159
  25.0 4.4 %collective-permute-done.3 = f32[33792]{0:T(1024)S(1)} collective-permute-done((f32[33792]{0:T(1024)S(1)}, f32[33792]{0:T(1024)S(1)}, u32[]{:S(2)}, u32[]{:S(2)}) %collective-permute-start.3) | collective-permute-done | bytes 135200 | tf_op jit(solution)/shard_map/ppermute | solution.py:9
  29.4 1.1 select_maximum_fusion
  30.8 0.5 fusion.44
  31.6 0.3 copy-done.5
  32.0 3.8 %fusion = f32[2048,17]{0,1:T(8,128)S(1)} fusion(s32[1024]{0:T(1024)S(1)} %convert_add_fusion, f32[1024,1]{0,1:T(1,128)S(1)} %convert_bitcast_fusion, f32[1024,16]{0,1:T(8,128)S(1)} %fusion.37), kind=kOutput, calls=%fused_computation.1 | convolution fusion | flops 429933568 | bytes 212992 | tf_op jit(solution)/shard_map/dot_general | solution.py:137
  35.9 0.2 pad_maximum_fusion
  36.1 0.3 copy.209
  36.5 1.2 reshape.198
  37.7 43.3 %all-to-all-start = ((f32[64,1,714]{2,1,0:T(1,128)}), f32[64,1,714]{2,1,0:T(1,128)S(1)}, u32[]{:S(2)}, u32[]{:S(2)}) async-start(f32[64,1,714]{2,1,0:T(1,128)} %reshape.198), calls=%async_computation | async-start | bytes 393216 | tf_op jit(solution)/shard_map/all_to_all | solution.py:151
  81.1 39.2 %all-to-all-done = f32[64,1,714]{2,1,0:T(1,128)S(1)} async-done(((f32[64,1,714]{2,1,0:T(1,128)}), f32[64,1,714]{2,1,0:T(1,128)S(1)}, u32[]{:S(2)}, u32[]{:S(2)}) %all-to-all-start) | async-done | bytes 182816 | tf_op jit(solution)/shard_map/all_to_all | solution.py:151
  120.3 0.5 broadcast.137
  120.8 1.1 reduce.12
  121.9 0.3 reshape.199
  124.7 0.5 fusion.10
  125.5 0.2 fusion.31
  125.8 0.8 fusion.41
  (104 shorter events, 5.9 us)
Async XLA Ops:
  0.6 15.9 %copy-start.2 = (f32[2,8,128]{2,1,0:T(8,128)S(1)}, f32[2,8,128]{2,1,0:T(8,128)}, u32[]{:S(2)}) copy-start(f32[2,8,128]{2,1,0:T(8,128)} %param.10) | copy-start | bytes 24580
  0.6 19.4 %copy-start = (f32[16,4,128]{2,1,0:T(4,128)S(1)}, f32[16,4,128]{2,1,0:T(4,128)}, u32[]{:S(2)}) copy-start(f32[16,4,128]{2,1,0:T(4,128)} %param.14) | copy-start | bytes 98308
  0.7 19.6 %copy-start.3 = (f32[4,128]{1,0:T(4,128)S(1)}, f32[4,128]{1,0:T(4,128)}, u32[]{:S(2)}) copy-start(f32[4,128]{1,0:T(4,128)} %param.15) | copy-start | bytes 6148
  0.7 19.8 %copy-start.4 = (s32[1,1,1024,1]{2,3,1,0:T(1,128)S(1)}, s32[1,1,1024,1]{2,3,1,0:T(1,128)}, u32[]{:S(2)}) copy-start(s32[1,1,1024,1]{2,3,1,0:T(1,128)} %param.12) | copy-start | bytes 12292
  2.5 18.6 %copy-start.6 = (s32[1,1,1024]{2,1,0:T(1,128)S(1)}, s32[1,1,1024]{2,1,0:T(1,128)}, u32[]{:S(2)}) copy-start(s32[1,1,1024]{2,1,0:T(1,128)} %param.13) | copy-start | bytes 12292
  4.2 19.6 %collective-permute-start.4 = (f32[12672]{0:T(1024)S(1)}, f32[12672]{0:T(1024)S(1)}, u32[]{:S(2)}, u32[]{:S(2)}) collective-permute-start(f32[12672]{0:T(1024)S(1)} %pad_maximum_fusion.12), channel_id=1, source_target_pairs={{64,0},{128,64},{192,128},{256,192},{320,256},{384,320},{448,384},... | collective-permute-start | bytes 152072 | tf_op jit(solution)/shard_map/ppermute | solution.py:9
  6.2 17.6 %collective-permute-start.1 = (f32[12672]{0:T(1024)S(1)}, f32[12672]{0:T(1024)S(1)}, u32[]{:S(2)}, u32[]{:S(2)}) collective-permute-start(f32[12672]{0:T(1024)S(1)} %pad_maximum_fusion.11), channel_id=1, source_target_pairs={{0,64},{64,128},{128,192},{192,256},{256,320},{320,384},{384,448},... | collective-permute-start | bytes 152072 | tf_op jit(solution)/shard_map/ppermute | solution.py:9
  10.1 11.2 %collective-permute-start.5 = (f32[528]{0:T(1024)S(1)}, f32[528]{0:T(1024)S(1)}, u32[]{:S(2)}, u32[]{:S(2)}) collective-permute-start(f32[528]{0:T(1024)S(1)} %reshape.177), channel_id=1, source_target_pairs={{4,0},{8,4},{12,8},{16,12},{20,16},{24,20},{28,24},{32,28},{36,32}... | collective-permute-start | bytes 6344 | tf_op jit(solution)/shard_map/ppermute | solution.py:9
  12.0 11.2 %collective-permute-start = (f32[528]{0:T(1024)S(1)}, f32[528]{0:T(1024)S(1)}, u32[]{:S(2)}, u32[]{:S(2)}) collective-permute-start(f32[528]{0:T(1024)S(1)} %reshape.163), channel_id=1, source_target_pairs={{0,4},{4,8},{8,12},{12,16},{16,20},{20,24},{24,28},{28,32},{32,36}... | collective-permute-start | bytes 6344 | tf_op jit(solution)/shard_map/ppermute | solution.py:9
  16.6 8.4 %collective-permute-start.2 = (f32[33792]{0:T(1024)S(1)}, f32[33792]{0:T(1024)S(1)}, u32[]{:S(2)}, u32[]{:S(2)}) collective-permute-start(f32[33792]{0:T(1024)S(1)} %get-tuple-element.17), channel_id=1, source_target_pairs={{0,1},{1,2},{2,3},{4,5},{5,6},{6,7},{8,9},{9,10},{10,11},{12,13},{... | collective-permute-start | bytes 405512 | tf_op jit(solution)/shard_map/ppermute | solution.py:9
  21.3 8.1 %collective-permute-start.3 = (f32[33792]{0:T(1024)S(1)}, f32[33792]{0:T(1024)S(1)}, u32[]{:S(2)}, u32[]{:S(2)}) collective-permute-start(f32[33792]{0:T(1024)S(1)} %get-tuple-element.18), channel_id=1, source_target_pairs={{1,0},{2,1},{3,2},{5,4},{6,5},{7,6},{9,8},{10,9},{11,10},{13,12},{... | collective-permute-start | bytes 405512 | tf_op jit(solution)/shard_map/ppermute | solution.py:9
  30.7 0.7 copy-start.7
  30.7 0.7 copy-start.8
  31.3 0.7 copy-start.5
  31.6 4.3 %copy-start.1 = (f32[16,2,2,8,128]{4,3,2,1,0:T(8,128)}, f32[16,2,2,8,128]{4,3,2,1,0:T(8,128)S(1)}, u32[]{:S(2)}) copy-start(f32[16,2,2,8,128]{4,3,2,1,0:T(8,128)S(1)} %fusion.14) | copy-start | bytes 786436
  37.7 82.6 %all-to-all-start = ((f32[64,1,714]{2,1,0:T(1,128)}), f32[64,1,714]{2,1,0:T(1,128)S(1)}, u32[]{:S(2)}, u32[]{:S(2)}) async-start(f32[64,1,714]{2,1,0:T(1,128)} %reshape.198), calls=%async_computation | async-start | bytes 393216 | tf_op jit(solution)/shard_map/all_to_all | solution.py:151

commit v8 on v7

--- a/solution.py
+++ b/solution.py
@@ -86,6 +86,26 @@
     count_layer = lax.axis_size("layer")
     my_layer = lax.axis_index("layer")
     stacked = jnp.concatenate([velocity.reshape(probes * 2, depth, rows, cols), viscosity[None]], 0)
+    face_count = rows * cols
+    targets = owner.reshape(face_count)
+    local_cells = cell.reshape(face_count).astype(jnp.float32)
+    count_y = lax.axis_size("mapy")
+    owner_count = count_y * count_layer
+    capacity = 2 * face_count // owner_count
+    onehot = (targets[:, None] == jnp.arange(owner_count, dtype=jnp.int32)[None, :]).astype(
+        jnp.bfloat16
+    )
+    order = lax.broadcasted_iota(jnp.int32, (face_count, face_count), 0)
+    earlier = (order > lax.broadcasted_iota(jnp.int32, (face_count, face_count), 1)).astype(
+        jnp.bfloat16
+    )
+    before = jnp.dot(earlier, onehot, preferred_element_type=jnp.float32)
+    rank = jnp.sum(before * onehot.astype(jnp.float32), axis=1).astype(jnp.int32)
+    position = targets * capacity + rank
+    total_slots = owner_count * capacity
+    chooser = (
+        lax.broadcasted_iota(jnp.int32, (total_slots, face_count), 0) == position[None, :]
+    ).astype(jnp.bfloat16)
     fwd_x, bwd_x = steps(count_x)
     fwd_c, bwd_c = steps(count_col)
     fwd_y, bwd_y = steps(lax.axis_size("mapy"))
@@ -98,6 +118,7 @@
     (z_hi,) = send([stacked[:, :1]], "layer", bwd_l)
     (y_lo,) = send([stacked[..., -1:]], "mapy", fwd_y)
     (y_hi,) = send([stacked[..., :1]], "mapy", bwd_y)
+    chooser, y_lo, y_hi = lax.optimization_barrier((chooser, y_lo, y_hi))
 
     extended = jnp.concatenate([z_lo, stacked, z_hi], axis=1)
     extended = jnp.concatenate([pad_dims(x_lo[0], (1,)), extended, pad_dims(x_hi[0], (1,))], axis=2)
@@ -112,29 +133,9 @@
         (tall[:, 1 : rmap + 3, 0], tall[:, 2 : rmap + 2, 1], tall_k[1 : rmap + 1, 0]),
     ]
 
-    face_count = rows * cols
     face_rows = (friction * (image[:, 0, 0] + image[:, 1, 0])).reshape(probes, face_count).T
-    targets = owner.reshape(face_count)
-    local_cells = cell.reshape(face_count).astype(jnp.float32)
-    count_y = lax.axis_size("mapy")
-    owner_count = count_y * count_layer
-    capacity = 2 * face_count // owner_count
-    onehot = (targets[:, None] == jnp.arange(owner_count, dtype=jnp.int32)[None, :]).astype(
-        jnp.bfloat16
-    )
-    order = lax.broadcasted_iota(jnp.int32, (face_count, face_count), 0)
-    earlier = (order > lax.broadcasted_iota(jnp.int32, (face_count, face_count), 1)).astype(
-        jnp.bfloat16
-    )
-    before = jnp.dot(earlier, onehot, preferred_element_type=jnp.float32)
-    rank = jnp.sum(before * onehot.astype(jnp.float32), axis=1).astype(jnp.int32)
-    position = targets * capacity + rank
-    total_slots = owner_count * capacity
     rows_out = jnp.concatenate([face_rows, local_cells[:, None]], axis=1)
-    chooser = (
-        lax.broadcasted_iota(jnp.int32, (total_slots, face_count), 0) == position[None, :]
-    ).astype(jnp.float32)
-    packed = jnp.dot(chooser, rows_out, precision=lax.Precision.HIGHEST)
+    packed = jnp.dot(chooser.astype(jnp.float32), rows_out, precision=lax.Precision.HIGHEST)
     me = lax.axis_index(column)
     strips = [jnp.concatenate([p.reshape(-1) for p in parts]) for parts in strip_parts]
     strip_size = strips[0].size

time: 127 us -> 129 us (1.016)
  other arithmetic: 6.1 us -> 10.1 us
  starting transfers between devices: 58.3 us -> 56.2 us
    convert_element_type x0 -> x1, other arithmetic: none -> 4.03 us  [shards(): chooser = (lax.broadcasted_iota(jnp.int32, (total_slots, face_count), 0)...]
    unnamed x26 -> x29, local copies, waits for them, and re-layouts: 3.59 us -> 5.14 us
  transfers between devices with their start and end apart: 7 -> 7, of which waited for: 2 -> 3; matrix products, arithmetic and copies ran while one was open for 4% -> 7% of each run, Pallas kernels for 0% -> 0%
where the time goes in v8:
time: 129 us; the launch traced here: 128 us
  starting transfers between devices  56.2 us (44%)
  waiting for transfers between devices  44.6 us (35%)
  local copies, waits for them, and re-layouts  11.9 us (9%)
  other arithmetic  10.1 us (8%)
  matrix products  4.43 us (3%)
    all_to_all x1, starting transfers between devices, shards(): lax.all_to_all(packed, column, split_axis=0, concat_axis=0, tiled=True)  42.4 us
    all_to_all x1, waiting for transfers between devices, shards(): lax.all_to_all(packed, column, split_axis=0, concat_axis=0, tiled=True)  40.1 us
    ppermute x6, starting transfers between devices, send(): got = lax.ppermute(flat, axis, pairs)  13.8 us
    unnamed x29, local copies, waits for them, and re-layouts  5.14 us
    ppermute x6, waiting for transfers between devices, send(): got = lax.ppermute(flat, axis, pairs)  4.46 us
    convert_element_type x1, other arithmetic, shards(): chooser = (lax.broadcasted_iota(jnp.int32, (total_slots, face_count), 0)...  4.03 us
    dot_general x1, matrix products, shards(): jnp.dot(chooser.astype(jnp.float32), rows_out, precision=lax.Precision.HI...  3.35 us
  transfers between devices with their start and end apart: 7, of which 3 were waited for; matrix products, arithmetic and copies ran while one was open for 7% of the time, Pallas kernels for 0%

profile of v8, /device:TPU:32, one launch (start us, length us, event | category | flops | bytes accessed | tf_op | source)
XLA Modules:
  0.0 128.5 jit_solution(86905976398881370)
XLA Ops:
  0.7 1.0 copy.113
  1.7 0.9 fusion.12
  2.6 0.5 copy.114
  3.1 3.4 %collective-permute-start = (f32[528]{0:T(1024)S(1)}, f32[528]{0:T(1024)S(1)}, u32[]{:S(2)}, u32[]{:S(2)}) collective-permute-start(f32[528]{0:T(1024)S(1)} %reshape.164), channel_id=1, source_target_pairs={{0,4},{4,8},{8,12},{12,16},{16,20},{20,24},{24,28},{28,32},{32,36}... | collective-permute-start | bytes 6344 | tf_op jit(solution)/shard_map/ppermute | solution.py:9
  6.5 0.5 copy.115
  7.1 1.3 %collective-permute-start.1 = (f32[528]{0:T(1024)S(1)}, f32[528]{0:T(1024)S(1)}, u32[]{:S(2)}, u32[]{:S(2)}) collective-permute-start(f32[528]{0:T(1024)S(1)} %reshape.166), channel_id=1, source_target_pairs={{4,0},{8,4},{12,8},{16,12},{20,16},{24,20},{28,24},{32,28},{36,32}... | collective-permute-start | bytes 6344 | tf_op jit(solution)/shard_map/ppermute | solution.py:9
  8.4 0.8 fusion.39
  9.4 1.9 %collective-permute-start.5 = (f32[12672]{0:T(1024)S(1)}, f32[12672]{0:T(1024)S(1)}, u32[]{:S(2)}, u32[]{:S(2)}) collective-permute-start(f32[12672]{0:T(1024)S(1)} %pad_maximum_fusion.11), channel_id=1, source_target_pairs={{64,0},{128,64},{192,128},{256,192},{320,256},{384,320},{448,384},... | collective-permute-start | bytes 152072 | tf_op jit(solution)/shard_map/ppermute | solution.py:9
  11.4 2.4 %collective-permute-start.2 = (f32[12672]{0:T(1024)S(1)}, f32[12672]{0:T(1024)S(1)}, u32[]{:S(2)}, u32[]{:S(2)}) collective-permute-start(f32[12672]{0:T(1024)S(1)} %pad_maximum_fusion.10), channel_id=1, source_target_pairs={{0,64},{64,128},{128,192},{192,256},{256,320},{320,384},{384,448},... | collective-permute-start | bytes 152072 | tf_op jit(solution)/shard_map/ppermute | solution.py:9
  13.8 3.5 %collective-permute-start.3 = (f32[33792]{0:T(1024)S(1)}, f32[33792]{0:T(1024)S(1)}, u32[]{:S(2)}, u32[]{:S(2)}) collective-permute-start(f32[33792]{0:T(1024)S(1)} %get-tuple-element.23), channel_id=1, source_target_pairs={{0,1},{1,2},{2,3},{4,5},{5,6},{6,7},{8,9},{9,10},{10,11},{12,13},{... | collective-permute-start | bytes 405512 | tf_op jit(solution)/shard_map/ppermute | solution.py:9
  17.7 0.6 fusion.8
  18.3 4.0 %fusion = bf16[2048,1024]{1,0:T(8,128)(2,1)} fusion(s32[1024]{0:T(1024)S(1)} %convert_add_fusion), kind=kLoop, calls=%fused_computation.1 | loop fusion | flops 4194304 | bytes 4198400 | tf_op jit(solution)/shard_map/convert_element_type | solution.py:108
  22.6 1.3 %collective-permute-start.4 = (f32[33792]{0:T(1024)S(1)}, f32[33792]{0:T(1024)S(1)}, u32[]{:S(2)}, u32[]{:S(2)}) collective-permute-start(f32[33792]{0:T(1024)S(1)} %get-tuple-element.24), channel_id=1, source_target_pairs={{1,0},{2,1},{3,2},{5,4},{6,5},{7,6},{9,8},{10,9},{11,10},{13,12},{... | collective-permute-start | bytes 405512 | tf_op jit(solution)/shard_map/ppermute | solution.py:9
  24.1 0.5 copy.159
  24.6 0.5 copy.161
  25.1 0.7 collective-permute-done.2
  26.9 3.7 %collective-permute-done.4 = f32[33792]{0:T(1024)S(1)} collective-permute-done((f32[33792]{0:T(1024)S(1)}, f32[33792]{0:T(1024)S(1)}, u32[]{:S(2)}, u32[]{:S(2)}) %collective-permute-start.4) | collective-permute-done | bytes 135200 | tf_op jit(solution)/shard_map/ppermute | solution.py:9
  30.6 1.1 select_maximum_fusion
  32.0 0.5 fusion.44
  32.9 0.6 copy-done.6
  33.5 0.9 copy-done
  34.3 3.3 %fusion.34 = f32[2048,17]{0,1:T(8,128)S(1)} fusion(bf16[2048,1024]{1,0:T(8,128)(2,1)S(1)} %copy-done, f32[1024,1]{0,1:T(1,128)S(1)} %convert_bitcast_fusion, f32[1024,16]{0,1:T(8,128)S(1)} %fusion.38), kind=kOutput, calls=%fused_computation.74 | convolution fusion | flops 427836416 | bytes 4403200 | tf_op jit(solution)/shard_map/dot_general | solution.py:138
  38.1 0.3 copy.210
  38.4 1.2 reshape.198
  39.6 42.4 %all-to-all-start = ((f32[64,1,714]{2,1,0:T(1,128)}), f32[64,1,714]{2,1,0:T(1,128)S(1)}, u32[]{:S(2)}, u32[]{:S(2)}) async-start(f32[64,1,714]{2,1,0:T(1,128)} %reshape.198), calls=%async_computation | async-start | bytes 393216 | tf_op jit(solution)/shard_map/all_to_all | solution.py:152
  82.1 40.1 %all-to-all-done = f32[64,1,714]{2,1,0:T(1,128)S(1)} async-done(((f32[64,1,714]{2,1,0:T(1,128)}), f32[64,1,714]{2,1,0:T(1,128)S(1)}, u32[]{:S(2)}, u32[]{:S(2)}) %all-to-all-start) | async-done | bytes 182816 | tf_op jit(solution)/shard_map/all_to_all | solution.py:152
  122.2 0.5 broadcast.137
  122.7 1.1 reduce.12
  123.8 0.3 reshape.199
  126.7 0.5 fusion.9
  127.5 0.2 fusion.31
  127.7 0.8 fusion.41
  (107 shorter events, 6.1 us)
Async XLA Ops:
  0.6 13.2 %copy-start.3 = (f32[2,8,128]{2,1,0:T(8,128)S(1)}, f32[2,8,128]{2,1,0:T(8,128)}, u32[]{:S(2)}) copy-start(f32[2,8,128]{2,1,0:T(8,128)} %param.10) | copy-start | bytes 24580
  0.6 8.7 %copy-start.1 = (f32[16,4,128]{2,1,0:T(4,128)S(1)}, f32[16,4,128]{2,1,0:T(4,128)}, u32[]{:S(2)}) copy-start(f32[16,4,128]{2,1,0:T(4,128)} %param.14) | copy-start | bytes 98308
  0.7 8.7 %copy-start.4 = (f32[4,128]{1,0:T(4,128)S(1)}, f32[4,128]{1,0:T(4,128)}, u32[]{:S(2)}) copy-start(f32[4,128]{1,0:T(4,128)} %param.15) | copy-start | bytes 6148
  0.7 17.0 %copy-start.5 = (s32[1,1,1024,1]{2,3,1,0:T(1,128)S(1)}, s32[1,1,1024,1]{2,3,1,0:T(1,128)}, u32[]{:S(2)}) copy-start(s32[1,1,1024,1]{2,3,1,0:T(1,128)} %param.12) | copy-start | bytes 12292
  3.1 19.4 %collective-permute-start = (f32[528]{0:T(1024)S(1)}, f32[528]{0:T(1024)S(1)}, u32[]{:S(2)}, u32[]{:S(2)}) collective-permute-start(f32[528]{0:T(1024)S(1)} %reshape.164), channel_id=1, source_target_pairs={{0,4},{4,8},{8,12},{12,16},{16,20},{20,24},{24,28},{28,32},{32,36}... | collective-permute-start | bytes 6344 | tf_op jit(solution)/shard_map/ppermute | solution.py:9
  7.1 16.9 %collective-permute-start.1 = (f32[528]{0:T(1024)S(1)}, f32[528]{0:T(1024)S(1)}, u32[]{:S(2)}, u32[]{:S(2)}) collective-permute-start(f32[528]{0:T(1024)S(1)} %reshape.166), channel_id=1, source_target_pairs={{4,0},{8,4},{12,8},{16,12},{20,16},{24,20},{28,24},{32,28},{36,32}... | collective-permute-start | bytes 6344 | tf_op jit(solution)/shard_map/ppermute | solution.py:9
  9.4 15.7 %collective-permute-start.5 = (f32[12672]{0:T(1024)S(1)}, f32[12672]{0:T(1024)S(1)}, u32[]{:S(2)}, u32[]{:S(2)}) collective-permute-start(f32[12672]{0:T(1024)S(1)} %pad_maximum_fusion.11), channel_id=1, source_target_pairs={{64,0},{128,64},{192,128},{256,192},{320,256},{384,320},{448,384},... | collective-permute-start | bytes 152072 | tf_op jit(solution)/shard_map/ppermute | solution.py:9
  11.4 14.4 %collective-permute-start.2 = (f32[12672]{0:T(1024)S(1)}, f32[12672]{0:T(1024)S(1)}, u32[]{:S(2)}, u32[]{:S(2)}) collective-permute-start(f32[12672]{0:T(1024)S(1)} %pad_maximum_fusion.10), channel_id=1, source_target_pairs={{0,64},{64,128},{128,192},{192,256},{256,320},{320,384},{384,448},... | collective-permute-start | bytes 152072 | tf_op jit(solution)/shard_map/ppermute | solution.py:9
  13.8 13.1 %collective-permute-start.3 = (f32[33792]{0:T(1024)S(1)}, f32[33792]{0:T(1024)S(1)}, u32[]{:S(2)}, u32[]{:S(2)}) collective-permute-start(f32[33792]{0:T(1024)S(1)} %get-tuple-element.23), channel_id=1, source_target_pairs={{0,1},{1,2},{2,3},{4,5},{5,6},{6,7},{8,9},{9,10},{10,11},{12,13},{... | collective-permute-start | bytes 405512 | tf_op jit(solution)/shard_map/ppermute | solution.py:9
  18.3 4.1 %copy-start.7 = (s32[1,1,1024]{2,1,0:T(1,128)S(1)}, s32[1,1,1024]{2,1,0:T(1,128)}, u32[]{:S(2)}) copy-start(s32[1,1,1024]{2,1,0:T(1,128)} %param.13) | copy-start | bytes 12292
  22.6 8.1 %collective-permute-start.4 = (f32[33792]{0:T(1024)S(1)}, f32[33792]{0:T(1024)S(1)}, u32[]{:S(2)}, u32[]{:S(2)}) collective-permute-start(f32[33792]{0:T(1024)S(1)} %get-tuple-element.24), channel_id=1, source_target_pairs={{1,0},{2,1},{3,2},{5,4},{6,5},{7,6},{9,8},{10,9},{11,10},{13,12},{... | collective-permute-start | bytes 405512 | tf_op jit(solution)/shard_map/ppermute | solution.py:9
  31.9 0.7 copy-start.8
  31.9 0.7 copy-start.9
  32.0 2.3 %copy-start = (bf16[2048,1024]{1,0:T(8,128)(2,1)S(1)}, bf16[2048,1024]{1,0:T(8,128)(2,1)}, u32[]{:S(2)}) copy-start(bf16[2048,1024]{1,0:T(8,128)(2,1)} %fusion) | copy-start | bytes 12582916
  32.5 0.9 copy-start.6
  32.8 4.9 %copy-start.2 = (f32[16,2,2,8,128]{4,3,2,1,0:T(8,128)}, f32[16,2,2,8,128]{4,3,2,1,0:T(8,128)S(1)}, u32[]{:S(2)}) copy-start(f32[16,2,2,8,128]{4,3,2,1,0:T(8,128)S(1)} %fusion.14) | copy-start | bytes 786436
  39.6 82.6 %all-to-all-start = ((f32[64,1,714]{2,1,0:T(1,128)}), f32[64,1,714]{2,1,0:T(1,128)S(1)}, u32[]{:S(2)}, u32[]{:S(2)}) async-start(f32[64,1,714]{2,1,0:T(1,128)} %reshape.198), calls=%async_computation | async-start | bytes 393216 | tf_op jit(solution)/shard_map/all_to_all | solution.py:152

commit v9 on v7

--- a/solution.py
+++ b/solution.py
@@ -131,10 +131,11 @@
     position = targets * capacity + rank
     total_slots = owner_count * capacity
     rows_out = jnp.concatenate([face_rows, local_cells[:, None]], axis=1)
-    chooser = (
-        lax.broadcasted_iota(jnp.int32, (total_slots, face_count), 0) == position[None, :]
-    ).astype(jnp.float32)
-    packed = jnp.dot(chooser, rows_out, precision=lax.Precision.HIGHEST)
+    source = jnp.full((total_slots,), face_count, jnp.int32).at[position].set(
+        jnp.arange(face_count, dtype=jnp.int32), mode="drop"
+    )
+    rows_out = jnp.concatenate([rows_out, jnp.zeros((1, probes + 1), jnp.float32)], axis=0)
+    packed = jnp.take(rows_out, source, axis=0, mode="clip")
     me = lax.axis_index(column)
     strips = [jnp.concatenate([p.reshape(-1) for p in parts]) for parts in strip_parts]
     strip_size = strips[0].size

time: 127 us -> 134 us (1.055)
  local copies, waits for them, and re-layouts: 12.4 us -> 23 us
  matrix products: 4.85 us -> 1.08 us
    gather x0 -> x1, local copies, waits for them, and re-layouts: none -> 5.46 us  [shards(): packed = jnp.take(rows_out, source, axis=0, mode='clip')]
    scatter x0 -> x1, local copies, waits for them, and re-layouts: none -> 4.32 us  [shards(): jnp.full((total_slots,), face_count, jnp.int32).at[position]]
    dot_general x1 -> x0, matrix products: 3.77 us -> none  [shards(): packed = jnp.dot(chooser, rows_out, precision=lax.Precision.HIGHEST)]
    unnamed x26 -> x27, local copies, waits for them, and re-layouts: 3.59 us -> 3.56 us
  transfers between devices with their start and end apart: 7 -> 7, of which waited for: 2 -> 2; matrix products, arithmetic and copies ran while one was open for 4% -> 8% of each run, Pallas kernels for 0% -> 0%
where the time goes in v9:
time: 134 us; the launch traced here: 133 us
  starting transfers between devices  58.3 us (44%)
  waiting for transfers between devices  43 us (32%)
  local copies, waits for them, and re-layouts  23 us (17%)
  other arithmetic  6.26 us (5%)
    all_to_all x1, starting transfers between devices, shards(): lax.all_to_all(packed, column, split_axis=0, concat_axis=0, tiled=True)  43.3 us
    all_to_all x1, waiting for transfers between devices, shards(): lax.all_to_all(packed, column, split_axis=0, concat_axis=0, tiled=True)  38.6 us
    ppermute x6, starting transfers between devices, send(): got = lax.ppermute(flat, axis, pairs)  14.9 us
    gather x1, local copies, waits for them, and re-layouts, shards(): packed = jnp.take(rows_out, source, axis=0, mode='clip')  5.46 us
    ppermute x6, waiting for transfers between devices, send(): got = lax.ppermute(flat, axis, pairs)  4.38 us
    scatter x1, local copies, waits for them, and re-layouts, shards(): jnp.full((total_slots,), face_count, jnp.int32).at[position]  4.32 us
    unnamed x27, local copies, waits for them, and re-layouts  3.56 us
  transfers between devices with their start and end apart: 7, of which 2 were waited for; matrix products, arithmetic and copies ran while one was open for 8% of the time, Pallas kernels for 0%

profile of v9, /device:TPU:32, one launch (start us, length us, event | category | flops | bytes accessed | tf_op | source)
XLA Modules:
  0.0 133.0 jit_solution(12949921402123796778)
XLA Ops:
  0.7 1.0 copy.149
  1.7 0.8 fusion.34
  2.6 0.9 fusion.41
  3.4 0.8 slice_bitcast_fusion.4
  4.2 1.9 %collective-permute-start.4 = (f32[12672]{0:T(1024)S(1)}, f32[12672]{0:T(1024)S(1)}, u32[]{:S(2)}, u32[]{:S(2)}) collective-permute-start(f32[12672]{0:T(1024)S(1)} %pad_maximum_fusion.13), channel_id=1, source_target_pairs={{64,0},{128,64},{192,128},{256,192},{320,256},{384,320},{448,384},... | collective-permute-start | bytes 152072 | tf_op jit(solution)/shard_map/ppermute | solution.py:9
  6.2 2.4 %collective-permute-start.1 = (f32[12672]{0:T(1024)S(1)}, f32[12672]{0:T(1024)S(1)}, u32[]{:S(2)}, u32[]{:S(2)}) collective-permute-start(f32[12672]{0:T(1024)S(1)} %pad_maximum_fusion.12), channel_id=1, source_target_pairs={{0,64},{64,128},{128,192},{192,256},{256,320},{320,384},{384,448},... | collective-permute-start | bytes 152072 | tf_op jit(solution)/shard_map/ppermute | solution.py:9
  8.6 0.9 fusion.10
  9.5 0.5 copy.155
  10.1 1.3 collective-permute-start.5
  11.4 0.5 copy.150
  12.0 4.5 %collective-permute-start = (f32[528]{0:T(1024)S(1)}, f32[528]{0:T(1024)S(1)}, u32[]{:S(2)}, u32[]{:S(2)}) collective-permute-start(f32[528]{0:T(1024)S(1)} %reshape.184), channel_id=1, source_target_pairs={{0,4},{4,8},{8,12},{12,16},{16,20},{20,24},{24,28},{28,32},{32,36}... | collective-permute-start | bytes 6344 | tf_op jit(solution)/shard_map/ppermute | solution.py:9
  16.6 3.5 %collective-permute-start.2 = (f32[33792]{0:T(1024)S(1)}, f32[33792]{0:T(1024)S(1)}, u32[]{:S(2)}, u32[]{:S(2)}) collective-permute-start(f32[33792]{0:T(1024)S(1)} %get-tuple-element.17), channel_id=1, source_target_pairs={{0,1},{1,2},{2,3},{4,5},{5,6},{6,7},{8,9},{9,10},{10,11},{12,13},{... | collective-permute-start | bytes 405512 | tf_op jit(solution)/shard_map/ppermute | solution.py:9
  20.5 0.6 fusion.7
  21.1 4.3 %scatter_custom_fusion = s32[2048]{0:T(1024)S(1)} fusion(s32[1024]{0:T(1024)S(1)} %bitcast.102, s32[1024]{0:T(1024)S(1)} %iota.33, s32[]{:T(128)} %constant.20.clone.1), kind=kCustom, calls=%fused_computation.117 | custom fusion | bytes 8196 | tf_op jit(solution)/shard_map/scatter | solution.py:134
  25.7 1.3 collective-permute-start.3
  27.1 0.5 copy.156
  27.7 0.5 copy.195
  29.4 4.4 %collective-permute-done.3 = f32[33792]{0:T(1024)S(1)} collective-permute-done((f32[33792]{0:T(1024)S(1)}, f32[33792]{0:T(1024)S(1)}, u32[]{:S(2)}, u32[]{:S(2)}) %collective-permute-start.3) | collective-permute-done | bytes 135200 | tf_op jit(solution)/shard_map/ppermute | solution.py:9
  33.8 1.1 select_maximum_fusion
  35.1 0.5 fusion.40
  36.0 0.3 copy-done.6
  36.6 5.5 %gather_fusion = f32[2048,17]{1,0:T(8,128)S(1)} fusion(f32[1025,17]{1,0:T(8,128)S(1)} %concatenate.61, s32[2048]{0:T(1024)S(1)} %broadcast_clamp_fusion), kind=kCustom, calls=%fused_computation | custom fusion | bytes 286720 | tf_op jit(solution)/shard_map/jit(_take)/gather | solution.py:138
  42.1 0.5 copy.168
  42.6 0.3 fusion.42
  42.8 1.2 reshape.237
  44.0 43.3 %all-to-all-start = ((f32[64,1,714]{2,1,0:T(1,128)}), f32[64,1,714]{2,1,0:T(1,128)S(1)}, u32[]{:S(2)}, u32[]{:S(2)}) async-start(f32[64,1,714]{2,1,0:T(1,128)} %reshape.237), calls=%async_computation | async-start | bytes 393216 | tf_op jit(solution)/shard_map/all_to_all | solution.py:152
  87.4 0.7 slice_bitcast_fusion.2
  88.1 38.6 %all-to-all-done = f32[64,1,714]{2,1,0:T(1,128)S(1)} async-done(((f32[64,1,714]{2,1,0:T(1,128)}), f32[64,1,714]{2,1,0:T(1,128)S(1)}, u32[]{:S(2)}, u32[]{:S(2)}) %all-to-all-start) | async-done | bytes 182816 | tf_op jit(solution)/shard_map/all_to_all | solution.py:152
  126.7 0.5 broadcast.163
  127.2 1.1 reduce.12
  131.2 0.5 fusion.8
  132.2 0.8 fusion.36
  (112 shorter events, 6.5 us)
Async XLA Ops:
  0.6 15.9 %copy-start.2 = (f32[2,8,128]{2,1,0:T(8,128)S(1)}, f32[2,8,128]{2,1,0:T(8,128)}, u32[]{:S(2)}) copy-start(f32[2,8,128]{2,1,0:T(8,128)} %param.10) | copy-start | bytes 24580
  0.6 19.4 %copy-start = (f32[16,4,128]{2,1,0:T(4,128)S(1)}, f32[16,4,128]{2,1,0:T(4,128)}, u32[]{:S(2)}) copy-start(f32[16,4,128]{2,1,0:T(4,128)} %param.14) | copy-start | bytes 98308
  0.7 19.6 %copy-start.4 = (f32[4,128]{1,0:T(4,128)S(1)}, f32[4,128]{1,0:T(4,128)}, u32[]{:S(2)}) copy-start(f32[4,128]{1,0:T(4,128)} %param.15) | copy-start | bytes 6148
  0.7 19.8 %copy-start.7 = (s32[1,1,1024]{2,1,0:T(1,128)S(1)}, s32[1,1,1024]{2,1,0:T(1,128)}, u32[]{:S(2)}) copy-start(s32[1,1,1024]{2,1,0:T(1,128)} %param.13) | copy-start | bytes 12292
  0.7 19.8 %copy-start.5 = (s32[1,1,1024,1]{2,3,1,0:T(1,128)S(1)}, s32[1,1,1024,1]{2,3,1,0:T(1,128)}, u32[]{:S(2)}) copy-start(s32[1,1,1024,1]{2,3,1,0:T(1,128)} %param.12) | copy-start | bytes 12292
  4.2 23.9 %collective-permute-start.4 = (f32[12672]{0:T(1024)S(1)}, f32[12672]{0:T(1024)S(1)}, u32[]{:S(2)}, u32[]{:S(2)}) collective-permute-start(f32[12672]{0:T(1024)S(1)} %pad_maximum_fusion.13), channel_id=1, source_target_pairs={{64,0},{128,64},{192,128},{256,192},{320,256},{384,320},{448,384},... | collective-permute-start | bytes 152072 | tf_op jit(solution)/shard_map/ppermute | solution.py:9
  6.2 22.0 %collective-permute-start.1 = (f32[12672]{0:T(1024)S(1)}, f32[12672]{0:T(1024)S(1)}, u32[]{:S(2)}, u32[]{:S(2)}) collective-permute-start(f32[12672]{0:T(1024)S(1)} %pad_maximum_fusion.12), channel_id=1, source_target_pairs={{0,64},{64,128},{128,192},{192,256},{256,320},{320,384},{384,448},... | collective-permute-start | bytes 152072 | tf_op jit(solution)/shard_map/ppermute | solution.py:9
  10.1 15.6 %collective-permute-start.5 = (f32[528]{0:T(1024)S(1)}, f32[528]{0:T(1024)S(1)}, u32[]{:S(2)}, u32[]{:S(2)}) collective-permute-start(f32[528]{0:T(1024)S(1)} %reshape.198), channel_id=1, source_target_pairs={{4,0},{8,4},{12,8},{16,12},{20,16},{24,20},{28,24},{32,28},{36,32}... | collective-permute-start | bytes 6344 | tf_op jit(solution)/shard_map/ppermute | solution.py:9
  12.0 15.6 %collective-permute-start = (f32[528]{0:T(1024)S(1)}, f32[528]{0:T(1024)S(1)}, u32[]{:S(2)}, u32[]{:S(2)}) collective-permute-start(f32[528]{0:T(1024)S(1)} %reshape.184), channel_id=1, source_target_pairs={{0,4},{4,8},{8,12},{12,16},{16,20},{20,24},{24,28},{28,32},{32,36}... | collective-permute-start | bytes 6344 | tf_op jit(solution)/shard_map/ppermute | solution.py:9
  16.6 12.8 %collective-permute-start.2 = (f32[33792]{0:T(1024)S(1)}, f32[33792]{0:T(1024)S(1)}, u32[]{:S(2)}, u32[]{:S(2)}) collective-permute-start(f32[33792]{0:T(1024)S(1)} %get-tuple-element.17), channel_id=1, source_target_pairs={{0,1},{1,2},{2,3},{4,5},{5,6},{6,7},{8,9},{9,10},{10,11},{12,13},{... | collective-permute-start | bytes 405512 | tf_op jit(solution)/shard_map/ppermute | solution.py:9
  25.7 8.1 %collective-permute-start.3 = (f32[33792]{0:T(1024)S(1)}, f32[33792]{0:T(1024)S(1)}, u32[]{:S(2)}, u32[]{:S(2)}) collective-permute-start(f32[33792]{0:T(1024)S(1)} %get-tuple-element.18), channel_id=1, source_target_pairs={{1,0},{2,1},{3,2},{5,4},{6,5},{7,6},{9,8},{10,9},{11,10},{13,12},{... | collective-permute-start | bytes 405512 | tf_op jit(solution)/shard_map/ppermute | solution.py:9
  28.2 6.6 %copy-start.3 = (f32[12672]{0:T(1024)}, f32[12672]{0:T(1024)S(1)}, u32[]{:S(2)}) copy-start(f32[12672]{0:T(1024)S(1)} %collective-permute-done.1) | copy-start | bytes 152068
  35.0 0.7 copy-start.8
  35.1 0.7 copy-start.9
  35.6 0.7 copy-start.6
  35.9 6.1 %copy-start.1 = (f32[16,2,2,8,128]{4,3,2,1,0:T(8,128)}, f32[16,2,2,8,128]{4,3,2,1,0:T(8,128)S(1)}, u32[]{:S(2)}) copy-start(f32[16,2,2,8,128]{4,3,2,1,0:T(8,128)S(1)} %fusion.12) | copy-start | bytes 786436
  44.0 82.7 %all-to-all-start = ((f32[64,1,714]{2,1,0:T(1,128)}), f32[64,1,714]{2,1,0:T(1,128)S(1)}, u32[]{:S(2)}, u32[]{:S(2)}) async-start(f32[64,1,714]{2,1,0:T(1,128)} %reshape.237), calls=%async_computation | async-start | bytes 393216 | tf_op jit(solution)/shard_map/all_to_all | solution.py:152
